TPU v7x, 32 devices: a whole 2x2x4 slice. The times are simulated.
32 devices in a mesh: row: 8 (over y, x, core), col: 4 (over z).
Axes of the slice: x: 2, y: 2, z: 4, core: 2. Of those that a mesh axis runs over, the one named last changes fastest.
Arguments:
- queries: bfloat16 [512, 2, 2048], P('row', None, 'col'), may hold values from -15 to 15
- new_keys: bfloat16 [512, 2, 2048], P('row', None, 'col'), may hold values from -6 to 6
- new_values: bfloat16 [512, 2, 2048], P('row', None, 'col'), may hold values from -6 to 6
- cache_keys: bfloat16 [1024, 2, 2048], P('row', None, 'col'), may hold values from -6 to 6
- cache_values: bfloat16 [1024, 2, 2048], P('row', None, 'col'), may hold values from -6 to 6
- cached_len: int32 [2], replicated, may hold values from 256 to 1024, as said below
- residual: bfloat16 [512, 2, 2048], P('row'), may hold values from -4 to 4
- out_weight: bfloat16 [2048, 2048], P('col'), may hold values from -0.125 to 0.125
- norm_gain: float32 [2048], replicated, may hold values from 0.5 to 1.5
- expert_ids: int32 [512, 2, 6], P('row'), may hold values from 0 to 63, all different within a row; in each aligned block of 128 rows (0 to 127, 128 to 255, ..., all dimensions but the last counted through in order) at most 24 rows name the same one
- gate_values: float32 [512, 2, 6], P('row'), may hold values from 0.1 to 0.6
- w_gate: bfloat16 [256, 2048, 352], P(('row', 'col')), may hold values from -0.125 to 0.125
- w_up: bfloat16 [256, 2048, 352], P(('row', 'col')), may hold values from -0.125 to 0.125
- w_down: bfloat16 [256, 352, 2048], P(('row', 'col')), may hold values from -0.15625 to 0.15625
- shared_gate: bfloat16 [2048, 2816], P(None, 'col'), may hold values from -0.125 to 0.125
- shared_up: bfloat16 [2048, 2816], P(None, 'col'), may hold values from -0.125 to 0.125
- shared_down: bfloat16 [2816, 2048], P('col'), may hold values from -0.109375 to 0.109375
Outputs:
- mixed: bfloat16 [512, 2, 2048], P('row', None, 'col')
- ffn_out: bfloat16 [512, 2, 2048], P('row', None, 'col')
Inputs may be any that keep to these rules, and one draw needn't show every extreme that they name: `cached_len`: some request has exactly 1024 cached positions. `expert_ids`: each token names 6 different experts. Among the 128 tokens of one index of row (positions taken in order, requests inside), no expert is named more than 24 times, and in some such blocks one expert is named exactly 24 times.
All inputs are finite; a program needn't handle non-finite values.
Results may differ from a plain program's by a relative error of at most 0.023.
Values may be sent and summed in bfloat16 or wider, within the bound.
No kernel may reach another device: no remote copies, remote signals or barrier semaphores. Data moves between devices by JAX's collectives and lax.ppermute only.
A program may use at most 192 MiB of HBM per device.

v0:
```python
import math

import jax
import jax.numpy as jnp
from jax import lax
from jax.sharding import PartitionSpec as P

HD = 128
E = 64
TOPK = 6
GROUPS = 4
CAP = 24


def body(
    queries,
    new_keys,
    new_values,
    cache_keys,
    cache_values,
    cached_len,
    residual,
    out_weight,
    norm_gain,
    expert_ids,
    gate_values,
    w_gate,
    w_up,
    w_down,
    shared_gate,
    shared_up,
    shared_down,
):
    rows_here = queries.shape[0]
    requests = queries.shape[1]
    heads_here = queries.shape[2] // HD
    cache_rows = cache_keys.shape[0]
    block_rows = cache_rows + rows_here
    model_width = residual.shape[2]
    row_index = lax.axis_index("row")
    row_count = lax.axis_size("row")
    score_scale = 1.0 / math.sqrt(HD)
    keys_here = jnp.concatenate([cache_keys, new_keys], axis=0)
    values_here = jnp.concatenate([cache_values, new_values], axis=0)
    query_heads = queries.reshape(rows_here, requests, heads_here, HD)
    local_pos = row_index * rows_here + jnp.arange(rows_here, dtype=jnp.int32)
    key_piece = lax.all_gather(keys_here, "row", axis=0, tiled=True)
    key_count = key_piece.shape[0]
    global_row = jnp.arange(key_count, dtype=jnp.int32)
    shard_index = global_row // block_rows
    offset_rows = global_row % block_rows
    in_cache = offset_rows < cache_rows
    cache_pos = shard_index * cache_rows + offset_rows
    new_pos = shard_index * rows_here + offset_rows - cache_rows
    cache_ok = in_cache[None, :] & (cache_pos[None, :] < cached_len[:, None])
    new_ok = jnp.logical_not(in_cache)[None, :] & (new_pos[None, :] <= local_pos[:, None])
    allowed = cache_ok[:, None, None, :] | new_ok[None, None, :, :]
    key_heads = key_piece.reshape(key_count, requests, heads_here, HD)
    value_heads = lax.all_gather(values_here, "row", axis=0, tiled=True).reshape(
        key_count, requests, heads_here, HD
    )
    scores = (
        jnp.einsum("irhd,jrhd->rhij", query_heads, key_heads, preferred_element_type=jnp.float32)
        * score_scale
    )
    masked = jnp.where(allowed, scores, -1e30)
    old_max = jnp.full((requests, heads_here, rows_here), -1e30, jnp.float32)
    new_max = jnp.maximum(old_max, jnp.max(masked, axis=-1))
    weights_now = jnp.where(allowed, jnp.exp(masked - new_max[..., None]), 0.0)
    new_sum = jnp.sum(weights_now, axis=-1)
    product = jnp.einsum(
        "rhij,jrhd->rhid",
        weights_now.astype(jnp.bfloat16),
        value_heads,
        preferred_element_type=jnp.float32,
    )
    attended = (product / new_sum[..., None]).astype(jnp.bfloat16)
    head_weights = out_weight.reshape(heads_here, HD, model_width)
    attn_part = jnp.einsum(
        "rhid,hde->ire", attended, head_weights, preferred_element_type=jnp.float32
    )
    attn_full = lax.psum(attn_part.astype(jnp.bfloat16), "col").astype(jnp.float32)
    mixed_full = (residual.astype(jnp.float32) + attn_full).astype(jnp.bfloat16)
    mixed_f32 = mixed_full.astype(jnp.float32)
    normed = (
        mixed_f32
        * lax.rsqrt(jnp.mean(mixed_f32 * mixed_f32, axis=-1, keepdims=True) + 1e-06)
        * norm_gain
    ).astype(jnp.bfloat16)
    token_count = rows_here * requests
    tokens = normed.reshape(token_count, model_width)
    col_index = lax.axis_index("col")
    col_count = lax.axis_size("col")
    entries_here = w_gate.shape[0]
    experts_dev = max(1, entries_here // GROUPS)
    groups_dev = entries_here // experts_dev
    experts_per_row = col_count * entries_here // GROUPS
    slots = row_count * experts_dev * CAP
    chosen = expert_ids.reshape(token_count * TOPK)
    onehot = (chosen[:, None] == jnp.arange(E, dtype=jnp.int32)[None, :]).astype(jnp.int32)
    slot_index = jnp.sum(jnp.cumsum(onehot, axis=0) * onehot, axis=1) - 1
    dest_row = chosen // experts_per_row
    local_expert = chosen - (dest_row * col_count + col_index) * entries_here // GROUPS
    valid = (local_expert >= 0) & (local_expert < experts_dev)
    place = (dest_row * experts_dev + local_expert) * CAP + slot_index
    place = jnp.where(valid, place, -1).reshape(token_count, TOPK)
    hit = place[:, :, None] == jnp.arange(slots, dtype=jnp.int32)[None, None, :]
    dispatch = jnp.sum(hit.astype(jnp.float32), axis=1).astype(jnp.bfloat16)
    combine = jnp.sum(
        jnp.where(hit, gate_values.reshape(token_count, TOPK, 1), 0.0), axis=1
    )
    outgoing = lax.dot_general(
        dispatch, tokens, (((0,), (0,)), ((), ())), preferred_element_type=jnp.float32
    ).astype(jnp.bfloat16)
    outgoing = outgoing.reshape(row_count, experts_dev, CAP, model_width)
    arrived = lax.all_to_all(outgoing, "row", 0, 0, tiled=True)
    hidden = w_gate.shape[2]
    wg = w_gate.reshape(experts_dev, groups_dev, model_width, hidden)
    wu = w_up.reshape(experts_dev, groups_dev, model_width, hidden)
    wd = w_down.reshape(experts_dev, groups_dev, hidden, model_width)
    gate_proj = jnp.einsum("nlsd,lgdf->lgnsf", arrived, wg, preferred_element_type=jnp.float32)
    up_proj = jnp.einsum("nlsd,lgdf->lgnsf", arrived, wu, preferred_element_type=jnp.float32)
    hidden_act = (jax.nn.silu(gate_proj) * up_proj).astype(jnp.bfloat16)
    expert_out = jnp.einsum(
        "lgnsf,lgfd->nlsd", hidden_act, wd, preferred_element_type=jnp.float32
    ).astype(jnp.bfloat16)
    returned = lax.all_to_all(expert_out, "row", 0, 0, tiled=True).reshape(slots, model_width)
    combine_hi = combine.astype(jnp.bfloat16)
    combine_lo = (combine - combine_hi.astype(jnp.float32)).astype(jnp.bfloat16)
    routed = jnp.dot(combine_hi, returned, preferred_element_type=jnp.float32) + jnp.dot(
        combine_lo, returned, preferred_element_type=jnp.float32
    )
    shared_g = jnp.dot(tokens, shared_gate, preferred_element_type=jnp.float32)
    shared_u = jnp.dot(tokens, shared_up, preferred_element_type=jnp.float32)
    shared_act = (jax.nn.silu(shared_g) * shared_u).astype(jnp.bfloat16)
    shared_part = jnp.dot(shared_act, shared_down, preferred_element_type=jnp.float32)
    ffn_total = lax.psum_scatter(
        (routed + shared_part).astype(jnp.bfloat16), "col", scatter_dimension=1, tiled=True
    )
    col_width = model_width // col_count
    ffn_here = ffn_total.reshape(rows_here, requests, col_width)
    mixed_here = lax.dynamic_slice_in_dim(mixed_full, col_index * col_width, col_width, 2)
    return (mixed_here, ffn_here)


def solution(mesh):
    in_specs = (
        P("row", None, "col"),
        P("row", None, "col"),
        P("row", None, "col"),
        P("row", None, "col"),
        P("row", None, "col"),
        P(),
        P("row", None, None),
        P("col", None),
        P(),
        P("row", None, None),
        P("row", None, None),
        P(("row", "col"), None, None),
        P(("row", "col"), None, None),
        P(("row", "col"), None, None),
        P(None, "col"),
        P(None, "col"),
        P("col", None),
    )
    out_specs = (P("row", None, "col"), P("row", None, "col"))
    return jax.shard_map(body, mesh=mesh, in_specs=in_specs, out_specs=out_specs, check_vma=False)
```

profile of v0, /device:TPU:0, one launch (start us, length us, event | category | flops | bytes accessed | tf_op | source)
XLA Modules:
  0.0 250.1 jit_solution(14127599166133961431)
XLA Ops:
  7.2 2.4 pad_maximum_fusion
  9.7 0.0 all-gather.5.cloned.1.call-start
  9.8 2.3 pad_maximum_fusion.1
  12.1 0.8 copy.73
  12.9 0.1 eq.44
  13.1 0.1 eq.40
  13.2 1.0 reshape.257
  14.2 1.8 reduce-window.6
  16.0 0.3 slice_reduce_fusion
  16.4 0.1 fusion.38
  16.6 0.1 compare_and_fusion.1
  16.7 0.1 compare_and_fusion
  16.8 0.1 broadcast_or_fusion
  16.9 28.1 %all-gather.3.cloned.1.call-done = bf16[1536,2,512]{2,1,0:T(2,128)(2,1)} async-done(((bf16[192,2,512]{2,1,0:T(2,128)(2,1)}), bf16[1536,2,512]{2,1,0:T(2,128)(2,1)}) %all-gather.3.cloned.1.call-update) | async-done | bytes 3145744 | tf_op jit(solution)/shard_map/all_gather | solution.py:47
  45.0 8.7 %copy.68 = bf16[1536,2,512]{0,2,1:T(8,128)(2,1)} copy(bf16[1536,2,512]{2,1,0:T(2,128)(2,1)} %all-gather.3.cloned.1.call-done) | data formatting | bytes 6291456 | tf_op jit(solution)/shard_map/all_gather | solution.py:47
  53.7 3.0 %fusion.62 = (f32[2,4,64]{2,1,0:T(4,128)S(1)}, f32[2,4,64,1536]{3,2,1,0:T(8,128)S(1)}) fusion(bf16[1536,2,4,128]{0,3,2,1:T(8,128)(2,1)} %bitcast.114, bf16[64,2,4,128]{3,2,1,0:T(4,128)(2,1)S(1)} %reshape.257, pred[2,64,1536]{2,1,0:T(8,128)(4,1)S(1)} %broadcast_or_fusion), kind=kOutput, calls=%fused_computation.106 | convolution fusion | flops 203685376 | bytes 6621184 | tf_op jit(solution)/shard_map/irhd,jrhd->rhij/dot_general | solution.py:63
  56.7 1.7 copy-done.1
  58.4 0.8 fusion.3
  59.2 20.0 %all-gather.5.cloned.1.call-done = bf16[1536,2,512]{2,1,0:T(2,128)(2,1)} async-done(((bf16[192,2,512]{2,1,0:T(2,128)(2,1)}), bf16[1536,2,512]{2,1,0:T(2,128)(2,1)}) %all-gather.5.cloned.1.call-update) | async-done | bytes 3145744 | tf_op jit(solution)/shard_map/all_gather | solution.py:59
  79.2 8.7 %copy.71 = bf16[1536,2,512]{0,2,1:T(8,128)(2,1)} copy(bf16[1536,2,512]{2,1,0:T(2,128)(2,1)} %all-gather.5.cloned.1.call-done) | data formatting | bytes 6291456 | tf_op jit(solution)/shard_map/all_gather | solution.py:59
  87.9 5.9 %fusion.11 = bf16[64,2,2048]{2,0,1:T(8,128)(2,1)} fusion(bf16[4,128,2048,1]{2,1,0,3:T(8,128)(2,1)} %bitcast.123, bf16[1536,2,4,128]{0,3,2,1:T(8,128)(2,1)} %bitcast.116, f32[2,4,64,1536]{3,2,1,0:T(8,128)} %copy-done.1, f32[2,4,64]{2,1,0:T(4,128)S(1)} %broadcast_maximum_fusion, pred[2,64,1536]{2,1,0:T(8,128)(4,1)S(1)} %broadcast_or_fusion, ...), kind=kOutput, calls=%fused_computation.21 | convolution fusion | flops 472514560 | bytes 9113600 | tf_op jit(solution)/shard_map/rhid,hde->ire/dot_general | solution.py:79
  93.8 0.1 sub.53
  94.0 0.1 add_select_fusion.2
  94.1 0.1 copy.77
  94.1 0.1 copy.78
  94.3 0.1 copy.79
  94.3 1.0 select_reduce_fusion
  95.3 37.0 %all-reduce.2.cloned.1.call-done = bf16[64,2,2048]{2,0,1:T(8,128)(2,1)} async-done(((bf16[64,2,2048]{2,0,1:T(8,128)(2,1)}), bf16[64,2,2048]{2,0,1:T(8,128)(2,1)}) %all-reduce.2.cloned.1.call-update) | async-done | bytes 524304 | tf_op jit(solution)/shard_map/psum | solution.py:82
  132.3 1.5 fusion.29
  133.8 0.8 copy-done.2
  134.6 0.2 fusion.31
  134.8 1.3 copy.80
  136.2 1.2 reshape.262
  137.4 0.6 convolution_convert_fusion
  138.0 24.4 %all_to_all.10 = bf16[8,2,24,2048]{3,2,1,0:T(8,128)(2,1)S(1)} all-to-all(bf16[8,2,24,2048]{3,2,1,0:T(8,128)(2,1)S(1)} %bitcast.115), channel_id=1, replica_groups=mesh['row'=8,'col'=4] {'row'}, dimensions={0} | all-to-all | bytes 3145728 | tf_op jit(solution)/shard_map/all_to_all | solution.py:116
  162.4 8.5 %fusion.17 = f32[2,8,24,4,352]{4,2,3,1,0:T(8,128)} fusion(bf16[2,4,2048,352,1]{2,3,1,4,0:T(8,128)(2,1)} %bitcast.120, bf16[8,2,24,2048]{3,2,1,0:T(8,128)(2,1)S(1)} %all_to_all.10), kind=kOutput, calls=%fused_computation.26 | convolution fusion | flops 2214592512 | bytes 15269888 | tf_op jit(solution)/shard_map/nlsd,lgdf->lgnsf/dot_general | solution.py:122
  171.0 12.9 %fusion.2 = bf16[8,2,24,2048]{3,2,0,1:T(8,128)(2,1)} fusion(bf16[2,4,352,2048,1]{3,2,1,4,0:T(8,128)(2,1)} %bitcast.121, f32[2,8,24,4,352]{4,2,3,1,0:T(8,128)} %fusion.17, bf16[2,4,2048,352,1]{2,3,1,4,0:T(8,128)(2,1)} %bitcast.122, bf16[8,2,24,2048]{3,2,1,0:T(8,128)(2,1)} %copy-done.4), kind=kOutput, calls=%fused_computation.6 | convolution fusion | flops 4433215488 | bytes 28377088 | tf_op jit(solution)/shard_map/lgnsf,lgfd->nlsd/dot_general | solution.py:124
  183.9 2.7 %copy.83 = bf16[8,2,24,2048]{3,2,1,0:T(8,128)(2,1)} copy(bf16[8,2,24,2048]{3,2,0,1:T(8,128)(2,1)} %fusion.2) | data formatting | bytes 3145728 | tf_op jit(solution)/shard_map/convert_element_type | solution.py:126
  186.6 4.3 %all-to-all-start.1 = ((bf16[8,2,24,2048]{3,2,1,0:T(8,128)(2,1)}), bf16[8,2,24,2048]{3,2,1,0:T(8,128)(2,1)}, u32[]{:S(2)}, u32[]{:S(2)}) async-start(bf16[8,2,24,2048]{3,2,1,0:T(8,128)(2,1)} %copy.83), calls=%async_computation.1 | async-start | bytes 3145728 | tf_op jit(solution)/shard_map/all_to_all | solution.py:127
  191.0 3.5 %fusion.63 = f32[128,704]{0,1:T(8,128)} fusion(bf16[128,2048]{1,0:T(8,128)(2,1)S(1)} %reshape.262, bf16[2048,704]{0,1:T(8,128)(2,1)} %param.31), kind=kOutput, calls=%fused_computation.107 | convolution fusion | flops 369098752 | bytes 3768320 | tf_op jit(solution)/shard_map/dot_general | solution.py:133
  194.4 17.5 %all-to-all-done.1 = bf16[8,2,24,2048]{3,2,1,0:T(8,128)(2,1)} async-done(((bf16[8,2,24,2048]{3,2,1,0:T(8,128)(2,1)}), bf16[8,2,24,2048]{3,2,1,0:T(8,128)(2,1)}, u32[]{:S(2)}, u32[]{:S(2)}) %all-to-all-start.1) | async-done | bytes 1572896 | tf_op jit(solution)/shard_map/all_to_all | solution.py:127
  212.0 2.0 fusion.50
  214.0 2.8 %convolution_add_fusion.1 = f32[128,2048]{1,0:T(8,128)} fusion(f32[128,2048]{1,0:T(8,128)S(1)} %fusion.50, bf16[384,2048]{1,0:T(8,128)(2,1)} %bitcast.28, f32[128,384]{1,0:T(8,128)S(1)} %copy-done.3), kind=kOutput, calls=%fused_computation.10 | convolution fusion | flops 201785344 | bytes 3866624 | tf_op jit(solution)/shard_map/dot_general | solution.py:130
  216.8 5.1 %fusion.5 = bf16[128,2048]{1,0:T(8,128)(2,1)} fusion(f32[128,2048]{1,0:T(8,128)} %convolution_add_fusion.1, bf16[704,2048]{1,0:T(8,128)(2,1)S(1)} %copy-done, bf16[128,2048]{1,0:T(8,128)(2,1)S(1)} %reshape.262, bf16[2048,704]{0,1:T(8,128)(2,1)} %param.32, f32[128,704]{0,1:T(8,128)} %fusion.63), kind=kOutput, calls=%fused_computation.12 | convolution fusion | flops 739262464 | bytes 8224768 | tf_op jit(solution)/shard_map/dot_general | solution.py:136
  221.9 0.9 constant_dynamic-slice_fusion
  222.9 0.8 copy.84
  223.7 18.3 %reduce-scatter.2.cloned.1.call-done = bf16[128,512]{1,0:T(8,128)(2,1)} async-done(((bf16[128,2048]{1,0:T(8,128)(2,1)}), bf16[128,512]{1,0:T(8,128)(2,1)}) %reduce-scatter.2.cloned.1.call-update) | async-done | bytes 131088 | tf_op jit(solution)/shard_map/reduce_scatter | solution.py:137
  241.9 1.6 reshape.268
  (31 shorter events, 0.3 us)
Async XLA Ops:
  7.2 209.6 %copy-start = (bf16[704,2048]{1,0:T(8,128)(2,1)S(1)}, bf16[704,2048]{1,0:T(8,128)(2,1)}, u32[]{:S(2)}) copy-start(bf16[704,2048]{1,0:T(8,128)(2,1)} %param.33) | copy-start | bytes 8650756
  7.2 9.4 %copy-start.7 = (s32[2]{0:T(128)S(1)}, s32[2]{0:T(128)}, u32[]{:S(2)}) copy-start(s32[2]{0:T(128)} %param.22) | copy-start | bytes 28
  7.2 37.8 %all-gather.3.cloned.1.call-start = ((), (), s32[]{:S(2)}) async-start(), calls=%async_computation.3 | async-start | bytes 3538944 | tf_op jit(solution)/shard_map/all_gather | solution.py:47
  9.7 69.5 %all-gather.5.cloned.1.call-start = ((), (), s32[]{:S(2)}) async-start(), calls=%async_computation.4 | async-start | bytes 3538944 | tf_op jit(solution)/shard_map/all_gather | solution.py:59
  12.1 120.3 %all-reduce.2.cloned.1.call-start = ((), (), s32[]{:S(2)}) async-start(), calls=%async_computation.5 | async-start | bytes 1048576 | tf_op jit(solution)/shard_map/psum | solution.py:82
  56.7 1.7 copy-start.1
  87.9 6.3 %copy-start.6 = (f32[64,2,6]{0,1,2:T(2,128)S(1)}, f32[64,2,6]{0,1,2:T(2,128)}, u32[]{:S(2)}) copy-start(f32[64,2,6]{0,1,2:T(2,128)} %param.27) | copy-start | bytes 9220
  93.8 40.9 %copy-start.5 = (f32[2048]{0:T(1024)S(1)}, f32[2048]{0:T(1024)}, u32[]{:S(2)}) copy-start(f32[2048]{0:T(1024)} %param.25) | copy-start | bytes 24580
  133.8 0.8 copy-start.2
  162.4 8.5 %copy-start.4 = (bf16[8,2,24,2048]{3,2,1,0:T(8,128)(2,1)}, bf16[8,2,24,2048]{3,2,1,0:T(8,128)(2,1)S(1)}, u32[]{:S(2)}) copy-start(bf16[8,2,24,2048]{3,2,1,0:T(8,128)(2,1)S(1)} %all_to_all.10) | copy-start | bytes 4718596
  186.6 25.3 %all-to-all-start.1 = ((bf16[8,2,24,2048]{3,2,1,0:T(8,128)(2,1)}), bf16[8,2,24,2048]{3,2,1,0:T(8,128)(2,1)}, u32[]{:S(2)}, u32[]{:S(2)}) async-start(bf16[8,2,24,2048]{3,2,1,0:T(8,128)(2,1)} %copy.83), calls=%async_computation.1 | async-start | bytes 3145728 | tf_op jit(solution)/shard_map/all_to_all | solution.py:127
  190.9 51.0 %reduce-scatter.2.cloned.1.call-start = ((), (), s32[]{:S(2)}) async-start(), calls=%async_computation.6 | async-start | bytes 655360 | tf_op jit(solution)/shard_map/reduce_scatter | solution.py:137
  212.0 2.0 copy-start.3
Sparse Core Ops, SparseCore 0:
  9.9 35.0 all-gather.2
  46.8 32.3 all-gather.4
  93.9 38.3 all-reduce.1
  222.1 19.8 reduce-scatter.1
where the time goes:
time: 251 us; the launch traced here: 250 us
  waiting for transfers between devices  121 us (48%)
  matrix products  44.3 us (18%)
  local copies, waits for them, and re-layouts  31.3 us (12%)
  blocking collectives  24.4 us (10%)
  between operations  14 us (6%)
  other arithmetic  10.7 us (4%)
  starting transfers between devices  4.45 us (2%)
    psum x1, waiting for transfers between devices, body(): lax.psum(attn_part.astype(jnp.bfloat16), 'col').astype(jnp.float32)  37 us
    all_gather x1, waiting for transfers between devices, body(): key_piece = lax.all_gather(keys_here, 'row', axis=0, tiled=True)  28.1 us
    all_to_all x1, blocking collectives, body(): arrived = lax.all_to_all(outgoing, 'row', 0, 0, tiled=True)  24.4 us
    all_gather x1, waiting for transfers between devices, body(): lax.all_gather(values_here, 'row', axis=0, tiled=True)  20 us
    reduce_scatter x1, waiting for transfers between devices, body(): lax.psum_scatter((routed + shared_part).astype(jnp.bfloat16), 'col', scat...  18.3 us
    all_to_all x1, waiting for transfers between devices, body(): lax.all_to_all(expert_out, 'row', 0, 0, tiled=True)  17.5 us
    dot_general x1, matrix products, body(): jnp.einsum('lgnsf,lgfd->nlsd', hidden_act, wd, preferred_element_type=jnp...  12.9 us
    all_gather x1, local copies, waits for them, and re-layouts, body(): key_piece = lax.all_gather(keys_here, 'row', axis=0, tiled=True)  8.71 us
  transfers between devices with their start and end apart: 5, of which 5 were waited for; matrix products, arithmetic and copies ran while one was open for 10% of the time, Pallas kernels for 0%

commit v1 on v0

--- a/solution.py
+++ b/solution.py
@@ -40,44 +40,53 @@
     row_index = lax.axis_index("row")
     row_count = lax.axis_size("row")
     score_scale = 1.0 / math.sqrt(HD)
-    keys_here = jnp.concatenate([cache_keys, new_keys], axis=0)
-    values_here = jnp.concatenate([cache_values, new_values], axis=0)
-    query_heads = queries.reshape(rows_here, requests, heads_here, HD)
-    local_pos = row_index * rows_here + jnp.arange(rows_here, dtype=jnp.int32)
-    key_piece = lax.all_gather(keys_here, "row", axis=0, tiled=True)
-    key_count = key_piece.shape[0]
-    global_row = jnp.arange(key_count, dtype=jnp.int32)
-    shard_index = global_row // block_rows
-    offset_rows = global_row % block_rows
+    keys_here = jnp.concatenate([cache_keys, new_keys], axis=0).reshape(
+        block_rows, requests, heads_here, HD
+    )
+    values_here = jnp.concatenate([cache_values, new_values], axis=0).reshape(
+        block_rows, requests, heads_here, HD
+    )
+    all_queries = lax.all_gather(queries, "row", axis=0, tiled=True)
+    query_count = all_queries.shape[0]
+    query_heads = all_queries.reshape(query_count, requests, heads_here, HD)
+    query_pos = jnp.arange(query_count, dtype=jnp.int32)
+    offset_rows = jnp.arange(block_rows, dtype=jnp.int32)
     in_cache = offset_rows < cache_rows
-    cache_pos = shard_index * cache_rows + offset_rows
-    new_pos = shard_index * rows_here + offset_rows - cache_rows
+    cache_pos = row_index * cache_rows + offset_rows
+    new_pos = row_index * rows_here + offset_rows - cache_rows
     cache_ok = in_cache[None, :] & (cache_pos[None, :] < cached_len[:, None])
-    new_ok = jnp.logical_not(in_cache)[None, :] & (new_pos[None, :] <= local_pos[:, None])
+    new_ok = jnp.logical_not(in_cache)[None, :] & (new_pos[None, :] <= query_pos[:, None])
     allowed = cache_ok[:, None, None, :] | new_ok[None, None, :, :]
-    key_heads = key_piece.reshape(key_count, requests, heads_here, HD)
-    value_heads = lax.all_gather(values_here, "row", axis=0, tiled=True).reshape(
-        key_count, requests, heads_here, HD
-    )
     scores = (
-        jnp.einsum("irhd,jrhd->rhij", query_heads, key_heads, preferred_element_type=jnp.float32)
+        jnp.einsum("irhd,jrhd->rhij", query_heads, keys_here, preferred_element_type=jnp.float32)
         * score_scale
     )
     masked = jnp.where(allowed, scores, -1e30)
-    old_max = jnp.full((requests, heads_here, rows_here), -1e30, jnp.float32)
-    new_max = jnp.maximum(old_max, jnp.max(masked, axis=-1))
-    weights_now = jnp.where(allowed, jnp.exp(masked - new_max[..., None]), 0.0)
-    new_sum = jnp.sum(weights_now, axis=-1)
+    block_max = jnp.max(masked, axis=-1)
+    weights_now = jnp.where(allowed, jnp.exp(masked - block_max[..., None]), 0.0)
+    block_sum = jnp.sum(weights_now, axis=-1)
     product = jnp.einsum(
-        "rhij,jrhd->rhid",
+        "rhij,jrhd->irhd",
         weights_now.astype(jnp.bfloat16),
-        value_heads,
+        values_here,
         preferred_element_type=jnp.float32,
+    ).astype(jnp.bfloat16)
+    stats = jnp.stack([block_max, block_sum], axis=-1).transpose(2, 0, 1, 3)
+    product_back = lax.all_to_all(
+        product.reshape(row_count, rows_here, requests, heads_here, HD), "row", 0, 0, tiled=True
     )
-    attended = (product / new_sum[..., None]).astype(jnp.bfloat16)
+    stats_back = lax.all_to_all(
+        stats.reshape(row_count, rows_here, requests, heads_here, 2), "row", 0, 0, tiled=True
+    )
+    part_max = stats_back[..., 0]
+    row_top = jnp.max(part_max, axis=0)
+    rescale = jnp.exp(part_max - row_top[None])
+    row_total = jnp.sum(rescale * stats_back[..., 1], axis=0)
+    summed = jnp.sum(rescale[..., None] * product_back.astype(jnp.float32), axis=0)
+    attended = (summed / row_total[..., None]).astype(jnp.bfloat16)
     head_weights = out_weight.reshape(heads_here, HD, model_width)
     attn_part = jnp.einsum(
-        "rhid,hde->ire", attended, head_weights, preferred_element_type=jnp.float32
+        "irhd,hde->ire", attended, head_weights, preferred_element_type=jnp.float32
     )
     attn_full = lax.psum(attn_part.astype(jnp.bfloat16), "col").astype(jnp.float32)
     mixed_full = (residual.astype(jnp.float32) + attn_full).astype(jnp.bfloat16)

time: 251 us -> 243 us (0.968)
  waiting for transfers between devices: 121 us -> 99 us
  starting transfers between devices: 4.45 us -> 12.6 us
  other arithmetic: 10.7 us -> 15 us
    all_gather x2 -> x1, waiting for transfers between devices: 48.1 us -> 16.8 us  [body(): all_queries = lax.all_gather(queries, 'row', axis=0, tiled=True)]
    all_gather x2 -> x1, local copies, waits for them, and re-layouts: 17.4 us -> 3.66 us  [body(): all_queries = lax.all_gather(queries, 'row', axis=0, tiled=True)]
    all_to_all x0 -> x2, waiting for transfers between devices: none -> 10.9 us  [the longest x1 10.9 us: body(): lax.all_to_all(product.reshape(row_count, rows_here, requests, heads_here...]
    all_to_all x0 -> x2, starting transfers between devices: none -> 8.2 us  [the longest x1 4.24 us: body(): lax.all_to_all(product.reshape(row_count, rows_here, requests, heads_here...]
    reshape x1 -> x5, local copies, waits for them, and re-layouts: 0.99 us -> 8.52 us  [the longest x2 2.98 us: body(): stats.reshape(row_count, rows_here, requests, heads_here, 2)]
    unnamed x19 -> x31, local copies, waits for them, and re-layouts: 4.27 us -> 5.99 us
    dot_general x2 -> x3, matrix products: 8.91 us -> 8.91 us  [the longest x1 3.95 us: body(): jnp.einsum('rhij,jrhd->irhd', weights_now.astype(jnp.bfloat16), values_he...]
  transfers between devices with their start and end apart: 5 -> 6, of which waited for: 5 -> 5; matrix products, arithmetic and copies ran while one was open for 10% -> 13% of each run, Pallas kernels for 0% -> 0%
where the time goes in v1:
time: 243 us; the launch traced here: 242 us
  waiting for transfers between devices  99 us (41%)
  matrix products  44.3 us (18%)
  local copies, waits for them, and re-layouts  32.3 us (13%)
  blocking collectives  24.4 us (10%)
  other arithmetic  15 us (6%)
  between operations  14 us (6%)
  starting transfers between devices  12.6 us (5%)
    psum x1, waiting for transfers between devices, body(): lax.psum(attn_part.astype(jnp.bfloat16), 'col').astype(jnp.float32)  34.8 us
    all_to_all x1, blocking collectives, body(): arrived = lax.all_to_all(outgoing, 'row', 0, 0, tiled=True)  24.4 us
    reduce_scatter x1, waiting for transfers between devices, body(): lax.psum_scatter((routed + shared_part).astype(jnp.bfloat16), 'col', scat...  18.3 us
    all_to_all x1, waiting for transfers between devices, body(): lax.all_to_all(expert_out, 'row', 0, 0, tiled=True)  17.5 us
    all_gather x1, waiting for transfers between devices, body(): all_queries = lax.all_gather(queries, 'row', axis=0, tiled=True)  16.8 us
    dot_general x1, matrix products, body(): jnp.einsum('lgnsf,lgfd->nlsd', hidden_act, wd, preferred_element_type=jnp...  12.9 us
    all_to_all x1, waiting for transfers between devices, body(): lax.all_to_all(product.reshape(row_count, rows_here, requests, heads_here...  10.9 us
    dot_general x1, matrix products, body(): jnp.einsum('nlsd,lgdf->lgnsf', arrived, wu, preferred_element_type=jnp.fl...  8.52 us
  transfers between devices with their start and end apart: 6, of which 5 were waited for; matrix products, arithmetic and copies ran while one was open for 13% of the time, Pallas kernels for 0%

profile of v1, /device:TPU:0, one launch (start us, length us, event | category | flops | bytes accessed | tf_op | source)
XLA Modules:
  0.0 241.7 jit_solution(18139187755410058040)
XLA Ops:
  7.2 0.7 all-gather.2.cloned.1.call-update
  7.9 0.9 copy.91
  8.9 0.7 eq.38
  9.6 0.7 eq.42
  10.3 2.3 pad_maximum_fusion
  12.6 1.2 reshape.257
  13.9 2.3 pad_maximum_fusion.1
  16.1 2.0 reshape.258
  19.4 16.8 %all-gather.2.cloned.1.call-done = bf16[512,2,512]{2,1,0:T(2,128)(2,1)} async-done(((bf16[64,2,512]{2,1,0:T(2,128)(2,1)}), bf16[512,2,512]{2,1,0:T(2,128)(2,1)}) %all-gather.2.cloned.1.call-update) | async-done | bytes 1048592 | tf_op jit(solution)/shard_map/all_gather | solution.py:49
  36.1 3.7 %copy.82 = bf16[512,2,512]{0,2,1:T(8,128)(2,1)} copy(bf16[512,2,512]{2,1,0:T(2,128)(2,1)} %all-gather.2.cloned.1.call-done) | data formatting | bytes 2097152 | tf_op jit(solution)/shard_map/all_gather | solution.py:49
  39.8 2.0 fusion
  41.9 1.6 copy-done.1
  43.5 0.8 fusion.9
  45.0 1.5 reshape.236
  46.5 1.5 copy.139
  48.0 1.6 reshape.260
  49.5 4.0 %all-to-all-start = ((f32[8,1,1024]{2,1,0:T(1,128)}), f32[8,1,1024]{2,1,0:T(1,128)}, u32[]{:S(2)}, u32[]{:S(2)}) async-start(f32[8,1,1024]{2,1,0:T(1,128)} %reshape.260), calls=%async_computation | async-start | bytes 65536 | tf_op jit(solution)/shard_map/all_to_all | solution.py:78
  53.5 3.9 %fusion.23 = bf16[512,2,4,128]{0,3,2,1:T(8,128)(2,1)} fusion(f32[2,4,192,512]{3,2,1,0:T(8,128)} %copy-done.1, f32[2,4,512]{2,1,0:T(4,128)S(1)} %get-tuple-element.16, pred[2,512,192]{1,2,0:T(8,128)(4,1)S(1)} %broadcast_or_fusion, bf16[192,2,4,128]{3,2,1,0:T(4,128)(2,1)S(1)} %copy-done.6), kind=kOutput, calls=%fused_computation.31 | convolution fusion | flops 205783040 | bytes 4800512 | tf_op jit(solution)/shard_map/rhij,jrhd->irhd/dot_general | solution.py:68
  57.5 2.3 copy.89
  59.7 2.3 copy.90
  62.1 4.2 %all-to-all-start.1 = ((bf16[8,64,2,4,128]{4,1,3,2,0:T(8,128)(2,1)}), bf16[8,64,2,4,128]{4,1,3,2,0:T(8,128)(2,1)}, u32[]{:S(2)}, u32[]{:S(2)}) async-start(bf16[8,64,2,4,128]{4,1,3,2,0:T(8,128)(2,1)} %copy.90), calls=%async_computation.1 | async-start | bytes 2097152 | tf_op jit(solution)/shard_map/all_to_all | solution.py:75
  66.4 1.8 reduce-window.6
  69.1 1.5 reduce.3
  70.8 10.9 %all-to-all-done.1 = bf16[8,64,2,4,128]{4,1,3,2,0:T(8,128)(2,1)} async-done(((bf16[8,64,2,4,128]{4,1,3,2,0:T(8,128)(2,1)}), bf16[8,64,2,4,128]{4,1,3,2,0:T(8,128)(2,1)}, u32[]{:S(2)}, u32[]{:S(2)}) %all-to-all-start.1) | async-done | bytes 1048608 | tf_op jit(solution)/shard_map/all_to_all | solution.py:75
  81.7 1.8 multiply_reduce_fusion
  83.5 3.0 %fusion.3 = bf16[64,2,2048]{2,0,1:T(8,128)(2,1)} fusion(bf16[4,128,2048,1]{2,1,0,3:T(8,128)(2,1)} %bitcast.155, f32[64,2,4,128]{3,0,2,1:T(8,128)S(1)} %multiply_reduce_fusion, f32[64,2,4]{0,2,1:T(4,128)S(1)} %fusion.54), kind=kOutput, calls=%fused_computation.10 | convolution fusion | flops 268828672 | bytes 2885632 | tf_op jit(solution)/shard_map/irhd,hde->ire/dot_general | solution.py:88
  86.6 0.7 add_select_fusion.2
  87.4 0.9 copy.95
  88.3 1.0 select_reduce_fusion
  89.3 34.8 %all-reduce.2.cloned.1.call-done = bf16[64,2,2048]{2,0,1:T(8,128)(2,1)} async-done(((bf16[64,2,2048]{2,0,1:T(8,128)(2,1)}), bf16[64,2,2048]{2,0,1:T(8,128)(2,1)}) %all-reduce.2.cloned.1.call-update) | async-done | bytes 524304 | tf_op jit(solution)/shard_map/psum | solution.py:91
  124.1 1.3 fusion.27
  125.4 0.8 copy-done.2
  126.5 1.3 copy.98
  127.8 1.2 reshape.242
  129.6 24.4 %all_to_all.20 = bf16[8,2,24,2048]{3,2,1,0:T(8,128)(2,1)S(1)} all-to-all(bf16[8,2,24,2048]{3,2,1,0:T(8,128)(2,1)S(1)} %bitcast.152), channel_id=1, replica_groups=mesh['row'=8,'col'=4] {'row'}, dimensions={0} | all-to-all | bytes 3145728 | tf_op jit(solution)/shard_map/all_to_all | solution.py:125
  154.1 8.5 %fusion.20 = f32[2,8,24,4,352]{4,2,3,1,0:T(8,128)} fusion(bf16[2,4,2048,352,1]{2,3,1,4,0:T(8,128)(2,1)} %bitcast.163, bf16[8,2,24,2048]{3,2,1,0:T(8,128)(2,1)S(1)} %all_to_all.20), kind=kOutput, calls=%fused_computation.28 | convolution fusion | flops 2214592512 | bytes 15269888 | tf_op jit(solution)/shard_map/nlsd,lgdf->lgnsf/dot_general | solution.py:131
  162.6 12.9 %fusion.1 = bf16[8,2,24,2048]{3,2,0,1:T(8,128)(2,1)} fusion(bf16[2,4,352,2048,1]{3,2,1,4,0:T(8,128)(2,1)} %bitcast.164, f32[2,8,24,4,352]{4,2,3,1,0:T(8,128)} %fusion.20, bf16[2,4,2048,352,1]{2,3,1,4,0:T(8,128)(2,1)} %bitcast.165, bf16[8,2,24,2048]{3,2,1,0:T(8,128)(2,1)} %copy-done.4), kind=kOutput, calls=%fused_computation.5 | convolution fusion | flops 4433215488 | bytes 28377088 | tf_op jit(solution)/shard_map/lgnsf,lgfd->nlsd/dot_general | solution.py:133
  175.5 2.7 %copy.101 = bf16[8,2,24,2048]{3,2,1,0:T(8,128)(2,1)} copy(bf16[8,2,24,2048]{3,2,0,1:T(8,128)(2,1)} %fusion.1) | data formatting | bytes 3145728 | tf_op jit(solution)/shard_map/convert_element_type | solution.py:135
  178.2 4.3 %all-to-all-start.3 = ((bf16[8,2,24,2048]{3,2,1,0:T(8,128)(2,1)}), bf16[8,2,24,2048]{3,2,1,0:T(8,128)(2,1)}, u32[]{:S(2)}, u32[]{:S(2)}) async-start(bf16[8,2,24,2048]{3,2,1,0:T(8,128)(2,1)} %copy.101), calls=%async_computation.3 | async-start | bytes 3145728 | tf_op jit(solution)/shard_map/all_to_all | solution.py:136
  182.6 3.5 %fusion.63 = f32[128,704]{0,1:T(8,128)} fusion(bf16[128,2048]{1,0:T(8,128)(2,1)S(1)} %reshape.242, bf16[2048,704]{0,1:T(8,128)(2,1)} %param.31), kind=kOutput, calls=%fused_computation.112 | convolution fusion | flops 369098752 | bytes 3768320 | tf_op jit(solution)/shard_map/dot_general | solution.py:142
  186.1 17.5 %all-to-all-done.3 = bf16[8,2,24,2048]{3,2,1,0:T(8,128)(2,1)} async-done(((bf16[8,2,24,2048]{3,2,1,0:T(8,128)(2,1)}), bf16[8,2,24,2048]{3,2,1,0:T(8,128)(2,1)}, u32[]{:S(2)}, u32[]{:S(2)}) %all-to-all-start.3) | async-done | bytes 1572896 | tf_op jit(solution)/shard_map/all_to_all | solution.py:136
  203.6 2.0 fusion.51
  205.6 2.8 %convolution_add_fusion.1 = f32[128,2048]{1,0:T(8,128)} fusion(f32[128,2048]{1,0:T(8,128)S(1)} %fusion.51, bf16[384,2048]{1,0:T(8,128)(2,1)} %bitcast.32, f32[128,384]{1,0:T(8,128)S(1)} %copy-done.3), kind=kOutput, calls=%fused_computation.7 | convolution fusion | flops 201785344 | bytes 3866624 | tf_op jit(solution)/shard_map/dot_general | solution.py:139
  208.4 5.1 %fusion.2 = bf16[128,2048]{1,0:T(8,128)(2,1)} fusion(f32[128,2048]{1,0:T(8,128)} %convolution_add_fusion.1, bf16[704,2048]{1,0:T(8,128)(2,1)S(1)} %copy-done, bf16[128,2048]{1,0:T(8,128)(2,1)S(1)} %reshape.242, bf16[2048,704]{0,1:T(8,128)(2,1)} %param.32, f32[128,704]{0,1:T(8,128)} %fusion.63), kind=kOutput, calls=%fused_computation.9 | convolution fusion | flops 739262464 | bytes 8224768 | tf_op jit(solution)/shard_map/dot_general | solution.py:145
  213.6 0.9 constant_dynamic-slice_fusion
  214.5 0.8 copy.102
  215.3 18.3 %reduce-scatter.2.cloned.1.call-done = bf16[128,512]{1,0:T(8,128)(2,1)} async-done(((bf16[128,2048]{1,0:T(8,128)(2,1)}), bf16[128,512]{1,0:T(8,128)(2,1)}) %reduce-scatter.2.cloned.1.call-update) | async-done | bytes 131088 | tf_op jit(solution)/shard_map/reduce_scatter | solution.py:146
  233.5 1.6 reshape.248
  (56 shorter events, 4.1 us)
Async XLA Ops:
  7.2 201.2 %copy-start = (bf16[704,2048]{1,0:T(8,128)(2,1)S(1)}, bf16[704,2048]{1,0:T(8,128)(2,1)}, u32[]{:S(2)}) copy-start(bf16[704,2048]{1,0:T(8,128)(2,1)} %param.33) | copy-start | bytes 8650756
  7.2 11.0 %copy-start.11 = (f32[64,2,6]{0,1,2:T(2,128)S(1)}, f32[64,2,6]{0,1,2:T(2,128)}, u32[]{:S(2)}) copy-start(f32[64,2,6]{0,1,2:T(2,128)} %param.27) | copy-start | bytes 9220
  7.2 11.8 %copy-start.12 = (s32[2]{0:T(128)S(1)}, s32[2]{0:T(128)}, u32[]{:S(2)}) copy-start(s32[2]{0:T(128)} %param.22) | copy-start | bytes 28
  7.2 28.9 %all-gather.2.cloned.1.call-start = ((), (), s32[]{:S(2)}) async-start(), calls=%async_computation.5 | async-start | bytes 1179648 | tf_op jit(solution)/shard_map/all_gather | solution.py:49
  41.8 1.7 copy-start.1
  41.8 11.7 %copy-start.6 = (bf16[192,2,4,128]{3,2,1,0:T(4,128)(2,1)S(1)}, bf16[192,2,4,128]{3,2,1,0:T(4,128)(2,1)}, u32[]{:S(2)}) copy-start(bf16[192,2,4,128]{3,2,1,0:T(4,128)(2,1)} %reshape.258) | copy-start | bytes 1179652
  49.5 12.5 %all-to-all-start = ((f32[8,1,1024]{2,1,0:T(1,128)}), f32[8,1,1024]{2,1,0:T(1,128)}, u32[]{:S(2)}, u32[]{:S(2)}) async-start(f32[8,1,1024]{2,1,0:T(1,128)} %reshape.260), calls=%async_computation | async-start | bytes 65536 | tf_op jit(solution)/shard_map/all_to_all | solution.py:78
  59.7 6.6 %copy-start.9 = (s32[6,128]{1,0:T(8,128)S(1)}, s32[6,128]{1,0:T(8,128)}, u32[]{:S(2)}) copy-start(s32[6,128]{1,0:T(8,128)} %eq.42) | copy-start | bytes 9220
  59.7 8.8 %copy-start.8 = (s32[768]{0:T(1024)S(1)}, s32[768]{0:T(1024)}, u32[]{:S(2)}) copy-start(s32[768]{0:T(1024)} %eq.38) | copy-start | bytes 9220
  62.1 19.7 %all-to-all-start.1 = ((bf16[8,64,2,4,128]{4,1,3,2,0:T(8,128)(2,1)}), bf16[8,64,2,4,128]{4,1,3,2,0:T(8,128)(2,1)}, u32[]{:S(2)}, u32[]{:S(2)}) async-start(bf16[8,64,2,4,128]{4,1,3,2,0:T(8,128)(2,1)} %copy.90), calls=%async_computation.1 | async-start | bytes 2097152 | tf_op jit(solution)/shard_map/all_to_all | solution.py:75
  66.3 57.8 %all-reduce.2.cloned.1.call-start = ((), (), s32[]{:S(2)}) async-start(), calls=%async_computation.6 | async-start | bytes 1048576 | tf_op jit(solution)/shard_map/psum | solution.py:91
  70.8 17.5 %copy-start.7 = (f32[128,6]{0,1:T(8,128)S(1)}, f32[128,6]{0,1:T(8,128)}, u32[]{:S(2)}) copy-start(f32[128,6]{0,1:T(8,128)} %copy.97) | copy-start | bytes 9220
  83.5 40.6 %copy-start.5 = (bf16[64,2,2048]{2,1,0:T(2,128)(2,1)S(1)}, bf16[64,2,2048]{2,1,0:T(2,128)(2,1)}, u32[]{:S(2)}) copy-start(bf16[64,2,2048]{2,1,0:T(2,128)(2,1)} %param.23) | copy-start | bytes 1572868
  83.5 42.8 %copy-start.10 = (f32[2048]{0:T(1024)S(1)}, f32[2048]{0:T(1024)}, u32[]{:S(2)}) copy-start(f32[2048]{0:T(1024)} %param.25) | copy-start | bytes 24580
  125.4 0.8 copy-start.2
  154.1 8.5 %copy-start.4 = (bf16[8,2,24,2048]{3,2,1,0:T(8,128)(2,1)}, bf16[8,2,24,2048]{3,2,1,0:T(8,128)(2,1)S(1)}, u32[]{:S(2)}) copy-start(bf16[8,2,24,2048]{3,2,1,0:T(8,128)(2,1)S(1)} %all_to_all.20) | copy-start | bytes 4718596
  178.2 25.3 %all-to-all-start.3 = ((bf16[8,2,24,2048]{3,2,1,0:T(8,128)(2,1)}), bf16[8,2,24,2048]{3,2,1,0:T(8,128)(2,1)}, u32[]{:S(2)}, u32[]{:S(2)}) async-start(bf16[8,2,24,2048]{3,2,1,0:T(8,128)(2,1)} %copy.101), calls=%async_computation.3 | async-start | bytes 3145728 | tf_op jit(solution)/shard_map/all_to_all | solution.py:136
  182.5 51.0 %reduce-scatter.2.cloned.1.call-start = ((), (), s32[]{:S(2)}) async-start(), calls=%async_computation.7 | async-start | bytes 655360 | tf_op jit(solution)/shard_map/reduce_scatter | solution.py:146
  203.6 2.0 copy-start.3
Sparse Core Ops, SparseCore 0:
  9.9 26.1 all-gather.1
  86.6 37.4 all-reduce.1
  213.7 19.8 reduce-scatter.1

commit v2 on v1

--- a/solution.py
+++ b/solution.py
@@ -46,8 +46,10 @@
     values_here = jnp.concatenate([cache_values, new_values], axis=0).reshape(
         block_rows, requests, heads_here, HD
     )
-    all_queries = lax.all_gather(queries, "row", axis=0, tiled=True)
-    query_count = all_queries.shape[0]
+    all_queries = lax.all_to_all(
+        jnp.broadcast_to(queries[None], (row_count,) + queries.shape), "row", 0, 0, tiled=True
+    )
+    query_count = row_count * rows_here
     query_heads = all_queries.reshape(query_count, requests, heads_here, HD)
     query_pos = jnp.arange(query_count, dtype=jnp.int32)
     offset_rows = jnp.arange(block_rows, dtype=jnp.int32)
@@ -88,18 +90,37 @@
     attn_part = jnp.einsum(
         "irhd,hde->ire", attended, head_weights, preferred_element_type=jnp.float32
     )
-    attn_full = lax.psum(attn_part.astype(jnp.bfloat16), "col").astype(jnp.float32)
-    mixed_full = (residual.astype(jnp.float32) + attn_full).astype(jnp.bfloat16)
+    col_index = lax.axis_index("col")
+    col_count = lax.axis_size("col")
+    col_width = model_width // col_count
+    token_count = rows_here * requests
+    attn_chunks = (
+        attn_part.astype(jnp.bfloat16)
+        .reshape(token_count, col_count, col_width)
+        .transpose(1, 0, 2)
+    )
+    attn_summed = jnp.sum(
+        lax.all_to_all(attn_chunks, "col", 0, 0, tiled=True).astype(jnp.float32), axis=0
+    )
+    residual_here = lax.dynamic_slice_in_dim(
+        residual.reshape(token_count, model_width), col_index * col_width, col_width, 1
+    )
+    mixed_slice = (residual_here.astype(jnp.float32) + attn_summed).astype(jnp.bfloat16)
+    mixed_gathered = lax.all_to_all(
+        jnp.broadcast_to(mixed_slice[None], (col_count, token_count, col_width)),
+        "col",
+        0,
+        0,
+        tiled=True,
+    )
+    mixed_full = mixed_gathered.transpose(1, 0, 2).reshape(token_count, model_width)
     mixed_f32 = mixed_full.astype(jnp.float32)
     normed = (
         mixed_f32
         * lax.rsqrt(jnp.mean(mixed_f32 * mixed_f32, axis=-1, keepdims=True) + 1e-06)
         * norm_gain
     ).astype(jnp.bfloat16)
-    token_count = rows_here * requests
-    tokens = normed.reshape(token_count, model_width)
-    col_index = lax.axis_index("col")
-    col_count = lax.axis_size("col")
+    tokens = normed
     entries_here = w_gate.shape[0]
     experts_dev = max(1, entries_here // GROUPS)
     groups_dev = entries_here // experts_dev
@@ -143,12 +164,17 @@
     shared_u = jnp.dot(tokens, shared_up, preferred_element_type=jnp.float32)
     shared_act = (jax.nn.silu(shared_g) * shared_u).astype(jnp.bfloat16)
     shared_part = jnp.dot(shared_act, shared_down, preferred_element_type=jnp.float32)
-    ffn_total = lax.psum_scatter(
-        (routed + shared_part).astype(jnp.bfloat16), "col", scatter_dimension=1, tiled=True
-    )
-    col_width = model_width // col_count
-    ffn_here = ffn_total.reshape(rows_here, requests, col_width)
-    mixed_here = lax.dynamic_slice_in_dim(mixed_full, col_index * col_width, col_width, 2)
+    ffn_chunks = (
+        (routed + shared_part)
+        .astype(jnp.bfloat16)
+        .reshape(token_count, col_count, col_width)
+        .transpose(1, 0, 2)
+    )
+    ffn_total = jnp.sum(
+        lax.all_to_all(ffn_chunks, "col", 0, 0, tiled=True).astype(jnp.float32), axis=0
+    )
+    ffn_here = ffn_total.astype(jnp.bfloat16).reshape(rows_here, requests, col_width)
+    mixed_here = mixed_slice.reshape(rows_here, requests, col_width)
     return (mixed_here, ffn_here)
 
 

time: 243 us -> 221 us (0.909)
  waiting for transfers between devices: 99 us -> 58.4 us
  starting transfers between devices: 12.6 us -> 29.4 us
  between operations: 14 us -> 0.98 us
  local copies, waits for them, and re-layouts: 32.3 us -> 39.4 us
  other arithmetic: 15 us -> 18.6 us
  blocking collectives: 24.4 us -> 27.6 us
    psum x1 -> x0, waiting for transfers between devices: 34.8 us -> none  [body(): lax.psum(attn_part.astype(jnp.bfloat16), 'col').astype(jnp.float32)]
    all_to_all x0 -> x4, waiting for transfers between devices: none -> 26.8 us  [the longest x1 11.1 us: body(): lax.all_to_all(ffn_chunks, 'col', 0, 0, tiled=True).astype(jnp.float32)]
    reduce_scatter x1 -> x0, waiting for transfers between devices: 18.3 us -> none  [body(): lax.psum_scatter((routed + shared_part).astype(jnp.bfloat16), 'col', scat...]
    all_to_all x0 -> x4, starting transfers between devices: none -> 17.5 us  [the longest x1 5.3 us: body(): lax.all_to_all(jnp.broadcast_to(queries[None], (row_count,) + queries.sha...]
    all_gather x1 -> x0, waiting for transfers between devices: 16.8 us -> none  [body(): all_queries = lax.all_gather(queries, 'row', axis=0, tiled=True)]
    reshape x2 -> x6, local copies, waits for them, and re-layouts: 2.85 us -> 8.67 us  [the longest x1 2.16 us: body(): query_heads = all_queries.reshape(query_count, requests, heads_here, HD)]
    all_gather x1 -> x0, local copies, waits for them, and re-layouts: 3.66 us -> none  [body(): all_queries = lax.all_gather(queries, 'row', axis=0, tiled=True)]
    all_to_all x1, blocking collectives: 24.4 us -> 27.6 us  [body(): arrived = lax.all_to_all(outgoing, 'row', 0, 0, tiled=True)]
  transfers between devices with their start and end apart: 6 -> 7, of which waited for: 5 -> 6; matrix products, arithmetic and copies ran while one was open for 13% -> 17% of each run, Pallas kernels for 0% -> 0%
where the time goes in v2:
time: 221 us; the launch traced here: 219 us
  waiting for transfers between devices  58.4 us (26%)
  matrix products  44.4 us (20%)
  local copies, waits for them, and re-layouts  39.4 us (18%)
  starting transfers between devices  29.4 us (13%)
  blocking collectives  27.6 us (12%)
  other arithmetic  18.6 us (8%)
    all_to_all x1, blocking collectives, body(): arrived = lax.all_to_all(outgoing, 'row', 0, 0, tiled=True)  27.6 us
    all_to_all x1, waiting for transfers between devices, body(): lax.all_to_all(expert_out, 'row', 0, 0, tiled=True)  17.6 us
    all_to_all x1, waiting for transfers between devices, body(): lax.all_to_all(product.reshape(row_count, rows_here, requests, heads_here...  14 us
    dot_general x1, matrix products, body(): jnp.einsum('lgnsf,lgfd->nlsd', hidden_act, wd, preferred_element_type=jnp...  12.9 us
    all_to_all x1, waiting for transfers between devices, body(): lax.all_to_all(ffn_chunks, 'col', 0, 0, tiled=True).astype(jnp.float32)  11.1 us
    all_to_all x1, waiting for transfers between devices, body(): lax.all_to_all(jnp.broadcast_to(queries[None], (row_count,) + queries.sha...  9.38 us
    dot_general x1, matrix products, body(): jnp.einsum('nlsd,lgdf->lgnsf', arrived, wu, preferred_element_type=jnp.fl...  8.52 us
    unnamed x31, local copies, waits for them, and re-layouts  6.47 us
  transfers between devices with their start and end apart: 7, of which 6 were waited for; matrix products, arithmetic and copies ran while one was open for 17% of the time, Pallas kernels for 0%

profile of v2, /device:TPU:0, one launch (start us, length us, event | category | flops | bytes accessed | tf_op | source)
XLA Modules:
  0.0 218.7 jit_solution(14638649557254309013)
XLA Ops:
  0.7 1.1 copy.85
  1.7 1.1 broadcast_in_dim.35
  2.9 5.3 %all-to-all-start = ((bf16[8,64,2,512]{3,1,2,0:T(8,128)(2,1)}), bf16[8,64,2,512]{3,1,2,0:T(8,128)(2,1)}, u32[]{:S(2)}, u32[]{:S(2)}) async-start(bf16[8,64,2,512]{3,1,2,0:T(8,128)(2,1)} %broadcast_in_dim.35), calls=%async_computation | async-start | bytes 2097152 | tf_op jit(solution)/shard_map/all_to_all | solution.py:49
  8.2 1.3 pad_maximum_fusion
  9.5 1.4 pad_maximum_fusion.1
  10.9 2.0 reshape.275
  14.3 9.4 %all-to-all-done = bf16[8,64,2,512]{3,1,2,0:T(8,128)(2,1)} async-done(((bf16[8,64,2,512]{3,1,2,0:T(8,128)(2,1)}), bf16[8,64,2,512]{3,1,2,0:T(8,128)(2,1)}, u32[]{:S(2)}, u32[]{:S(2)}) %all-to-all-start) | async-done | bytes 1048608 | tf_op jit(solution)/shard_map/all_to_all | solution.py:49
  23.7 2.4 %copy.86 = bf16[8,64,2,512]{3,1,0,2:T(8,128)(2,1)} copy(bf16[8,64,2,512]{3,1,2,0:T(8,128)(2,1)} %all-to-all-done) | data formatting | bytes 2097152 | tf_op jit(solution)/shard_map/all_to_all | solution.py:49
  26.1 2.2 reshape.250
  28.2 2.0 fusion
  30.3 1.6 copy-done.2
  34.9 1.6 reshape.278
  36.5 3.3 %all-to-all-start.1 = ((f32[8,1,1024]{2,1,0:T(1,128)}), f32[8,1,1024]{2,1,0:T(1,128)S(1)}, u32[]{:S(2)}, u32[]{:S(2)}) async-start(f32[8,1,1024]{2,1,0:T(1,128)} %reshape.278), calls=%async_computation.1 | async-start | bytes 65536 | tf_op jit(solution)/shard_map/all_to_all | solution.py:80
  39.9 3.9 %fusion.23 = bf16[512,2,4,128]{0,3,2,1:T(8,128)(2,1)} fusion(f32[2,4,192,512]{3,2,1,0:T(8,128)} %copy-done.2, f32[2,4,512]{2,1,0:T(4,128)S(1)} %get-tuple-element.4, pred[2,512,192]{1,2,0:T(8,128)(4,1)S(1)} %broadcast_or_fusion, bf16[192,2,4,128]{3,2,1,0:T(4,128)(2,1)S(1)} %copy-done.6), kind=kOutput, calls=%fused_computation.31 | convolution fusion | flops 205783040 | bytes 4800512 | tf_op jit(solution)/shard_map/rhij,jrhd->irhd/dot_general | solution.py:70
  43.8 2.3 %copy.93 = bf16[512,2,4,128]{3,0,2,1:T(8,128)(2,1)} copy(bf16[512,2,4,128]{0,3,2,1:T(8,128)(2,1)} %fusion.23) | data formatting | bytes 2097152 | tf_op jit(solution)/shard_map/convert_element_type | solution.py:75
  46.1 2.4 %copy.94 = bf16[8,64,2,4,128]{4,1,3,2,0:T(8,128)(2,1)} copy(bf16[8,64,2,4,128]{4,1,0,3,2:T(8,128)(2,1)} %bitcast.171) | data formatting | bytes 2097152 | tf_op jit(solution)/shard_map/reshape | solution.py:78
  48.4 4.2 %all-to-all-start.2 = ((bf16[8,64,2,4,128]{4,1,3,2,0:T(8,128)(2,1)}), bf16[8,64,2,4,128]{4,1,3,2,0:T(8,128)(2,1)}, u32[]{:S(2)}, u32[]{:S(2)}) async-start(bf16[8,64,2,4,128]{4,1,3,2,0:T(8,128)(2,1)} %copy.94), calls=%async_computation.2 | async-start | bytes 2097152 | tf_op jit(solution)/shard_map/all_to_all | solution.py:77
  54.1 14.0 %all-to-all-done.2 = bf16[8,64,2,4,128]{4,1,3,2,0:T(8,128)(2,1)} async-done(((bf16[8,64,2,4,128]{4,1,3,2,0:T(8,128)(2,1)}), bf16[8,64,2,4,128]{4,1,3,2,0:T(8,128)(2,1)}, u32[]{:S(2)}, u32[]{:S(2)}) %all-to-all-start.2) | async-done | bytes 1048608 | tf_op jit(solution)/shard_map/all_to_all | solution.py:77
  68.1 1.8 multiply_reduce_fusion
  69.9 2.1 fusion.3
  72.5 1.1 reshape.255
  73.7 1.9 copy.96
  75.6 5.3 %all-to-all-start.3 = ((bf16[4,128,512]{2,1,0:T(8,128)(2,1)}), bf16[4,128,512]{2,1,0:T(8,128)(2,1)S(1)}, u32[]{:S(2)}, u32[]{:S(2)}) async-start(bf16[4,128,512]{2,1,0:T(8,128)(2,1)} %copy.96), calls=%async_computation.3 | async-start | bytes 1048576 | tf_op jit(solution)/shard_map/all_to_all | solution.py:103
  80.9 2.0 reshape.248
  83.9 4.4 %reduce-window.6 = s32[64,6,128]{2,0,1:T(8,128)} reduce-window(s32[64,6,128]{2,0,1:T(8,128)} %fusion.41, s32[]{:T(128)} %constant.32.clone.1), window={size=1x1x128 pad=0_0x0_0x127_0}, to_apply=%region_6.7 | reduce-window | flops 6242304 | bytes 393220 | tf_op jit(solution)/shard_map/reduce-window
  88.3 4.2 %all-to-all-done.3 = bf16[4,128,512]{2,1,0:T(8,128)(2,1)S(1)} async-done(((bf16[4,128,512]{2,1,0:T(8,128)(2,1)}), bf16[4,128,512]{2,1,0:T(8,128)(2,1)S(1)}, u32[]{:S(2)}, u32[]{:S(2)}) %all-to-all-start.3) | async-done | bytes 524320 | tf_op jit(solution)/shard_map/all_to_all | solution.py:103
  94.4 3.5 %all-to-all-start.4 = ((bf16[4,128,512]{1,2,0:T(8,128)(2,1)}), bf16[4,128,512]{1,2,0:T(8,128)(2,1)S(1)}, u32[]{:S(2)}, u32[]{:S(2)}) async-start(bf16[4,128,512]{1,2,0:T(8,128)(2,1)} %broadcast_in_dim.69), calls=%async_computation.4 | async-start | bytes 1048576 | tf_op jit(solution)/shard_map/all_to_all | solution.py:109
  97.9 1.2 slice_reduce_fusion
  100.1 1.1 fusion.40
  101.9 1.6 add_select_fusion.2
  104.4 1.4 copy.103
  106.8 1.0 select_reduce_fusion
  107.8 2.2 %all-to-all-done.4 = bf16[4,128,512]{1,2,0:T(8,128)(2,1)S(1)} async-done(((bf16[4,128,512]{1,2,0:T(8,128)(2,1)}), bf16[4,128,512]{1,2,0:T(8,128)(2,1)S(1)}, u32[]{:S(2)}, u32[]{:S(2)}) %all-to-all-start.4) | async-done | bytes 524320 | tf_op jit(solution)/shard_map/all_to_all | solution.py:109
  110.8 1.4 fusion.28
  112.2 1.5 convolution_convert_fusion
  113.7 27.6 %all_to_all.40 = bf16[8,2,24,2048]{3,2,1,0:T(8,128)(2,1)S(1)} all-to-all(bf16[8,2,24,2048]{3,2,1,0:T(8,128)(2,1)S(1)} %bitcast.170), channel_id=1, replica_groups=mesh['row'=8,'col'=4] {'row'}, dimensions={0} | all-to-all | bytes 3145728 | tf_op jit(solution)/shard_map/all_to_all | solution.py:146
  141.3 8.5 %fusion.20 = f32[2,8,24,4,352]{4,2,3,1,0:T(8,128)} fusion(bf16[2,4,2048,352,1]{2,3,1,4,0:T(8,128)(2,1)} %bitcast.183, bf16[8,2,24,2048]{3,2,1,0:T(8,128)(2,1)S(1)} %all_to_all.40), kind=kOutput, calls=%fused_computation.28 | convolution fusion | flops 2214592512 | bytes 15269888 | tf_op jit(solution)/shard_map/nlsd,lgdf->lgnsf/dot_general | solution.py:152
  149.8 12.9 %fusion.1 = bf16[8,2,24,2048]{3,2,0,1:T(8,128)(2,1)} fusion(bf16[2,4,352,2048,1]{3,2,1,4,0:T(8,128)(2,1)} %bitcast.184, f32[2,8,24,4,352]{4,2,3,1,0:T(8,128)} %fusion.20, bf16[2,4,2048,352,1]{2,3,1,4,0:T(8,128)(2,1)} %bitcast.185, bf16[8,2,24,2048]{3,2,1,0:T(8,128)(2,1)} %copy-done.4), kind=kOutput, calls=%fused_computation.5 | convolution fusion | flops 4433215488 | bytes 28377088 | tf_op jit(solution)/shard_map/lgnsf,lgfd->nlsd/dot_general | solution.py:154
  162.7 2.7 %copy.108 = bf16[8,2,24,2048]{3,2,1,0:T(8,128)(2,1)} copy(bf16[8,2,24,2048]{3,2,0,1:T(8,128)(2,1)} %fusion.1) | data formatting | bytes 3145728 | tf_op jit(solution)/shard_map/convert_element_type | solution.py:156
  165.5 4.3 %all-to-all-start.6 = ((bf16[8,2,24,2048]{3,2,1,0:T(8,128)(2,1)}), bf16[8,2,24,2048]{3,2,1,0:T(8,128)(2,1)}, u32[]{:S(2)}, u32[]{:S(2)}) async-start(bf16[8,2,24,2048]{3,2,1,0:T(8,128)(2,1)} %copy.108), calls=%async_computation.6 | async-start | bytes 3145728 | tf_op jit(solution)/shard_map/all_to_all | solution.py:157
  169.8 3.5 %fusion.63 = f32[128,704]{0,1:T(8,128)} fusion(bf16[2048,704]{0,1:T(8,128)(2,1)} %param.31, bf16[128,2048]{0,1:T(8,128)(2,1)S(1)} %fusion.28), kind=kOutput, calls=%fused_computation.113 | convolution fusion | flops 369098752 | bytes 3768320 | tf_op jit(solution)/shard_map/dot_general | solution.py:163
  173.2 17.6 %all-to-all-done.6 = bf16[8,2,24,2048]{3,2,1,0:T(8,128)(2,1)} async-done(((bf16[8,2,24,2048]{3,2,1,0:T(8,128)(2,1)}), bf16[8,2,24,2048]{3,2,1,0:T(8,128)(2,1)}, u32[]{:S(2)}, u32[]{:S(2)}) %all-to-all-start.6) | async-done | bytes 1572896 | tf_op jit(solution)/shard_map/all_to_all | solution.py:157
  190.8 2.0 fusion.51
  192.8 2.8 %convolution_add_fusion.1 = f32[128,2048]{1,0:T(8,128)} fusion(f32[128,2048]{1,0:T(8,128)S(1)} %fusion.51, bf16[384,2048]{1,0:T(8,128)(2,1)} %bitcast.34, f32[128,384]{1,0:T(8,128)S(1)} %copy-done.3), kind=kOutput, calls=%fused_computation.7 | convolution fusion | flops 201785344 | bytes 3866624 | tf_op jit(solution)/shard_map/dot_general | solution.py:160
  195.6 5.1 %fusion.2 = bf16[128,2048]{1,0:T(8,128)(2,1)} fusion(f32[128,2048]{1,0:T(8,128)} %convolution_add_fusion.1, bf16[704,2048]{1,0:T(8,128)(2,1)S(1)} %copy-done, bf16[2048,704]{0,1:T(8,128)(2,1)} %param.32, bf16[128,2048]{0,1:T(8,128)(2,1)S(1)} %fusion.28, f32[128,704]{0,1:T(8,128)} %fusion.63), kind=kOutput, calls=%fused_computation.9 | convolution fusion | flops 739262464 | bytes 8224768 | tf_op jit(solution)/shard_map/dot_general | solution.py:166
  200.8 1.9 copy.150
  202.7 3.5 %all-to-all-start.7 = ((bf16[4,128,512]{2,1,0:T(8,128)(2,1)}), bf16[4,128,512]{2,1,0:T(8,128)(2,1)S(1)}, u32[]{:S(2)}, u32[]{:S(2)}) async-start(bf16[4,128,512]{2,1,0:T(8,128)(2,1)} %bitcast.174), calls=%async_computation.7 | async-start | bytes 1048576 | tf_op jit(solution)/shard_map/all_to_all | solution.py:174
  206.9 11.1 %all-to-all-done.7 = bf16[4,128,512]{2,1,0:T(8,128)(2,1)S(1)} async-done(((bf16[4,128,512]{2,1,0:T(8,128)(2,1)}), bf16[4,128,512]{2,1,0:T(8,128)(2,1)S(1)}, u32[]{:S(2)}, u32[]{:S(2)}) %all-to-all-start.7) | async-done | bytes 524320 | tf_op jit(solution)/shard_map/all_to_all | solution.py:174
  (65 shorter events, 15.2 us)
Async XLA Ops:
  0.6 195.0 %copy-start = (bf16[704,2048]{1,0:T(8,128)(2,1)S(1)}, bf16[704,2048]{1,0:T(8,128)(2,1)}, u32[]{:S(2)}) copy-start(bf16[704,2048]{1,0:T(8,128)(2,1)} %param.33) | copy-start | bytes 8650756
  0.6 7.6 %copy-start.10 = (bf16[64,2,512]{2,1,0:T(2,128)(2,1)S(1)}, bf16[64,2,512]{2,1,0:T(2,128)(2,1)}, u32[]{:S(2)}) copy-start(bf16[64,2,512]{2,1,0:T(2,128)(2,1)} %param.18) | copy-start | bytes 393220
  0.7 7.6 %copy-start.8 = (bf16[128,2,512]{2,1,0:T(2,128)(2,1)S(1)}, bf16[128,2,512]{2,1,0:T(2,128)(2,1)}, u32[]{:S(2)}) copy-start(bf16[128,2,512]{2,1,0:T(2,128)(2,1)} %param.20) | copy-start | bytes 786436
  0.7 8.8 %copy-start.9 = (bf16[128,2,512]{2,1,0:T(2,128)(2,1)S(1)}, bf16[128,2,512]{2,1,0:T(2,128)(2,1)}, u32[]{:S(2)}) copy-start(bf16[128,2,512]{2,1,0:T(2,128)(2,1)} %param.21) | copy-start | bytes 786436
  2.9 11.0 %copy-start.12 = (s32[2]{0:T(128)S(1)}, s32[2]{0:T(128)}, u32[]{:S(2)}) copy-start(s32[2]{0:T(128)} %param.22) | copy-start | bytes 28
  2.9 20.8 %all-to-all-start = ((bf16[8,64,2,512]{3,1,2,0:T(8,128)(2,1)}), bf16[8,64,2,512]{3,1,2,0:T(8,128)(2,1)}, u32[]{:S(2)}, u32[]{:S(2)}) async-start(bf16[8,64,2,512]{3,1,2,0:T(8,128)(2,1)} %broadcast_in_dim.35), calls=%async_computation | async-start | bytes 2097152 | tf_op jit(solution)/shard_map/all_to_all | solution.py:49
  13.9 14.3 %copy-start.7 = (bf16[192,2,4,128]{3,2,1,0:T(4,128)(2,1)S(1)}, bf16[192,2,4,128]{3,2,1,0:T(4,128)(2,1)}, u32[]{:S(2)}) copy-start(bf16[192,2,4,128]{3,2,1,0:T(4,128)(2,1)} %reshape.275) | copy-start | bytes 1179652
  30.3 1.7 copy-start.2
  30.3 9.6 %copy-start.6 = (bf16[192,2,4,128]{3,2,1,0:T(4,128)(2,1)S(1)}, bf16[192,2,4,128]{3,2,1,0:T(4,128)(2,1)}, u32[]{:S(2)}) copy-start(bf16[192,2,4,128]{3,2,1,0:T(4,128)(2,1)} %reshape.276) | copy-start | bytes 1179652
  36.5 11.9 %all-to-all-start.1 = ((f32[8,1,1024]{2,1,0:T(1,128)}), f32[8,1,1024]{2,1,0:T(1,128)S(1)}, u32[]{:S(2)}, u32[]{:S(2)}) async-start(f32[8,1,1024]{2,1,0:T(1,128)} %reshape.278), calls=%async_computation.1 | async-start | bytes 65536 | tf_op jit(solution)/shard_map/all_to_all | solution.py:80
  48.4 19.7 %all-to-all-start.2 = ((bf16[8,64,2,4,128]{4,1,3,2,0:T(8,128)(2,1)}), bf16[8,64,2,4,128]{4,1,3,2,0:T(8,128)(2,1)}, u32[]{:S(2)}, u32[]{:S(2)}) async-start(bf16[8,64,2,4,128]{4,1,3,2,0:T(8,128)(2,1)} %copy.94), calls=%async_computation.2 | async-start | bytes 2097152 | tf_op jit(solution)/shard_map/all_to_all | solution.py:77
  72.5 10.4 %copy-start.11 = (s32[64,2,6]{0,1,2:T(2,128)S(1)}, s32[64,2,6]{0,1,2:T(2,128)}, u32[]{:S(2)}) copy-start(s32[64,2,6]{0,1,2:T(2,128)} %param.26) | copy-start | bytes 9220
  75.6 16.8 %all-to-all-start.3 = ((bf16[4,128,512]{2,1,0:T(8,128)(2,1)}), bf16[4,128,512]{2,1,0:T(8,128)(2,1)S(1)}, u32[]{:S(2)}, u32[]{:S(2)}) async-start(bf16[4,128,512]{2,1,0:T(8,128)(2,1)} %copy.96), calls=%async_computation.3 | async-start | bytes 1048576 | tf_op jit(solution)/shard_map/all_to_all | solution.py:103
  83.0 9.4 %copy-start.5 = (s32[64,2,6]{2,1,0:T(2,128)}, s32[64,2,6]{2,1,0:T(2,128)S(1)}, u32[]{:S(2)}) copy-start(s32[64,2,6]{2,1,0:T(2,128)S(1)} %copy.98) | copy-start | bytes 9220
  94.4 15.6 %all-to-all-start.4 = ((bf16[4,128,512]{1,2,0:T(8,128)(2,1)}), bf16[4,128,512]{1,2,0:T(8,128)(2,1)S(1)}, u32[]{:S(2)}, u32[]{:S(2)}) async-start(bf16[4,128,512]{1,2,0:T(8,128)(2,1)} %broadcast_in_dim.69), calls=%async_computation.4 | async-start | bytes 1048576 | tf_op jit(solution)/shard_map/all_to_all | solution.py:109
  110.0 0.8 copy-start.1
  141.3 8.5 %copy-start.4 = (bf16[8,2,24,2048]{3,2,1,0:T(8,128)(2,1)}, bf16[8,2,24,2048]{3,2,1,0:T(8,128)(2,1)S(1)}, u32[]{:S(2)}) copy-start(bf16[8,2,24,2048]{3,2,1,0:T(8,128)(2,1)S(1)} %all_to_all.40) | copy-start | bytes 4718596
  165.5 25.3 %all-to-all-start.6 = ((bf16[8,2,24,2048]{3,2,1,0:T(8,128)(2,1)}), bf16[8,2,24,2048]{3,2,1,0:T(8,128)(2,1)}, u32[]{:S(2)}, u32[]{:S(2)}) async-start(bf16[8,2,24,2048]{3,2,1,0:T(8,128)(2,1)} %copy.108), calls=%async_computation.6 | async-start | bytes 3145728 | tf_op jit(solution)/shard_map/all_to_all | solution.py:157
  190.8 2.0 copy-start.3
  202.7 15.2 %all-to-all-start.7 = ((bf16[4,128,512]{2,1,0:T(8,128)(2,1)}), bf16[4,128,512]{2,1,0:T(8,128)(2,1)S(1)}, u32[]{:S(2)}, u32[]{:S(2)}) async-start(bf16[4,128,512]{2,1,0:T(8,128)(2,1)} %bitcast.174), calls=%async_computation.7 | async-start | bytes 1048576 | tf_op jit(solution)/shard_map/all_to_all | solution.py:174

commit v3 on v2

--- a/solution.py
+++ b/solution.py
@@ -121,11 +121,24 @@
         * norm_gain
     ).astype(jnp.bfloat16)
     tokens = normed
+    shared_g = jnp.dot(tokens, shared_gate, preferred_element_type=jnp.float32)
+    shared_u = jnp.dot(tokens, shared_up, preferred_element_type=jnp.float32)
+    shared_act = (jax.nn.silu(shared_g) * shared_u).astype(jnp.bfloat16)
+    shared_part = jnp.dot(shared_act, shared_down, preferred_element_type=jnp.float32)
+    shared_chunks = (
+        shared_part.astype(jnp.bfloat16).reshape(token_count, col_count, col_width).transpose(1, 0, 2)
+    )
+    shared_here = jnp.sum(
+        lax.all_to_all(shared_chunks, "col", 0, 0, tiled=True).astype(jnp.float32), axis=0
+    )
     entries_here = w_gate.shape[0]
     experts_dev = max(1, entries_here // GROUPS)
     groups_dev = entries_here // experts_dev
+    devs_per_expert = max(1, GROUPS // entries_here)
     experts_per_row = col_count * entries_here // GROUPS
-    slots = row_count * experts_dev * CAP
+    device_count = row_count * col_count
+    send_slots = row_count * experts_dev * CAP
+    all_slots = device_count * experts_dev * CAP
     chosen = expert_ids.reshape(token_count * TOPK)
     onehot = (chosen[:, None] == jnp.arange(E, dtype=jnp.int32)[None, :]).astype(jnp.int32)
     slot_index = jnp.sum(jnp.cumsum(onehot, axis=0) * onehot, axis=1) - 1
@@ -134,11 +147,17 @@
     valid = (local_expert >= 0) & (local_expert < experts_dev)
     place = (dest_row * experts_dev + local_expert) * CAP + slot_index
     place = jnp.where(valid, place, -1).reshape(token_count, TOPK)
-    hit = place[:, :, None] == jnp.arange(slots, dtype=jnp.int32)[None, None, :]
+    hit = place[:, :, None] == jnp.arange(send_slots, dtype=jnp.int32)[None, None, :]
     dispatch = jnp.sum(hit.astype(jnp.float32), axis=1).astype(jnp.bfloat16)
-    combine = jnp.sum(
-        jnp.where(hit, gate_values.reshape(token_count, TOPK, 1), 0.0), axis=1
-    )
+    first_device = chosen * GROUPS // entries_here
+    combine = jnp.zeros((token_count, all_slots), jnp.float32)
+    slot_ids = jnp.arange(all_slots, dtype=jnp.int32)[None, None, :]
+    gates = gate_values.reshape(token_count, TOPK, 1)
+    for part in range(devs_per_expert):
+        device = first_device + part
+        owner_expert = chosen - device * entries_here // GROUPS
+        spot = ((device * experts_dev + owner_expert) * CAP + slot_index).reshape(token_count, TOPK)
+        combine = combine + jnp.sum(jnp.where(spot[:, :, None] == slot_ids, gates, 0.0), axis=1)
     outgoing = lax.dot_general(
         dispatch, tokens, (((0,), (0,)), ((), ())), preferred_element_type=jnp.float32
     ).astype(jnp.bfloat16)
@@ -147,33 +166,26 @@
     hidden = w_gate.shape[2]
     wg = w_gate.reshape(experts_dev, groups_dev, model_width, hidden)
     wu = w_up.reshape(experts_dev, groups_dev, model_width, hidden)
-    wd = w_down.reshape(experts_dev, groups_dev, hidden, model_width)
+    wd = w_down.reshape(experts_dev, groups_dev, hidden, col_count, col_width)
     gate_proj = jnp.einsum("nlsd,lgdf->lgnsf", arrived, wg, preferred_element_type=jnp.float32)
     up_proj = jnp.einsum("nlsd,lgdf->lgnsf", arrived, wu, preferred_element_type=jnp.float32)
     hidden_act = (jax.nn.silu(gate_proj) * up_proj).astype(jnp.bfloat16)
     expert_out = jnp.einsum(
-        "lgnsf,lgfd->nlsd", hidden_act, wd, preferred_element_type=jnp.float32
-    ).astype(jnp.bfloat16)
-    returned = lax.all_to_all(expert_out, "row", 0, 0, tiled=True).reshape(slots, model_width)
+        "lgnsf,lgfcw->nclsw", hidden_act, wd, preferred_element_type=jnp.float32
+    ).astype(jnp.bfloat16)
+    returned = lax.all_to_all(
+        expert_out.reshape(device_count, experts_dev, CAP, col_width),
+        ("row", "col"),
+        0,
+        0,
+        tiled=True,
+    ).reshape(all_slots, col_width)
     combine_hi = combine.astype(jnp.bfloat16)
     combine_lo = (combine - combine_hi.astype(jnp.float32)).astype(jnp.bfloat16)
     routed = jnp.dot(combine_hi, returned, preferred_element_type=jnp.float32) + jnp.dot(
         combine_lo, returned, preferred_element_type=jnp.float32
     )
-    shared_g = jnp.dot(tokens, shared_gate, preferred_element_type=jnp.float32)
-    shared_u = jnp.dot(tokens, shared_up, preferred_element_type=jnp.float32)
-    shared_act = (jax.nn.silu(shared_g) * shared_u).astype(jnp.bfloat16)
-    shared_part = jnp.dot(shared_act, shared_down, preferred_element_type=jnp.float32)
-    ffn_chunks = (
-        (routed + shared_part)
-        .astype(jnp.bfloat16)
-        .reshape(token_count, col_count, col_width)
-        .transpose(1, 0, 2)
-    )
-    ffn_total = jnp.sum(
-        lax.all_to_all(ffn_chunks, "col", 0, 0, tiled=True).astype(jnp.float32), axis=0
-    )
-    ffn_here = ffn_total.astype(jnp.bfloat16).reshape(rows_here, requests, col_width)
+    ffn_here = (routed + shared_here).astype(jnp.bfloat16).reshape(rows_here, requests, col_width)
     mixed_here = mixed_slice.reshape(rows_here, requests, col_width)
     return (mixed_here, ffn_here)
 

time: 221 us -> 234 us (1.059)
  blocking collectives: 27.6 us -> 0 us
  local copies, waits for them, and re-layouts: 39.4 us -> 55 us
  starting transfers between devices: 29.4 us -> 38.8 us
  waiting for transfers between devices: 58.4 us -> 66.3 us
  matrix products: 44.4 us -> 50 us
    all_to_all x1 -> x0, blocking collectives: 27.6 us -> none  [body(): arrived = lax.all_to_all(outgoing, 'row', 0, 0, tiled=True)]
    reshape x2 -> x4, local copies, waits for them, and re-layouts: 2.61 us -> 23.5 us  [the longest x1 19.5 us: body(): wd = w_down.reshape(experts_dev, groups_dev, hidden, col_count, col_width)]
    all_to_all x2 -> x3, starting transfers between devices: 7.76 us -> 17.2 us  [the longest x1 6.86 us: body(): lax.all_to_all(expert_out.reshape(device_count, experts_dev, CAP, col_wid...]
    all_to_all x2 -> x3, waiting for transfers between devices: 28.6 us -> 33.3 us  [the longest x1 33.3 us: body(): lax.all_to_all(expert_out.reshape(device_count, experts_dev, CAP, col_wid...]
    dot_general x1, matrix products: 12.9 us -> 16.9 us  [body(): jnp.einsum('lgnsf,lgfcw->nclsw', hidden_act, wd, preferred_element_type=j...]
    all_to_all x1, waiting for transfers between devices: 2.2 us -> 5.6 us  [body(): lax.all_to_all(jnp.broadcast_to(mixed_slice[None], (col_count, token_coun...]
    convert_element_type x1 -> x0, local copies, waits for them, and re-layouts: 2.74 us -> none  [body(): expert_out = jnp.einsum('lgnsf,lgfd->nlsd', hidden_act, wd, preferred_ele...]
    unnamed x31 -> x37, local copies, waits for them, and re-layouts: 6.47 us -> 5.49 us
  transfers between devices with their start and end apart: 7 -> 8, of which waited for: 6 -> 5; matrix products, arithmetic and copies ran while one was open for 17% -> 39% of each run, Pallas kernels for 0% -> 0%
where the time goes in v3:
time: 234 us; the launch traced here: 231 us
  waiting for transfers between devices  66.3 us (28%)
  local copies, waits for them, and re-layouts  55 us (24%)
  matrix products  50 us (21%)
  starting transfers between devices  38.8 us (17%)
  other arithmetic  19.7 us (8%)
    all_to_all x1, waiting for transfers between devices, body(): lax.all_to_all(expert_out.reshape(device_count, experts_dev, CAP, col_wid...  33.3 us
    reshape x1, local copies, waits for them, and re-layouts, body(): wd = w_down.reshape(experts_dev, groups_dev, hidden, col_count, col_width)  19.5 us
    dot_general x1, matrix products, body(): jnp.einsum('lgnsf,lgfcw->nclsw', hidden_act, wd, preferred_element_type=j...  16.9 us
    all_to_all x1, waiting for transfers between devices, body(): lax.all_to_all(product.reshape(row_count, rows_here, requests, heads_here...  14 us
    dot_general x1, matrix products, body(): jnp.einsum('nlsd,lgdf->lgnsf', arrived, wu, preferred_element_type=jnp.fl...  10 us
    all_to_all x1, waiting for transfers between devices, body(): lax.all_to_all(jnp.broadcast_to(queries[None], (row_count,) + queries.sha...  9.38 us
    all_to_all x1, starting transfers between devices, body(): lax.all_to_all(expert_out.reshape(device_count, experts_dev, CAP, col_wid...  6.86 us
    all_to_all x1, starting transfers between devices, body(): arrived = lax.all_to_all(outgoing, 'row', 0, 0, tiled=True)  6.83 us
  transfers between devices with their start and end apart: 8, of which 5 were waited for; matrix products, arithmetic and copies ran while one was open for 39% of the time, Pallas kernels for 0%

profile of v3, /device:TPU:0, one launch (start us, length us, event | category | flops | bytes accessed | tf_op | source)
XLA Modules:
  0.0 230.8 jit_solution(5120925768866996284)
XLA Ops:
  0.7 1.1 copy.89
  1.8 1.1 broadcast_in_dim.35
  2.9 5.3 %all-to-all-start = ((bf16[8,64,2,512]{3,1,2,0:T(8,128)(2,1)}), bf16[8,64,2,512]{3,1,2,0:T(8,128)(2,1)}, u32[]{:S(2)}, u32[]{:S(2)}) async-start(bf16[8,64,2,512]{3,1,2,0:T(8,128)(2,1)} %broadcast_in_dim.35), calls=%async_computation | async-start | bytes 2097152 | tf_op jit(solution)/shard_map/all_to_all | solution.py:49
  8.2 1.3 pad_maximum_fusion
  9.5 1.4 pad_maximum_fusion.1
  10.9 2.0 reshape.327
  12.9 1.0 reshape.328
  14.3 9.4 %all-to-all-done = bf16[8,64,2,512]{3,1,2,0:T(8,128)(2,1)} async-done(((bf16[8,64,2,512]{3,1,2,0:T(8,128)(2,1)}), bf16[8,64,2,512]{3,1,2,0:T(8,128)(2,1)}, u32[]{:S(2)}, u32[]{:S(2)}) %all-to-all-start) | async-done | bytes 1048608 | tf_op jit(solution)/shard_map/all_to_all | solution.py:49
  23.7 2.4 %copy.90 = bf16[8,64,2,512]{3,1,0,2:T(8,128)(2,1)} copy(bf16[8,64,2,512]{3,1,2,0:T(8,128)(2,1)} %all-to-all-done) | data formatting | bytes 2097152 | tf_op jit(solution)/shard_map/all_to_all | solution.py:49
  26.1 2.2 reshape.300
  28.2 2.0 fusion.2
  30.3 1.6 copy-done.5
  34.9 1.6 reshape.330
  36.5 3.3 %all-to-all-start.1 = ((f32[8,1,1024]{2,1,0:T(1,128)}), f32[8,1,1024]{2,1,0:T(1,128)S(1)}, u32[]{:S(2)}, u32[]{:S(2)}) async-start(f32[8,1,1024]{2,1,0:T(1,128)} %reshape.330), calls=%async_computation.1 | async-start | bytes 65536 | tf_op jit(solution)/shard_map/all_to_all | solution.py:80
  39.9 3.9 %fusion.26 = bf16[512,2,4,128]{0,3,2,1:T(8,128)(2,1)} fusion(f32[2,4,192,512]{3,2,1,0:T(8,128)} %copy-done.5, f32[2,4,512]{2,1,0:T(4,128)S(1)} %get-tuple-element.4, pred[2,512,192]{1,2,0:T(8,128)(4,1)S(1)} %broadcast_or_fusion, bf16[192,2,4,128]{3,2,1,0:T(4,128)(2,1)S(1)} %copy-done.7), kind=kOutput, calls=%fused_computation.33 | convolution fusion | flops 205783040 | bytes 4800512 | tf_op jit(solution)/shard_map/rhij,jrhd->irhd/dot_general | solution.py:70
  43.8 2.3 copy.97
  46.1 2.4 %copy.98 = bf16[8,64,2,4,128]{4,1,3,2,0:T(8,128)(2,1)} copy(bf16[8,64,2,4,128]{4,1,0,3,2:T(8,128)(2,1)} %bitcast.178) | data formatting | bytes 2097152 | tf_op jit(solution)/shard_map/reshape | solution.py:78
  48.4 4.2 %all-to-all-start.2 = ((bf16[8,64,2,4,128]{4,1,3,2,0:T(8,128)(2,1)}), bf16[8,64,2,4,128]{4,1,3,2,0:T(8,128)(2,1)}, u32[]{:S(2)}, u32[]{:S(2)}) async-start(bf16[8,64,2,4,128]{4,1,3,2,0:T(8,128)(2,1)} %copy.98), calls=%async_computation.2 | async-start | bytes 2097152 | tf_op jit(solution)/shard_map/all_to_all | solution.py:77
  54.1 14.0 %all-to-all-done.2 = bf16[8,64,2,4,128]{4,1,3,2,0:T(8,128)(2,1)} async-done(((bf16[8,64,2,4,128]{4,1,3,2,0:T(8,128)(2,1)}), bf16[8,64,2,4,128]{4,1,3,2,0:T(8,128)(2,1)}, u32[]{:S(2)}, u32[]{:S(2)}) %all-to-all-start.2) | async-done | bytes 1048608 | tf_op jit(solution)/shard_map/all_to_all | solution.py:77
  68.1 1.8 multiply_reduce_fusion
  69.9 2.1 fusion.3
  72.5 1.1 reshape.305
  73.7 1.9 copy.100
  75.6 5.3 %all-to-all-start.3 = ((bf16[4,128,512]{2,1,0:T(8,128)(2,1)}), bf16[4,128,512]{2,1,0:T(8,128)(2,1)S(1)}, u32[]{:S(2)}, u32[]{:S(2)}) async-start(bf16[4,128,512]{2,1,0:T(8,128)(2,1)} %copy.100), calls=%async_computation.3 | async-start | bytes 1048576 | tf_op jit(solution)/shard_map/all_to_all | solution.py:103
  81.3 2.0 reshape.298
  84.0 4.4 %reduce-window.6 = s32[64,6,128]{2,0,1:T(8,128)} reduce-window(s32[64,6,128]{2,0,1:T(8,128)} %fusion.49, s32[]{:T(128)} %constant.70.clone.1), window={size=1x1x128 pad=0_0x0_0x127_0}, to_apply=%region_6.7 | reduce-window | flops 6242304 | bytes 393220 | tf_op jit(solution)/shard_map/reduce-window
  88.4 4.0 %all-to-all-done.3 = bf16[4,128,512]{2,1,0:T(8,128)(2,1)S(1)} async-done(((bf16[4,128,512]{2,1,0:T(8,128)(2,1)}), bf16[4,128,512]{2,1,0:T(8,128)(2,1)S(1)}, u32[]{:S(2)}, u32[]{:S(2)}) %all-to-all-start.3) | async-done | bytes 524320 | tf_op jit(solution)/shard_map/all_to_all | solution.py:103
  94.4 3.5 %all-to-all-start.4 = ((bf16[4,128,512]{1,2,0:T(8,128)(2,1)}), bf16[4,128,512]{1,2,0:T(8,128)(2,1)S(1)}, u32[]{:S(2)}, u32[]{:S(2)}) async-start(bf16[4,128,512]{1,2,0:T(8,128)(2,1)} %broadcast_in_dim.70), calls=%async_computation.4 | async-start | bytes 1048576 | tf_op jit(solution)/shard_map/all_to_all | solution.py:109
  97.9 1.2 slice_reduce_fusion
  99.1 1.1 fusion.45
  101.0 1.7 fusion.58
  104.4 5.6 %all-to-all-done.4 = bf16[4,128,512]{1,2,0:T(8,128)(2,1)S(1)} async-done(((bf16[4,128,512]{1,2,0:T(8,128)(2,1)}), bf16[4,128,512]{1,2,0:T(8,128)(2,1)S(1)}, u32[]{:S(2)}, u32[]{:S(2)}) %all-to-all-start.4) | async-done | bytes 524320 | tf_op jit(solution)/shard_map/all_to_all | solution.py:109
  110.3 1.0 fusion.33
  112.2 2.7 %convolution_convert_fusion = bf16[384,2048]{1,0:T(8,128)(2,1)} fusion(bf16[128,2048]{0,1:T(8,128)(2,1)S(1)} %fusion.33, bf16[128,384]{1,0:T(8,128)(2,1)} %convert_reduce_fusion), kind=kOutput, calls=%fused_computation.7 | convolution fusion | flops 202113024 | bytes 2195456 | tf_op jit(solution)/shard_map/dot_general | solution.py:161
  114.9 6.8 %all-to-all-start.5 = ((bf16[8,2,24,2048]{3,2,1,0:T(8,128)(2,1)}), bf16[8,2,24,2048]{3,2,1,0:T(8,128)(2,1)}, u32[]{:S(2)}, u32[]{:S(2)}) async-start(bf16[8,2,24,2048]{3,2,1,0:T(8,128)(2,1)} %bitcast.177), calls=%async_computation.5 | async-start | bytes 3145728 | tf_op jit(solution)/shard_map/all_to_all | solution.py:165
  121.7 19.5 %reshape.312 = bf16[2,4,352,4,512]{4,3,2,1,0:T(4,128)(2,1)} reshape(bf16[8,352,2048]{2,1,0:T(8,128)(2,1)} %param.30) | data formatting | bytes 23068672 | tf_op jit(solution)/shard_map/reshape | solution.py:169
  141.2 3.5 %fusion.76 = f32[128,704]{0,1:T(8,128)} fusion(bf16[2048,704]{0,1:T(8,128)(2,1)} %param.31, bf16[128,2048]{0,1:T(8,128)(2,1)S(1)} %copy-done.4), kind=kOutput, calls=%fused_computation.136 | convolution fusion | flops 369098752 | bytes 3768320 | tf_op jit(solution)/shard_map/dot_general | solution.py:124
  144.7 4.8 %convolution_convert_fusion.1 = bf16[128,2048]{1,0:T(8,128)(2,1)} fusion(bf16[704,2048]{1,0:T(8,128)(2,1)S(1)} %copy-done, bf16[2048,704]{0,1:T(8,128)(2,1)} %param.32, bf16[128,2048]{0,1:T(8,128)(2,1)S(1)} %copy-done.4, f32[128,704]{0,1:T(8,128)} %fusion.76), kind=kOutput, calls=%fused_computation.11 | convolution fusion | flops 739000320 | bytes 7176192 | tf_op jit(solution)/shard_map/dot_general | solution.py:127
  149.6 1.9 copy.163
  151.5 3.5 %all-to-all-start.7 = ((bf16[4,128,512]{2,1,0:T(8,128)(2,1)}), bf16[4,128,512]{2,1,0:T(8,128)(2,1)S(1)}, u32[]{:S(2)}, u32[]{:S(2)}) async-start(bf16[4,128,512]{2,1,0:T(8,128)(2,1)} %bitcast.173), calls=%async_computation.7 | async-start | bytes 1048576 | tf_op jit(solution)/shard_map/all_to_all | solution.py:132
  155.0 10.0 %fusion.23 = f32[2,8,24,4,352]{4,2,3,1,0:T(8,128)} fusion(bf16[2,4,2048,352,1]{2,3,1,4,0:T(8,128)(2,1)} %bitcast.190, bf16[8,2,24,2048]{3,2,1,0:T(8,128)(2,1)} %all-to-all-done.5), kind=kOutput, calls=%fused_computation.30 | convolution fusion | flops 2214592512 | bytes 15269888 | tf_op jit(solution)/shard_map/nlsd,lgdf->lgnsf/dot_general | solution.py:171
  165.0 16.9 %bitcast_convert_fusion = bf16[2,8,24,4,512]{4,2,3,1,0:T(8,128)(2,1)S(1)} fusion(bf16[2,4,352,4,512,1]{4,3,2,1,0,5:T(4,128)(2,1)} %bitcast.176, f32[2,8,24,4,352]{4,2,3,1,0:T(8,128)} %fusion.23, bf16[2,4,2048,352,1]{2,3,1,4,0:T(8,128)(2,1)} %bitcast.191, bf16[8,2,24,2048]{3,2,1,0:T(8,128)(2,1)} %all-to-all-done.5), kind=kOutput, calls=%fused_computation.4 | convolution fusion | flops 4433215488 | bytes 28377088 | tf_op jit(solution)/shard_map/lgnsf,lgfcw->nclsw/dot_general | solution.py:173
  181.9 1.4 copy.114
  183.3 6.9 %all-to-all-start.6 = ((bf16[32,2,24,512]{3,2,1,0:T(8,128)(2,1)}), bf16[32,2,24,512]{3,2,1,0:T(8,128)(2,1)}, u32[]{:S(2)}, u32[]{:S(2)}) async-start(bf16[32,2,24,512]{3,2,1,0:T(8,128)(2,1)} %copy.114), calls=%async_computation.6 | async-start | bytes 3145728 | tf_op jit(solution)/shard_map/all_to_all | solution.py:176
  190.5 1.6 select_reduce_fusion
  192.8 33.3 %all-to-all-done.6 = bf16[32,2,24,512]{3,2,1,0:T(8,128)(2,1)} async-done(((bf16[32,2,24,512]{3,2,1,0:T(8,128)(2,1)}), bf16[32,2,24,512]{3,2,1,0:T(8,128)(2,1)}, u32[]{:S(2)}, u32[]{:S(2)}) %all-to-all-start.6) | async-done | bytes 1572896 | tf_op jit(solution)/shard_map/all_to_all | solution.py:176
  226.1 2.2 fusion.47
  228.3 1.8 fusion.31
  (75 shorter events, 13.9 us)
Async XLA Ops:
  0.6 144.1 %copy-start = (bf16[704,2048]{1,0:T(8,128)(2,1)S(1)}, bf16[704,2048]{1,0:T(8,128)(2,1)}, u32[]{:S(2)}) copy-start(bf16[704,2048]{1,0:T(8,128)(2,1)} %param.33) | copy-start | bytes 8650756
  0.6 7.6 %copy-start.12 = (bf16[64,2,512]{2,1,0:T(2,128)(2,1)S(1)}, bf16[64,2,512]{2,1,0:T(2,128)(2,1)}, u32[]{:S(2)}) copy-start(bf16[64,2,512]{2,1,0:T(2,128)(2,1)} %param.18) | copy-start | bytes 393220
  0.7 7.6 %copy-start.9 = (bf16[128,2,512]{2,1,0:T(2,128)(2,1)S(1)}, bf16[128,2,512]{2,1,0:T(2,128)(2,1)}, u32[]{:S(2)}) copy-start(bf16[128,2,512]{2,1,0:T(2,128)(2,1)} %param.20) | copy-start | bytes 786436
  0.7 8.8 %copy-start.10 = (bf16[128,2,512]{2,1,0:T(2,128)(2,1)S(1)}, bf16[128,2,512]{2,1,0:T(2,128)(2,1)}, u32[]{:S(2)}) copy-start(bf16[128,2,512]{2,1,0:T(2,128)(2,1)} %param.21) | copy-start | bytes 786436
  2.9 11.0 %copy-start.15 = (s32[2]{0:T(128)S(1)}, s32[2]{0:T(128)}, u32[]{:S(2)}) copy-start(s32[2]{0:T(128)} %param.22) | copy-start | bytes 28
  2.9 20.8 %all-to-all-start = ((bf16[8,64,2,512]{3,1,2,0:T(8,128)(2,1)}), bf16[8,64,2,512]{3,1,2,0:T(8,128)(2,1)}, u32[]{:S(2)}, u32[]{:S(2)}) async-start(bf16[8,64,2,512]{3,1,2,0:T(8,128)(2,1)} %broadcast_in_dim.35), calls=%async_computation | async-start | bytes 2097152 | tf_op jit(solution)/shard_map/all_to_all | solution.py:49
  13.9 14.3 %copy-start.8 = (bf16[192,2,4,128]{3,2,1,0:T(4,128)(2,1)S(1)}, bf16[192,2,4,128]{3,2,1,0:T(4,128)(2,1)}, u32[]{:S(2)}) copy-start(bf16[192,2,4,128]{3,2,1,0:T(4,128)(2,1)} %reshape.327) | copy-start | bytes 1179652
  30.3 1.7 copy-start.5
  30.3 9.6 %copy-start.7 = (bf16[192,2,4,128]{3,2,1,0:T(4,128)(2,1)S(1)}, bf16[192,2,4,128]{3,2,1,0:T(4,128)(2,1)}, u32[]{:S(2)}) copy-start(bf16[192,2,4,128]{3,2,1,0:T(4,128)(2,1)} %reshape.328) | copy-start | bytes 1179652
  36.5 11.9 %all-to-all-start.1 = ((f32[8,1,1024]{2,1,0:T(1,128)}), f32[8,1,1024]{2,1,0:T(1,128)S(1)}, u32[]{:S(2)}, u32[]{:S(2)}) async-start(f32[8,1,1024]{2,1,0:T(1,128)} %reshape.330), calls=%async_computation.1 | async-start | bytes 65536 | tf_op jit(solution)/shard_map/all_to_all | solution.py:80
  48.4 19.7 %all-to-all-start.2 = ((bf16[8,64,2,4,128]{4,1,3,2,0:T(8,128)(2,1)}), bf16[8,64,2,4,128]{4,1,3,2,0:T(8,128)(2,1)}, u32[]{:S(2)}, u32[]{:S(2)}) async-start(bf16[8,64,2,4,128]{4,1,3,2,0:T(8,128)(2,1)} %copy.98), calls=%async_computation.2 | async-start | bytes 2097152 | tf_op jit(solution)/shard_map/all_to_all | solution.py:77
  69.9 11.0 %copy-start.13 = (s32[64,2,6]{0,1,2:T(2,128)S(1)}, s32[64,2,6]{0,1,2:T(2,128)}, u32[]{:S(2)}) copy-start(s32[64,2,6]{0,1,2:T(2,128)} %param.26) | copy-start | bytes 9220
  75.6 16.8 %all-to-all-start.3 = ((bf16[4,128,512]{2,1,0:T(8,128)(2,1)}), bf16[4,128,512]{2,1,0:T(8,128)(2,1)S(1)}, u32[]{:S(2)}, u32[]{:S(2)}) async-start(bf16[4,128,512]{2,1,0:T(8,128)(2,1)} %copy.100), calls=%async_computation.3 | async-start | bytes 1048576 | tf_op jit(solution)/shard_map/all_to_all | solution.py:103
  81.0 11.4 %copy-start.6 = (s32[64,2,6]{2,1,0:T(2,128)}, s32[64,2,6]{2,1,0:T(2,128)S(1)}, u32[]{:S(2)}) copy-start(s32[64,2,6]{2,1,0:T(2,128)S(1)} %copy.102) | copy-start | bytes 9220
  94.4 15.6 %all-to-all-start.4 = ((bf16[4,128,512]{1,2,0:T(8,128)(2,1)}), bf16[4,128,512]{1,2,0:T(8,128)(2,1)S(1)}, u32[]{:S(2)}, u32[]{:S(2)}) async-start(bf16[4,128,512]{1,2,0:T(8,128)(2,1)} %broadcast_in_dim.70), calls=%async_computation.4 | async-start | bytes 1048576 | tf_op jit(solution)/shard_map/all_to_all | solution.py:109
  111.3 0.8 copy-start.3
  114.9 36.6 %all-to-all-start.5 = ((bf16[8,2,24,2048]{3,2,1,0:T(8,128)(2,1)}), bf16[8,2,24,2048]{3,2,1,0:T(8,128)(2,1)}, u32[]{:S(2)}, u32[]{:S(2)}) async-start(bf16[8,2,24,2048]{3,2,1,0:T(8,128)(2,1)} %bitcast.177), calls=%async_computation.5 | async-start | bytes 3145728 | tf_op jit(solution)/shard_map/all_to_all | solution.py:165
  121.7 19.5 %copy-start.4 = (bf16[128,2048]{0,1:T(8,128)(2,1)S(1)}, bf16[128,2048]{0,1:T(8,128)(2,1)}, u32[]{:S(2)}) copy-start(bf16[128,2048]{0,1:T(8,128)(2,1)} %copy-done.3) | copy-start | bytes 1572868
  151.5 31.8 %all-to-all-start.7 = ((bf16[4,128,512]{2,1,0:T(8,128)(2,1)}), bf16[4,128,512]{2,1,0:T(8,128)(2,1)S(1)}, u32[]{:S(2)}, u32[]{:S(2)}) async-start(bf16[4,128,512]{2,1,0:T(8,128)(2,1)} %bitcast.173), calls=%async_computation.7 | async-start | bytes 1048576 | tf_op jit(solution)/shard_map/all_to_all | solution.py:132
  181.9 8.3 %copy-start.14 = (f32[64,2,6]{0,1,2:T(2,128)S(1)}, f32[64,2,6]{0,1,2:T(2,128)}, u32[]{:S(2)}) copy-start(f32[64,2,6]{0,1,2:T(2,128)} %param.27) | copy-start | bytes 9220
  181.9 8.4 %copy-start.11 = (s32[128,6]{1,0:T(8,128)S(1)}, s32[128,6]{1,0:T(8,128)}, u32[]{:S(2)}) copy-start(s32[128,6]{1,0:T(8,128)} %get-tuple-element.2) | copy-start | bytes 9220
  183.3 42.8 %all-to-all-start.6 = ((bf16[32,2,24,512]{3,2,1,0:T(8,128)(2,1)}), bf16[32,2,24,512]{3,2,1,0:T(8,128)(2,1)}, u32[]{:S(2)}, u32[]{:S(2)}) async-start(bf16[32,2,24,512]{3,2,1,0:T(8,128)(2,1)} %copy.114), calls=%async_computation.6 | async-start | bytes 3145728 | tf_op jit(solution)/shard_map/all_to_all | solution.py:176
  226.1 2.2 copy-start.2
  226.1 4.7 %copy-start.1 = (bf16[704,2048]{1,0:T(8,128)(2,1)S(1)}, bf16[704,2048]{1,0:T(8,128)(2,1)}, u32[]{:S(2)}) copy-start(bf16[704,2048]{1,0:T(8,128)(2,1)} %param.33) | copy-start | bytes 8650756

commit v4 on v2

--- a/solution.py
+++ b/solution.py
@@ -132,34 +132,45 @@
     dest_row = chosen // experts_per_row
     local_expert = chosen - (dest_row * col_count + col_index) * entries_here // GROUPS
     valid = (local_expert >= 0) & (local_expert < experts_dev)
-    place = (dest_row * experts_dev + local_expert) * CAP + slot_index
+    place = (local_expert * row_count + dest_row) * CAP + slot_index
     place = jnp.where(valid, place, -1).reshape(token_count, TOPK)
     hit = place[:, :, None] == jnp.arange(slots, dtype=jnp.int32)[None, None, :]
     dispatch = jnp.sum(hit.astype(jnp.float32), axis=1).astype(jnp.bfloat16)
     combine = jnp.sum(
         jnp.where(hit, gate_values.reshape(token_count, TOPK, 1), 0.0), axis=1
     )
+    combine_hi = combine.astype(jnp.bfloat16)
+    combine_lo = (combine - combine_hi.astype(jnp.float32)).astype(jnp.bfloat16)
     outgoing = lax.dot_general(
         dispatch, tokens, (((0,), (0,)), ((), ())), preferred_element_type=jnp.float32
     ).astype(jnp.bfloat16)
-    outgoing = outgoing.reshape(row_count, experts_dev, CAP, model_width)
-    arrived = lax.all_to_all(outgoing, "row", 0, 0, tiled=True)
+    outgoing = outgoing.reshape(experts_dev, row_count, CAP, model_width)
     hidden = w_gate.shape[2]
     wg = w_gate.reshape(experts_dev, groups_dev, model_width, hidden)
     wu = w_up.reshape(experts_dev, groups_dev, model_width, hidden)
     wd = w_down.reshape(experts_dev, groups_dev, hidden, model_width)
-    gate_proj = jnp.einsum("nlsd,lgdf->lgnsf", arrived, wg, preferred_element_type=jnp.float32)
-    up_proj = jnp.einsum("nlsd,lgdf->lgnsf", arrived, wu, preferred_element_type=jnp.float32)
-    hidden_act = (jax.nn.silu(gate_proj) * up_proj).astype(jnp.bfloat16)
-    expert_out = jnp.einsum(
-        "lgnsf,lgfd->nlsd", hidden_act, wd, preferred_element_type=jnp.float32
-    ).astype(jnp.bfloat16)
-    returned = lax.all_to_all(expert_out, "row", 0, 0, tiled=True).reshape(slots, model_width)
-    combine_hi = combine.astype(jnp.bfloat16)
-    combine_lo = (combine - combine_hi.astype(jnp.float32)).astype(jnp.bfloat16)
-    routed = jnp.dot(combine_hi, returned, preferred_element_type=jnp.float32) + jnp.dot(
-        combine_lo, returned, preferred_element_type=jnp.float32
-    )
+    chunk_slots = row_count * CAP
+    routed = jnp.zeros((token_count, model_width), jnp.float32)
+    for chunk in range(experts_dev):
+        arrived = lax.all_to_all(outgoing[chunk], "row", 0, 0, tiled=True).reshape(
+            chunk_slots, model_width
+        )
+        gate_proj = jnp.einsum(
+            "td,gdf->gtf", arrived, wg[chunk], preferred_element_type=jnp.float32
+        )
+        up_proj = jnp.einsum("td,gdf->gtf", arrived, wu[chunk], preferred_element_type=jnp.float32)
+        hidden_act = (jax.nn.silu(gate_proj) * up_proj).astype(jnp.bfloat16)
+        expert_out = jnp.einsum(
+            "gtf,gfd->td", hidden_act, wd[chunk], preferred_element_type=jnp.float32
+        ).astype(jnp.bfloat16)
+        returned = lax.all_to_all(
+            expert_out.reshape(row_count, CAP, model_width), "row", 0, 0, tiled=True
+        ).reshape(chunk_slots, model_width)
+        picks = slice(chunk * chunk_slots, (chunk + 1) * chunk_slots)
+        routed = routed + (
+            jnp.dot(combine_hi[:, picks], returned, preferred_element_type=jnp.float32)
+            + jnp.dot(combine_lo[:, picks], returned, preferred_element_type=jnp.float32)
+        )
     shared_g = jnp.dot(tokens, shared_gate, preferred_element_type=jnp.float32)
     shared_u = jnp.dot(tokens, shared_up, preferred_element_type=jnp.float32)
     shared_act = (jax.nn.silu(shared_g) * shared_u).astype(jnp.bfloat16)

time: 221 us -> 221 us (level)
  waiting for transfers between devices: 58.4 us -> 45.5 us
  matrix products: 44.4 us -> 56 us
  starting transfers between devices: 29.4 us -> 38.1 us
  blocking collectives: 27.6 us -> 19.3 us
    all_to_all x1 -> x3, waiting for transfers between devices: 17.6 us -> 4.84 us  [the longest x2 4.83 us: body(): lax.all_to_all(expert_out.reshape(row_count, CAP, model_width), 'row', 0,...]
    dot_general x4 -> x8, matrix products: 26.2 us -> 37.8 us  [the longest x2 18.1 us: body(): jnp.einsum('gtf,gfd->td', hidden_act, wd[chunk], preferred_element_type=j...]
    all_to_all x1 -> x3, starting transfers between devices: 4.29 us -> 13 us  [the longest x2 8.65 us: body(): lax.all_to_all(expert_out.reshape(row_count, CAP, model_width), 'row', 0,...]
    all_to_all x1, blocking collectives: 27.6 us -> 19.3 us  [body(): lax.all_to_all(outgoing[chunk], 'row', 0, 0, tiled=True)]
    convert_element_type x1 -> x0, local copies, waits for them, and re-layouts: 2.74 us -> none  [body(): expert_out = jnp.einsum('lgnsf,lgfd->nlsd', hidden_act, wd, preferred_ele...]
    unnamed x31 -> x33, local copies, waits for them, and re-layouts: 6.47 us -> 6.47 us
  transfers between devices with their start and end apart: 7 -> 9, of which waited for: 6 -> 6; matrix products, arithmetic and copies ran while one was open for 17% -> 33% of each run, Pallas kernels for 0% -> 0%
where the time goes in v4:
time: 221 us; the launch traced here: 218 us
  matrix products  56 us (25%)
  waiting for transfers between devices  45.5 us (21%)
  starting transfers between devices  38.1 us (17%)
  local copies, waits for them, and re-layouts  37.7 us (17%)
  other arithmetic  20.3 us (9%)
  blocking collectives  19.3 us (9%)
    all_to_all x1, blocking collectives, body(): lax.all_to_all(outgoing[chunk], 'row', 0, 0, tiled=True)  19.3 us
    dot_general x2, matrix products, body(): jnp.einsum('gtf,gfd->td', hidden_act, wd[chunk], preferred_element_type=j...  18.1 us
    all_to_all x1, waiting for transfers between devices, body(): lax.all_to_all(product.reshape(row_count, rows_here, requests, heads_here...  14 us
    dot_general x2, matrix products, body(): jnp.einsum('td,gdf->gtf', arrived, wg[chunk], preferred_element_type=jnp....  11.7 us
    all_to_all x1, waiting for transfers between devices, body(): lax.all_to_all(ffn_chunks, 'col', 0, 0, tiled=True).astype(jnp.float32)  10.9 us
    all_to_all x1, waiting for transfers between devices, body(): lax.all_to_all(jnp.broadcast_to(queries[None], (row_count,) + queries.sha...  9.38 us
    all_to_all x2, starting transfers between devices, body(): lax.all_to_all(expert_out.reshape(row_count, CAP, model_width), 'row', 0,...  8.65 us
    unnamed x33, local copies, waits for them, and re-layouts  6.47 us
  transfers between devices with their start and end apart: 9, of which 6 were waited for; matrix products, arithmetic and copies ran while one was open for 33% of the time, Pallas kernels for 0%

profile of v4, /device:TPU:0, one launch (start us, length us, event | category | flops | bytes accessed | tf_op | source)
XLA Modules:
  0.0 218.0 jit_solution(13995338077197089436)
XLA Ops:
  2.9 5.3 %all-to-all-start = ((bf16[8,64,2,512]{3,1,2,0:T(8,128)(2,1)}), bf16[8,64,2,512]{3,1,2,0:T(8,128)(2,1)}, u32[]{:S(2)}, u32[]{:S(2)}) async-start(bf16[8,64,2,512]{3,1,2,0:T(8,128)(2,1)} %broadcast_in_dim.35), calls=%async_computation | async-start | bytes 2097152 | tf_op jit(solution)/shard_map/all_to_all | solution.py:49
  8.2 1.3 pad_maximum_fusion
  9.5 1.4 pad_maximum_fusion.1
  10.9 2.0 reshape.297
  14.3 9.4 %all-to-all-done = bf16[8,64,2,512]{3,1,2,0:T(8,128)(2,1)} async-done(((bf16[8,64,2,512]{3,1,2,0:T(8,128)(2,1)}), bf16[8,64,2,512]{3,1,2,0:T(8,128)(2,1)}, u32[]{:S(2)}, u32[]{:S(2)}) %all-to-all-start) | async-done | bytes 1048608 | tf_op jit(solution)/shard_map/all_to_all | solution.py:49
  23.7 2.4 %copy.77 = bf16[8,64,2,512]{3,1,0,2:T(8,128)(2,1)} copy(bf16[8,64,2,512]{3,1,2,0:T(8,128)(2,1)} %all-to-all-done) | data formatting | bytes 2097152 | tf_op jit(solution)/shard_map/all_to_all | solution.py:49
  26.1 2.2 reshape.273
  28.2 2.0 fusion.12
  30.3 1.6 copy-done.3
  34.9 1.6 reshape.300
  36.5 3.3 %all-to-all-start.1 = ((f32[8,1,1024]{2,1,0:T(1,128)}), f32[8,1,1024]{2,1,0:T(1,128)S(1)}, u32[]{:S(2)}, u32[]{:S(2)}) async-start(f32[8,1,1024]{2,1,0:T(1,128)} %reshape.300), calls=%async_computation.1 | async-start | bytes 65536 | tf_op jit(solution)/shard_map/all_to_all | solution.py:80
  39.9 3.9 %fusion.52 = bf16[512,2,4,128]{0,3,2,1:T(8,128)(2,1)} fusion(f32[2,4,192,512]{3,2,1,0:T(8,128)} %copy-done.3, f32[2,4,512]{2,1,0:T(4,128)S(1)} %get-tuple-element.8, pred[2,512,192]{1,2,0:T(8,128)(4,1)S(1)} %broadcast_or_fusion, bf16[192,2,4,128]{3,2,1,0:T(4,128)(2,1)S(1)} %copy-done.7), kind=kOutput, calls=%fused_computation.41 | convolution fusion | flops 205783040 | bytes 4800512 | tf_op jit(solution)/shard_map/rhij,jrhd->irhd/dot_general | solution.py:70
  43.8 2.3 %copy.84 = bf16[512,2,4,128]{3,0,2,1:T(8,128)(2,1)} copy(bf16[512,2,4,128]{0,3,2,1:T(8,128)(2,1)} %fusion.52) | data formatting | bytes 2097152 | tf_op jit(solution)/shard_map/convert_element_type | solution.py:75
  46.1 2.4 %copy.85 = bf16[8,64,2,4,128]{4,1,3,2,0:T(8,128)(2,1)} copy(bf16[8,64,2,4,128]{4,1,0,3,2:T(8,128)(2,1)} %bitcast.150) | data formatting | bytes 2097152 | tf_op jit(solution)/shard_map/reshape | solution.py:78
  48.4 4.2 %all-to-all-start.2 = ((bf16[8,64,2,4,128]{4,1,3,2,0:T(8,128)(2,1)}), bf16[8,64,2,4,128]{4,1,3,2,0:T(8,128)(2,1)}, u32[]{:S(2)}, u32[]{:S(2)}) async-start(bf16[8,64,2,4,128]{4,1,3,2,0:T(8,128)(2,1)} %copy.85), calls=%async_computation.2 | async-start | bytes 2097152 | tf_op jit(solution)/shard_map/all_to_all | solution.py:77
  54.1 14.0 %all-to-all-done.2 = bf16[8,64,2,4,128]{4,1,3,2,0:T(8,128)(2,1)} async-done(((bf16[8,64,2,4,128]{4,1,3,2,0:T(8,128)(2,1)}), bf16[8,64,2,4,128]{4,1,3,2,0:T(8,128)(2,1)}, u32[]{:S(2)}, u32[]{:S(2)}) %all-to-all-start.2) | async-done | bytes 1048608 | tf_op jit(solution)/shard_map/all_to_all | solution.py:77
  68.1 1.8 multiply_reduce_fusion
  69.9 2.1 fusion.27
  73.7 1.9 copy.87
  75.6 5.3 %all-to-all-start.3 = ((bf16[4,128,512]{2,1,0:T(8,128)(2,1)}), bf16[4,128,512]{2,1,0:T(8,128)(2,1)S(1)}, u32[]{:S(2)}, u32[]{:S(2)}) async-start(bf16[4,128,512]{2,1,0:T(8,128)(2,1)} %copy.87), calls=%async_computation.3 | async-start | bytes 1048576 | tf_op jit(solution)/shard_map/all_to_all | solution.py:103
  80.9 2.0 reshape.271
  83.9 4.4 %reduce-window.6 = s32[64,6,128]{2,0,1:T(8,128)} reduce-window(s32[64,6,128]{2,0,1:T(8,128)} %fusion.88, s32[]{:T(128)} %constant.58.clone.1), window={size=1x1x128 pad=0_0x0_0x127_0}, to_apply=%region_6.7 | reduce-window | flops 6242304 | bytes 393220 | tf_op jit(solution)/shard_map/reduce-window
  88.3 4.2 %all-to-all-done.3 = bf16[4,128,512]{2,1,0:T(8,128)(2,1)S(1)} async-done(((bf16[4,128,512]{2,1,0:T(8,128)(2,1)}), bf16[4,128,512]{2,1,0:T(8,128)(2,1)S(1)}, u32[]{:S(2)}, u32[]{:S(2)}) %all-to-all-start.3) | async-done | bytes 524320 | tf_op jit(solution)/shard_map/all_to_all | solution.py:103
  94.4 3.5 %all-to-all-start.4 = ((bf16[4,128,512]{1,2,0:T(8,128)(2,1)}), bf16[4,128,512]{1,2,0:T(8,128)(2,1)S(1)}, u32[]{:S(2)}, u32[]{:S(2)}) async-start(bf16[4,128,512]{1,2,0:T(8,128)(2,1)} %broadcast_in_dim.69), calls=%async_computation.4 | async-start | bytes 1048576 | tf_op jit(solution)/shard_map/all_to_all | solution.py:109
  101.9 1.6 add_select_fusion.2
  104.4 1.4 copy.94
  107.8 2.2 %all-to-all-done.4 = bf16[4,128,512]{1,2,0:T(8,128)(2,1)S(1)} async-done(((bf16[4,128,512]{1,2,0:T(8,128)(2,1)}), bf16[4,128,512]{1,2,0:T(8,128)(2,1)S(1)}, u32[]{:S(2)}, u32[]{:S(2)}) %all-to-all-start.4) | async-done | bytes 524320 | tf_op jit(solution)/shard_map/all_to_all | solution.py:109
  110.8 1.4 fusion.69
  112.2 1.5 convolution_convert_fusion
  114.8 19.3 %all_to_all.50 = bf16[8,24,2048]{2,1,0:T(8,128)(2,1)} all-to-all(bf16[8,24,2048]{2,1,0:T(8,128)(2,1)S(1)} %bitcast.152), channel_id=1, replica_groups=mesh['row'=8,'col'=4] {'row'}, dimensions={0} | all-to-all | bytes 1572864 | tf_op jit(solution)/shard_map/all_to_all | solution.py:155
  134.1 4.4 %all-to-all-start.5 = ((bf16[8,24,2048]{2,1,0:T(8,128)(2,1)}), bf16[8,24,2048]{2,1,0:T(8,128)(2,1)}, u32[]{:S(2)}, u32[]{:S(2)}) async-start(bf16[8,24,2048]{2,1,0:T(8,128)(2,1)} %bitcast.151), calls=%async_computation.5 | async-start | bytes 1572864 | tf_op jit(solution)/shard_map/all_to_all | solution.py:155
  138.5 5.9 %fusion.46 = f32[4,192,352]{2,1,0:T(8,128)} fusion(bf16[192,2048,1]{1,0,2:T(8,128)(2,1)} %bitcast.160, bf16[8,2048,352]{1,2,0:T(8,128)(2,1)} %param.28), kind=kOutput, calls=%fused_computation.39 | convolution fusion | flops 1107296256 | bytes 7634944 | tf_op jit(solution)/shard_map/td,gdf->gtf/dot_general | solution.py:158
  144.3 9.1 %fusion.19 = bf16[192,2048]{1,0:T(8,128)(2,1)} fusion(bf16[8,352,2048]{2,1,0:T(8,128)(2,1)} %param.30, bf16[192,2048,1]{1,0,2:T(8,128)(2,1)} %bitcast.161, bf16[8,2048,352]{1,2,0:T(8,128)(2,1)} %param.29, f32[4,192,352]{2,1,0:T(8,128)} %fusion.46), kind=kOutput, calls=%fused_computation.18 | convolution fusion | flops 2216607744 | bytes 14286848 | tf_op jit(solution)/shard_map/gtf,gfd->td/dot_general | solution.py:163
  153.4 4.2 %all-to-all-start.8 = ((bf16[8,24,2048]{2,1,0:T(8,128)(2,1)}), bf16[8,24,2048]{2,1,0:T(8,128)(2,1)}, u32[]{:S(2)}, u32[]{:S(2)}) async-start(bf16[8,24,2048]{2,1,0:T(8,128)(2,1)} %bitcast.159), calls=%async_computation.8 | async-start | bytes 1572864 | tf_op jit(solution)/shard_map/all_to_all | solution.py:166
  157.6 5.9 %fusion.40 = f32[4,192,352]{2,1,0:T(8,128)} fusion(bf16[192,2048,1]{1,0,2:T(8,128)(2,1)} %bitcast.19, bf16[8,2048,352]{1,2,0:T(8,128)(2,1)} %param.28), kind=kOutput, calls=%fused_computation.37 | convolution fusion | flops 1107296256 | bytes 7634944 | tf_op jit(solution)/shard_map/td,gdf->gtf/dot_general | solution.py:158
  163.5 9.1 %fusion.22 = bf16[192,2048]{1,0:T(8,128)(2,1)} fusion(bf16[8,352,2048]{2,1,0:T(8,128)(2,1)} %param.30, bf16[192,2048,1]{1,0,2:T(8,128)(2,1)} %bitcast.19, bf16[8,2048,352]{1,2,0:T(8,128)(2,1)} %param.29, f32[4,192,352]{2,1,0:T(8,128)} %fusion.40), kind=kOutput, calls=%fused_computation.19 | convolution fusion | flops 2216607744 | bytes 14286848 | tf_op jit(solution)/shard_map/gtf,gfd->td/dot_general | solution.py:163
  172.6 4.4 %all-to-all-start.6 = ((bf16[8,24,2048]{2,1,0:T(8,128)(2,1)}), bf16[8,24,2048]{2,1,0:T(8,128)(2,1)}, u32[]{:S(2)}, u32[]{:S(2)}) async-start(bf16[8,24,2048]{2,1,0:T(8,128)(2,1)} %bitcast.158), calls=%async_computation.6 | async-start | bytes 1572864 | tf_op jit(solution)/shard_map/all_to_all | solution.py:166
  177.0 1.7 subtract_convert_fusion
  178.7 3.5 %fusion.116 = f32[128,704]{0,1:T(8,128)} fusion(bf16[2048,704]{0,1:T(8,128)(2,1)} %param.31, bf16[128,2048]{0,1:T(8,128)(2,1)S(1)} %fusion.69), kind=kOutput, calls=%fused_computation.135 | convolution fusion | flops 369098752 | bytes 3768320 | tf_op jit(solution)/shard_map/dot_general | solution.py:174
  182.2 2.5 %fusion.96 = f32[128,2048]{1,0:T(8,128)} fusion(bf16[192,2048]{1,0:T(8,128)(2,1)} %bitcast.34, bf16[128,384]{1,0:T(8,128)(2,1)S(1)} %get-tuple-element.5), kind=kOutput, calls=%fused_computation.99 | convolution fusion | flops 100663296 | bytes 1900544 | tf_op jit(solution)/shard_map/dot_general | solution.py:171
  184.7 4.8 %all-to-all-done.6 = bf16[8,24,2048]{2,1,0:T(8,128)(2,1)} async-done(((bf16[8,24,2048]{2,1,0:T(8,128)(2,1)}), bf16[8,24,2048]{2,1,0:T(8,128)(2,1)}, u32[]{:S(2)}, u32[]{:S(2)}) %all-to-all-start.6) | async-done | bytes 786464 | tf_op jit(solution)/shard_map/all_to_all | solution.py:166
  189.5 1.6 fusion.99
  191.1 1.5 convolution_add_fusion.2
  192.6 2.5 %fusion.25 = f32[128,2048]{1,0:T(8,128)} fusion(f32[128,2048]{1,0:T(8,128)S(1)} %convolution_add_fusion.2, f32[128,2048]{1,0:T(8,128)S(1)} %copy-done.2, bf16[192,2048]{1,0:T(8,128)(2,1)} %bitcast.34, bf16[128,384]{1,0:T(8,128)(2,1)S(1)} %copy-done.5), kind=kOutput, calls=%fused_computation.22 | convolution fusion | flops 101187584 | bytes 3997696 | tf_op jit(solution)/shard_map/dot_general | solution.py:172
  195.0 5.2 %fusion.26 = bf16[128,2048]{1,0:T(8,128)(2,1)} fusion(f32[128,2048]{1,0:T(8,128)} %fusion.25, bf16[704,2048]{1,0:T(8,128)(2,1)S(1)} %copy-done, bf16[2048,704]{0,1:T(8,128)(2,1)} %param.32, bf16[128,2048]{0,1:T(8,128)(2,1)S(1)} %fusion.69, f32[128,704]{0,1:T(8,128)} %fusion.116), kind=kOutput, calls=%fused_computation.25 | convolution fusion | flops 739262464 | bytes 8224768 | tf_op jit(solution)/shard_map/dot_general | solution.py:177
  200.2 1.9 copy.120
  202.1 3.5 %all-to-all-start.9 = ((bf16[4,128,512]{2,1,0:T(8,128)(2,1)}), bf16[4,128,512]{2,1,0:T(8,128)(2,1)S(1)}, u32[]{:S(2)}, u32[]{:S(2)}) async-start(bf16[4,128,512]{2,1,0:T(8,128)(2,1)} %bitcast.155), calls=%async_computation.9 | async-start | bytes 1048576 | tf_op jit(solution)/shard_map/all_to_all | solution.py:185
  206.3 10.9 %all-to-all-done.9 = bf16[4,128,512]{2,1,0:T(8,128)(2,1)S(1)} async-done(((bf16[4,128,512]{2,1,0:T(8,128)(2,1)}), bf16[4,128,512]{2,1,0:T(8,128)(2,1)S(1)}, u32[]{:S(2)}, u32[]{:S(2)}) %all-to-all-start.9) | async-done | bytes 524320 | tf_op jit(solution)/shard_map/all_to_all | solution.py:185
  (76 shorter events, 22.9 us)
Async XLA Ops:
  0.6 194.4 %copy-start = (bf16[704,2048]{1,0:T(8,128)(2,1)S(1)}, bf16[704,2048]{1,0:T(8,128)(2,1)}, u32[]{:S(2)}) copy-start(bf16[704,2048]{1,0:T(8,128)(2,1)} %param.33) | copy-start | bytes 8650756
  0.6 7.6 %copy-start.11 = (bf16[64,2,512]{2,1,0:T(2,128)(2,1)S(1)}, bf16[64,2,512]{2,1,0:T(2,128)(2,1)}, u32[]{:S(2)}) copy-start(bf16[64,2,512]{2,1,0:T(2,128)(2,1)} %param.18) | copy-start | bytes 393220
  0.7 7.6 %copy-start.9 = (bf16[128,2,512]{2,1,0:T(2,128)(2,1)S(1)}, bf16[128,2,512]{2,1,0:T(2,128)(2,1)}, u32[]{:S(2)}) copy-start(bf16[128,2,512]{2,1,0:T(2,128)(2,1)} %param.20) | copy-start | bytes 786436
  0.7 8.8 %copy-start.10 = (bf16[128,2,512]{2,1,0:T(2,128)(2,1)S(1)}, bf16[128,2,512]{2,1,0:T(2,128)(2,1)}, u32[]{:S(2)}) copy-start(bf16[128,2,512]{2,1,0:T(2,128)(2,1)} %param.21) | copy-start | bytes 786436
  2.9 11.0 %copy-start.13 = (s32[2]{0:T(128)S(1)}, s32[2]{0:T(128)}, u32[]{:S(2)}) copy-start(s32[2]{0:T(128)} %param.22) | copy-start | bytes 28
  2.9 20.8 %all-to-all-start = ((bf16[8,64,2,512]{3,1,2,0:T(8,128)(2,1)}), bf16[8,64,2,512]{3,1,2,0:T(8,128)(2,1)}, u32[]{:S(2)}, u32[]{:S(2)}) async-start(bf16[8,64,2,512]{3,1,2,0:T(8,128)(2,1)} %broadcast_in_dim.35), calls=%async_computation | async-start | bytes 2097152 | tf_op jit(solution)/shard_map/all_to_all | solution.py:49
  13.9 14.3 %copy-start.8 = (bf16[192,2,4,128]{3,2,1,0:T(4,128)(2,1)S(1)}, bf16[192,2,4,128]{3,2,1,0:T(4,128)(2,1)}, u32[]{:S(2)}) copy-start(bf16[192,2,4,128]{3,2,1,0:T(4,128)(2,1)} %reshape.297) | copy-start | bytes 1179652
  30.3 1.7 copy-start.3
  30.3 9.6 %copy-start.7 = (bf16[192,2,4,128]{3,2,1,0:T(4,128)(2,1)S(1)}, bf16[192,2,4,128]{3,2,1,0:T(4,128)(2,1)}, u32[]{:S(2)}) copy-start(bf16[192,2,4,128]{3,2,1,0:T(4,128)(2,1)} %reshape.298) | copy-start | bytes 1179652
  36.5 11.9 %all-to-all-start.1 = ((f32[8,1,1024]{2,1,0:T(1,128)}), f32[8,1,1024]{2,1,0:T(1,128)S(1)}, u32[]{:S(2)}, u32[]{:S(2)}) async-start(f32[8,1,1024]{2,1,0:T(1,128)} %reshape.300), calls=%async_computation.1 | async-start | bytes 65536 | tf_op jit(solution)/shard_map/all_to_all | solution.py:80
  48.4 19.7 %all-to-all-start.2 = ((bf16[8,64,2,4,128]{4,1,3,2,0:T(8,128)(2,1)}), bf16[8,64,2,4,128]{4,1,3,2,0:T(8,128)(2,1)}, u32[]{:S(2)}, u32[]{:S(2)}) async-start(bf16[8,64,2,4,128]{4,1,3,2,0:T(8,128)(2,1)} %copy.85), calls=%async_computation.2 | async-start | bytes 2097152 | tf_op jit(solution)/shard_map/all_to_all | solution.py:77
  71.9 11.0 %copy-start.12 = (s32[64,2,6]{0,1,2:T(2,128)S(1)}, s32[64,2,6]{0,1,2:T(2,128)}, u32[]{:S(2)}) copy-start(s32[64,2,6]{0,1,2:T(2,128)} %param.26) | copy-start | bytes 9220
  75.6 16.8 %all-to-all-start.3 = ((bf16[4,128,512]{2,1,0:T(8,128)(2,1)}), bf16[4,128,512]{2,1,0:T(8,128)(2,1)S(1)}, u32[]{:S(2)}, u32[]{:S(2)}) async-start(bf16[4,128,512]{2,1,0:T(8,128)(2,1)} %copy.87), calls=%async_computation.3 | async-start | bytes 1048576 | tf_op jit(solution)/shard_map/all_to_all | solution.py:103
  83.0 9.4 %copy-start.4 = (s32[64,2,6]{2,1,0:T(2,128)}, s32[64,2,6]{2,1,0:T(2,128)S(1)}, u32[]{:S(2)}) copy-start(s32[64,2,6]{2,1,0:T(2,128)S(1)} %copy.89) | copy-start | bytes 9220
  94.4 15.6 %all-to-all-start.4 = ((bf16[4,128,512]{1,2,0:T(8,128)(2,1)}), bf16[4,128,512]{1,2,0:T(8,128)(2,1)S(1)}, u32[]{:S(2)}, u32[]{:S(2)}) async-start(bf16[4,128,512]{1,2,0:T(8,128)(2,1)} %broadcast_in_dim.69), calls=%async_computation.4 | async-start | bytes 1048576 | tf_op jit(solution)/shard_map/all_to_all | solution.py:109
  110.0 0.8 copy-start.1
  134.1 19.3 %all-to-all-start.5 = ((bf16[8,24,2048]{2,1,0:T(8,128)(2,1)}), bf16[8,24,2048]{2,1,0:T(8,128)(2,1)}, u32[]{:S(2)}, u32[]{:S(2)}) async-start(bf16[8,24,2048]{2,1,0:T(8,128)(2,1)} %bitcast.151), calls=%async_computation.5 | async-start | bytes 1572864 | tf_op jit(solution)/shard_map/all_to_all | solution.py:155
  153.4 19.2 %all-to-all-start.8 = ((bf16[8,24,2048]{2,1,0:T(8,128)(2,1)}), bf16[8,24,2048]{2,1,0:T(8,128)(2,1)}, u32[]{:S(2)}, u32[]{:S(2)}) async-start(bf16[8,24,2048]{2,1,0:T(8,128)(2,1)} %bitcast.159), calls=%async_computation.8 | async-start | bytes 1572864 | tf_op jit(solution)/shard_map/all_to_all | solution.py:166
  172.6 16.9 %all-to-all-start.6 = ((bf16[8,24,2048]{2,1,0:T(8,128)(2,1)}), bf16[8,24,2048]{2,1,0:T(8,128)(2,1)}, u32[]{:S(2)}, u32[]{:S(2)}) async-start(bf16[8,24,2048]{2,1,0:T(8,128)(2,1)} %bitcast.158), calls=%async_computation.6 | async-start | bytes 1572864 | tf_op jit(solution)/shard_map/all_to_all | solution.py:166
  178.7 3.5 %copy-start.6 = (bf16[128,384]{1,0:T(8,128)(2,1)}, bf16[128,384]{1,0:T(8,128)(2,1)S(1)}, u32[]{:S(2)}) copy-start(bf16[128,384]{1,0:T(8,128)(2,1)S(1)} %get-tuple-element.5) | copy-start | bytes 294916
  189.5 3.0 %copy-start.2 = (f32[128,2048]{1,0:T(8,128)S(1)}, f32[128,2048]{1,0:T(8,128)}, u32[]{:S(2)}) copy-start(f32[128,2048]{1,0:T(8,128)} %fusion.96) | copy-start | bytes 3145732
  189.5 3.0 %copy-start.5 = (bf16[128,384]{1,0:T(8,128)(2,1)S(1)}, bf16[128,384]{1,0:T(8,128)(2,1)}, u32[]{:S(2)}) copy-start(bf16[128,384]{1,0:T(8,128)(2,1)} %get-tuple-element.4) | copy-start | bytes 294916
  202.1 15.1 %all-to-all-start.9 = ((bf16[4,128,512]{2,1,0:T(8,128)(2,1)}), bf16[4,128,512]{2,1,0:T(8,128)(2,1)S(1)}, u32[]{:S(2)}, u32[]{:S(2)}) async-start(bf16[4,128,512]{2,1,0:T(8,128)(2,1)} %bitcast.155), calls=%async_computation.9 | async-start | bytes 1048576 | tf_op jit(solution)/shard_map/all_to_all | solution.py:185

commit v5 on v2

--- a/solution.py
+++ b/solution.py
@@ -144,6 +144,11 @@
     ).astype(jnp.bfloat16)
     outgoing = outgoing.reshape(row_count, experts_dev, CAP, model_width)
     arrived = lax.all_to_all(outgoing, "row", 0, 0, tiled=True)
+    shared_g = jnp.dot(tokens, shared_gate, preferred_element_type=jnp.float32)
+    shared_u = jnp.dot(tokens, shared_up, preferred_element_type=jnp.float32)
+    shared_act = (jax.nn.silu(shared_g) * shared_u).astype(jnp.bfloat16)
+    shared_part = jnp.dot(shared_act, shared_down, preferred_element_type=jnp.float32)
+    arrived, shared_part = lax.optimization_barrier((arrived, shared_part))
     hidden = w_gate.shape[2]
     wg = w_gate.reshape(experts_dev, groups_dev, model_width, hidden)
     wu = w_up.reshape(experts_dev, groups_dev, model_width, hidden)
@@ -160,10 +165,6 @@
     routed = jnp.dot(combine_hi, returned, preferred_element_type=jnp.float32) + jnp.dot(
         combine_lo, returned, preferred_element_type=jnp.float32
     )
-    shared_g = jnp.dot(tokens, shared_gate, preferred_element_type=jnp.float32)
-    shared_u = jnp.dot(tokens, shared_up, preferred_element_type=jnp.float32)
-    shared_act = (jax.nn.silu(shared_g) * shared_u).astype(jnp.bfloat16)
-    shared_part = jnp.dot(shared_act, shared_down, preferred_element_type=jnp.float32)
     ffn_chunks = (
         (routed + shared_part)
         .astype(jnp.bfloat16)

time: 221 us -> 212 us (0.959)
  local copies, waits for them, and re-layouts: 39.4 us -> 34.8 us
  blocking collectives: 27.6 us -> 23.5 us
  starting transfers between devices: 29.4 us -> 31.9 us
    all_to_all x1, waiting for transfers between devices: 17.6 us -> 12.7 us  [body(): arrived = lax.all_to_all(outgoing, 'row', 0, 0, tiled=True)]
    all_to_all x1, blocking collectives: 27.6 us -> 23.5 us  [body(): lax.all_to_all(expert_out, 'row', 0, 0, tiled=True)]
    all_to_all x1, waiting for transfers between devices: 2.2 us -> 5.53 us  [body(): lax.all_to_all(jnp.broadcast_to(mixed_slice[None], (col_count, token_coun...]
    dot_general x1, matrix products: 12.9 us -> 15.5 us  [body(): jnp.einsum('lgnsf,lgfd->nlsd', hidden_act, wd, preferred_element_type=jnp...]
    all_to_all x1, starting transfers between devices: 4.29 us -> 6.83 us  [body(): arrived = lax.all_to_all(outgoing, 'row', 0, 0, tiled=True)]
    dot_general x1, matrix products: 2.81 us -> 0.44 us  [body(): jnp.dot(combine_lo, returned, preferred_element_type=jnp.float32)]
    all_to_all x1, waiting for transfers between devices: 11.1 us -> 13.4 us  [body(): lax.all_to_all(ffn_chunks, 'col', 0, 0, tiled=True).astype(jnp.float32)]
    unnamed x31 -> x33, local copies, waits for them, and re-layouts: 6.47 us -> 5.83 us
  transfers between devices with their start and end apart: 7 -> 7, of which waited for: 6 -> 6; matrix products, arithmetic and copies ran while one was open for 17% -> 19% of each run, Pallas kernels for 0% -> 0%
where the time goes in v5:
time: 212 us; the launch traced here: 211 us
  waiting for transfers between devices  58.1 us (27%)
  matrix products  42.6 us (20%)
  local copies, waits for them, and re-layouts  34.8 us (16%)
  starting transfers between devices  31.9 us (15%)
  blocking collectives  23.5 us (11%)
  other arithmetic  18.7 us (9%)
    all_to_all x1, blocking collectives, body(): lax.all_to_all(expert_out, 'row', 0, 0, tiled=True)  23.5 us
    dot_general x1, matrix products, body(): jnp.einsum('lgnsf,lgfd->nlsd', hidden_act, wd, preferred_element_type=jnp...  15.5 us
    all_to_all x1, waiting for transfers between devices, body(): lax.all_to_all(product.reshape(row_count, rows_here, requests, heads_here...  14 us
    all_to_all x1, waiting for transfers between devices, body(): lax.all_to_all(ffn_chunks, 'col', 0, 0, tiled=True).astype(jnp.float32)  13.4 us
    all_to_all x1, waiting for transfers between devices, body(): arrived = lax.all_to_all(outgoing, 'row', 0, 0, tiled=True)  12.7 us
    all_to_all x1, waiting for transfers between devices, body(): lax.all_to_all(jnp.broadcast_to(queries[None], (row_count,) + queries.sha...  9.38 us
    dot_general x1, matrix products, body(): jnp.einsum('nlsd,lgdf->lgnsf', arrived, wu, preferred_element_type=jnp.fl...  7.06 us
    all_to_all x1, starting transfers between devices, body(): arrived = lax.all_to_all(outgoing, 'row', 0, 0, tiled=True)  6.83 us
  transfers between devices with their start and end apart: 7, of which 6 were waited for; matrix products, arithmetic and copies ran while one was open for 19% of the time, Pallas kernels for 0%

profile of v5, /device:TPU:0, one launch (start us, length us, event | category | flops | bytes accessed | tf_op | source)
XLA Modules:
  0.0 210.7 jit_solution(14630542564371391322)
XLA Ops:
  0.7 1.1 copy.85
  1.8 1.1 broadcast_in_dim.35
  2.9 5.3 %all-to-all-start = ((bf16[8,64,2,512]{3,1,2,0:T(8,128)(2,1)}), bf16[8,64,2,512]{3,1,2,0:T(8,128)(2,1)}, u32[]{:S(2)}, u32[]{:S(2)}) async-start(bf16[8,64,2,512]{3,1,2,0:T(8,128)(2,1)} %broadcast_in_dim.35), calls=%async_computation | async-start | bytes 2097152 | tf_op jit(solution)/shard_map/all_to_all | solution.py:49
  8.2 1.3 pad_maximum_fusion
  9.5 1.4 pad_maximum_fusion.1
  10.9 2.0 reshape.275
  12.9 1.0 reshape.276
  14.3 9.4 %all-to-all-done = bf16[8,64,2,512]{3,1,2,0:T(8,128)(2,1)} async-done(((bf16[8,64,2,512]{3,1,2,0:T(8,128)(2,1)}), bf16[8,64,2,512]{3,1,2,0:T(8,128)(2,1)}, u32[]{:S(2)}, u32[]{:S(2)}) %all-to-all-start) | async-done | bytes 1048608 | tf_op jit(solution)/shard_map/all_to_all | solution.py:49
  23.7 2.4 %copy.86 = bf16[8,64,2,512]{3,1,0,2:T(8,128)(2,1)} copy(bf16[8,64,2,512]{3,1,2,0:T(8,128)(2,1)} %all-to-all-done) | data formatting | bytes 2097152 | tf_op jit(solution)/shard_map/all_to_all | solution.py:49
  26.1 2.2 %reshape.250 = bf16[512,2,4,128]{3,2,0,1:T(4,128)(2,1)} reshape(bf16[8,64,2,512]{3,1,0,2:T(8,128)(2,1)} %copy.86) | data formatting | bytes 2097152 | tf_op jit(solution)/shard_map/reshape | solution.py:53
  28.2 2.0 fusion
  30.3 1.6 copy-done.4
  34.9 1.6 reshape.278
  36.5 3.3 %all-to-all-start.1 = ((f32[8,1,1024]{2,1,0:T(1,128)}), f32[8,1,1024]{2,1,0:T(1,128)S(1)}, u32[]{:S(2)}, u32[]{:S(2)}) async-start(f32[8,1,1024]{2,1,0:T(1,128)} %reshape.278), calls=%async_computation.1 | async-start | bytes 65536 | tf_op jit(solution)/shard_map/all_to_all | solution.py:80
  39.9 3.9 %fusion.24 = bf16[512,2,4,128]{0,3,2,1:T(8,128)(2,1)} fusion(f32[2,4,192,512]{3,2,1,0:T(8,128)} %copy-done.4, f32[2,4,512]{2,1,0:T(4,128)S(1)} %get-tuple-element.8, pred[2,512,192]{1,2,0:T(8,128)(4,1)S(1)} %broadcast_or_fusion, bf16[192,2,4,128]{3,2,1,0:T(4,128)(2,1)S(1)} %copy-done.7), kind=kOutput, calls=%fused_computation.31 | convolution fusion | flops 205783040 | bytes 4800512 | tf_op jit(solution)/shard_map/rhij,jrhd->irhd/dot_general | solution.py:70
  43.8 2.3 %copy.93 = bf16[512,2,4,128]{3,0,2,1:T(8,128)(2,1)} copy(bf16[512,2,4,128]{0,3,2,1:T(8,128)(2,1)} %fusion.24) | data formatting | bytes 2097152 | tf_op jit(solution)/shard_map/convert_element_type | solution.py:75
  46.1 2.4 %copy.94 = bf16[8,64,2,4,128]{4,1,3,2,0:T(8,128)(2,1)} copy(bf16[8,64,2,4,128]{4,1,0,3,2:T(8,128)(2,1)} %bitcast.173) | data formatting | bytes 2097152 | tf_op jit(solution)/shard_map/reshape | solution.py:78
  48.4 4.2 %all-to-all-start.2 = ((bf16[8,64,2,4,128]{4,1,3,2,0:T(8,128)(2,1)}), bf16[8,64,2,4,128]{4,1,3,2,0:T(8,128)(2,1)}, u32[]{:S(2)}, u32[]{:S(2)}) async-start(bf16[8,64,2,4,128]{4,1,3,2,0:T(8,128)(2,1)} %copy.94), calls=%async_computation.2 | async-start | bytes 2097152 | tf_op jit(solution)/shard_map/all_to_all | solution.py:77
  54.1 14.0 %all-to-all-done.2 = bf16[8,64,2,4,128]{4,1,3,2,0:T(8,128)(2,1)} async-done(((bf16[8,64,2,4,128]{4,1,3,2,0:T(8,128)(2,1)}), bf16[8,64,2,4,128]{4,1,3,2,0:T(8,128)(2,1)}, u32[]{:S(2)}, u32[]{:S(2)}) %all-to-all-start.2) | async-done | bytes 1048608 | tf_op jit(solution)/shard_map/all_to_all | solution.py:77
  68.1 1.8 multiply_reduce_fusion
  69.9 2.1 fusion.4
  72.5 1.1 reshape.255
  73.7 1.9 copy.96
  75.6 5.3 %all-to-all-start.3 = ((bf16[4,128,512]{2,1,0:T(8,128)(2,1)}), bf16[4,128,512]{2,1,0:T(8,128)(2,1)S(1)}, u32[]{:S(2)}, u32[]{:S(2)}) async-start(bf16[4,128,512]{2,1,0:T(8,128)(2,1)} %copy.96), calls=%async_computation.3 | async-start | bytes 1048576 | tf_op jit(solution)/shard_map/all_to_all | solution.py:103
  82.9 4.4 %reduce-window.6 = s32[64,6,128]{2,0,1:T(8,128)} reduce-window(s32[64,6,128]{2,0,1:T(8,128)} %fusion.43, s32[]{:T(128)} %constant.32.clone.1), window={size=1x1x128 pad=0_0x0_0x127_0}, to_apply=%region_6.7 | reduce-window | flops 6242304 | bytes 393220 | tf_op jit(solution)/shard_map/reduce-window
  87.3 2.0 reshape.248
  89.3 3.1 %all-to-all-done.3 = bf16[4,128,512]{2,1,0:T(8,128)(2,1)S(1)} async-done(((bf16[4,128,512]{2,1,0:T(8,128)(2,1)}), bf16[4,128,512]{2,1,0:T(8,128)(2,1)S(1)}, u32[]{:S(2)}, u32[]{:S(2)}) %all-to-all-start.3) | async-done | bytes 524320 | tf_op jit(solution)/shard_map/all_to_all | solution.py:103
  92.5 0.9 add_convert_fusion
  93.6 0.9 broadcast_in_dim.69
  94.4 3.5 %all-to-all-start.4 = ((bf16[4,128,512]{1,2,0:T(8,128)(2,1)}), bf16[4,128,512]{1,2,0:T(8,128)(2,1)S(1)}, u32[]{:S(2)}, u32[]{:S(2)}) async-start(bf16[4,128,512]{1,2,0:T(8,128)(2,1)} %broadcast_in_dim.69), calls=%async_computation.4 | async-start | bytes 1048576 | tf_op jit(solution)/shard_map/all_to_all | solution.py:109
  97.9 1.2 slice_reduce_fusion
  99.1 1.1 fusion.42
  101.0 1.6 add_select_fusion.2
  102.6 0.9 copy.102
  103.5 1.0 select_reduce_fusion
  104.5 5.5 %all-to-all-done.4 = bf16[4,128,512]{1,2,0:T(8,128)(2,1)S(1)} async-done(((bf16[4,128,512]{1,2,0:T(8,128)(2,1)}), bf16[4,128,512]{1,2,0:T(8,128)(2,1)S(1)}, u32[]{:S(2)}, u32[]{:S(2)}) %all-to-all-start.4) | async-done | bytes 524320 | tf_op jit(solution)/shard_map/all_to_all | solution.py:109
  110.8 1.4 fusion.30
  112.2 2.6 %convolution_convert_fusion = bf16[384,2048]{1,0:T(8,128)(2,1)} fusion(bf16[128,2048]{0,1:T(8,128)(2,1)S(1)} %fusion.30, bf16[128,384]{1,0:T(8,128)(2,1)} %get-tuple-element.7), kind=kOutput, calls=%fused_computation.3 | convolution fusion | flops 202113024 | bytes 2195456 | tf_op jit(solution)/shard_map/dot_general | solution.py:142
  114.8 6.8 %all-to-all-start.5 = ((bf16[8,2,24,2048]{3,2,1,0:T(8,128)(2,1)}), bf16[8,2,24,2048]{3,2,1,0:T(8,128)(2,1)}, u32[]{:S(2)}, u32[]{:S(2)}) async-start(bf16[8,2,24,2048]{3,2,1,0:T(8,128)(2,1)} %bitcast.172), calls=%async_computation.5 | async-start | bytes 3145728 | tf_op jit(solution)/shard_map/all_to_all | solution.py:146
  121.7 3.5 %fusion.65 = f32[128,704]{0,1:T(8,128)} fusion(bf16[2048,704]{0,1:T(8,128)(2,1)} %param.31, bf16[128,2048]{0,1:T(8,128)(2,1)S(1)} %fusion.30), kind=kOutput, calls=%fused_computation.114 | convolution fusion | flops 369098752 | bytes 3768320 | tf_op jit(solution)/shard_map/dot_general | solution.py:147
  125.1 5.0 %fusion.28 = f32[128,2048]{1,0:T(8,128)} fusion(bf16[704,2048]{1,0:T(8,128)(2,1)S(1)} %copy-done, bf16[2048,704]{0,1:T(8,128)(2,1)} %param.32, bf16[128,2048]{0,1:T(8,128)(2,1)S(1)} %fusion.30, f32[128,704]{0,1:T(8,128)} %fusion.65), kind=kOutput, calls=%fused_computation.37 | convolution fusion | flops 738738176 | bytes 7700480 | tf_op jit(solution)/shard_map/dot_general | solution.py:150
  130.1 12.7 %all-to-all-done.5 = bf16[8,2,24,2048]{3,2,1,0:T(8,128)(2,1)} async-done(((bf16[8,2,24,2048]{3,2,1,0:T(8,128)(2,1)}), bf16[8,2,24,2048]{3,2,1,0:T(8,128)(2,1)}, u32[]{:S(2)}, u32[]{:S(2)}) %all-to-all-start.5) | async-done | bytes 1572896 | tf_op jit(solution)/shard_map/all_to_all | solution.py:146
  142.8 7.1 %fusion.21 = f32[2,8,24,4,352]{4,2,3,1,0:T(8,128)S(1)} fusion(bf16[2,4,2048,352,1]{2,3,1,4,0:T(8,128)(2,1)} %bitcast.185, bf16[8,2,24,2048]{3,2,1,0:T(8,128)(2,1)} %all-to-all-done.5), kind=kOutput, calls=%fused_computation.28 | convolution fusion | flops 2214592512 | bytes 15269888 | tf_op jit(solution)/shard_map/nlsd,lgdf->lgnsf/dot_general | solution.py:157
  149.9 15.5 %fusion.1 = bf16[8,2,24,2048]{3,2,0,1:T(8,128)(2,1)} fusion(bf16[2,4,352,2048,1]{3,2,1,4,0:T(8,128)(2,1)} %bitcast.186, f32[2,8,24,4,352]{4,2,3,1,0:T(8,128)S(1)} %fusion.21, bf16[2,4,2048,352,1]{2,3,1,4,0:T(8,128)(2,1)} %bitcast.187, bf16[8,2,24,2048]{3,2,1,0:T(8,128)(2,1)} %all-to-all-done.5), kind=kOutput, calls=%fused_computation.5 | convolution fusion | flops 4433215488 | bytes 28377088 | tf_op jit(solution)/shard_map/lgnsf,lgfd->nlsd/dot_general | solution.py:159
  165.4 1.6 copy.108
  167.0 23.5 %all_to_all.40 = bf16[8,2,24,2048]{3,2,1,0:T(8,128)(2,1)S(1)} all-to-all(bf16[8,2,24,2048]{3,2,1,0:T(8,128)(2,1)S(1)} %copy.108), channel_id=1, replica_groups=mesh['row'=8,'col'=4] {'row'}, dimensions={0} | all-to-all | bytes 3145728 | tf_op jit(solution)/shard_map/all_to_all | solution.py:162
  192.3 3.5 %all-to-all-start.7 = ((bf16[4,128,512]{2,1,0:T(8,128)(2,1)}), bf16[4,128,512]{2,1,0:T(8,128)(2,1)S(1)}, u32[]{:S(2)}, u32[]{:S(2)}) async-start(bf16[4,128,512]{2,1,0:T(8,128)(2,1)} %bitcast.176), calls=%async_computation.7 | async-start | bytes 1048576 | tf_op jit(solution)/shard_map/all_to_all | solution.py:175
  196.5 13.4 %all-to-all-done.7 = bf16[4,128,512]{2,1,0:T(8,128)(2,1)S(1)} async-done(((bf16[4,128,512]{2,1,0:T(8,128)(2,1)}), bf16[4,128,512]{2,1,0:T(8,128)(2,1)S(1)}, u32[]{:S(2)}, u32[]{:S(2)}) %all-to-all-start.7) | async-done | bytes 524320 | tf_op jit(solution)/shard_map/all_to_all | solution.py:175
  (67 shorter events, 12.4 us)
Async XLA Ops:
  0.6 124.5 %copy-start = (bf16[704,2048]{1,0:T(8,128)(2,1)S(1)}, bf16[704,2048]{1,0:T(8,128)(2,1)}, u32[]{:S(2)}) copy-start(bf16[704,2048]{1,0:T(8,128)(2,1)} %param.33) | copy-start | bytes 8650756
  0.6 7.6 %copy-start.9 = (bf16[128,2,512]{2,1,0:T(2,128)(2,1)S(1)}, bf16[128,2,512]{2,1,0:T(2,128)(2,1)}, u32[]{:S(2)}) copy-start(bf16[128,2,512]{2,1,0:T(2,128)(2,1)} %param.20) | copy-start | bytes 786436
  0.7 7.6 %copy-start.11 = (bf16[64,2,512]{2,1,0:T(2,128)(2,1)S(1)}, bf16[64,2,512]{2,1,0:T(2,128)(2,1)}, u32[]{:S(2)}) copy-start(bf16[64,2,512]{2,1,0:T(2,128)(2,1)} %param.18) | copy-start | bytes 393220
  0.7 8.8 %copy-start.10 = (bf16[128,2,512]{2,1,0:T(2,128)(2,1)S(1)}, bf16[128,2,512]{2,1,0:T(2,128)(2,1)}, u32[]{:S(2)}) copy-start(bf16[128,2,512]{2,1,0:T(2,128)(2,1)} %param.21) | copy-start | bytes 786436
  2.9 11.0 %copy-start.13 = (s32[2]{0:T(128)S(1)}, s32[2]{0:T(128)}, u32[]{:S(2)}) copy-start(s32[2]{0:T(128)} %param.22) | copy-start | bytes 28
  2.9 20.8 %all-to-all-start = ((bf16[8,64,2,512]{3,1,2,0:T(8,128)(2,1)}), bf16[8,64,2,512]{3,1,2,0:T(8,128)(2,1)}, u32[]{:S(2)}, u32[]{:S(2)}) async-start(bf16[8,64,2,512]{3,1,2,0:T(8,128)(2,1)} %broadcast_in_dim.35), calls=%async_computation | async-start | bytes 2097152 | tf_op jit(solution)/shard_map/all_to_all | solution.py:49
  13.9 14.3 %copy-start.8 = (bf16[192,2,4,128]{3,2,1,0:T(4,128)(2,1)S(1)}, bf16[192,2,4,128]{3,2,1,0:T(4,128)(2,1)}, u32[]{:S(2)}) copy-start(bf16[192,2,4,128]{3,2,1,0:T(4,128)(2,1)} %reshape.275) | copy-start | bytes 1179652
  30.3 1.7 copy-start.4
  30.3 9.6 %copy-start.7 = (bf16[192,2,4,128]{3,2,1,0:T(4,128)(2,1)S(1)}, bf16[192,2,4,128]{3,2,1,0:T(4,128)(2,1)}, u32[]{:S(2)}) copy-start(bf16[192,2,4,128]{3,2,1,0:T(4,128)(2,1)} %reshape.276) | copy-start | bytes 1179652
  36.5 11.9 %all-to-all-start.1 = ((f32[8,1,1024]{2,1,0:T(1,128)}), f32[8,1,1024]{2,1,0:T(1,128)S(1)}, u32[]{:S(2)}, u32[]{:S(2)}) async-start(f32[8,1,1024]{2,1,0:T(1,128)} %reshape.278), calls=%async_computation.1 | async-start | bytes 65536 | tf_op jit(solution)/shard_map/all_to_all | solution.py:80
  48.4 19.7 %all-to-all-start.2 = ((bf16[8,64,2,4,128]{4,1,3,2,0:T(8,128)(2,1)}), bf16[8,64,2,4,128]{4,1,3,2,0:T(8,128)(2,1)}, u32[]{:S(2)}, u32[]{:S(2)}) async-start(bf16[8,64,2,4,128]{4,1,3,2,0:T(8,128)(2,1)} %copy.94), calls=%async_computation.2 | async-start | bytes 2097152 | tf_op jit(solution)/shard_map/all_to_all | solution.py:77
  71.9 8.9 %copy-start.12 = (s32[64,2,6]{0,1,2:T(2,128)S(1)}, s32[64,2,6]{0,1,2:T(2,128)}, u32[]{:S(2)}) copy-start(s32[64,2,6]{0,1,2:T(2,128)} %param.26) | copy-start | bytes 9220
  75.6 16.8 %all-to-all-start.3 = ((bf16[4,128,512]{2,1,0:T(8,128)(2,1)}), bf16[4,128,512]{2,1,0:T(8,128)(2,1)S(1)}, u32[]{:S(2)}, u32[]{:S(2)}) async-start(bf16[4,128,512]{2,1,0:T(8,128)(2,1)} %copy.96), calls=%async_computation.3 | async-start | bytes 1048576 | tf_op jit(solution)/shard_map/all_to_all | solution.py:103
  81.0 11.4 %copy-start.6 = (s32[64,2,6]{2,1,0:T(2,128)}, s32[64,2,6]{2,1,0:T(2,128)S(1)}, u32[]{:S(2)}) copy-start(s32[64,2,6]{2,1,0:T(2,128)S(1)} %copy.98) | copy-start | bytes 9220
  94.4 15.6 %all-to-all-start.4 = ((bf16[4,128,512]{1,2,0:T(8,128)(2,1)}), bf16[4,128,512]{1,2,0:T(8,128)(2,1)S(1)}, u32[]{:S(2)}, u32[]{:S(2)}) async-start(bf16[4,128,512]{1,2,0:T(8,128)(2,1)} %broadcast_in_dim.69), calls=%async_computation.4 | async-start | bytes 1048576 | tf_op jit(solution)/shard_map/all_to_all | solution.py:109
  110.0 0.8 copy-start.2
  114.8 28.0 %all-to-all-start.5 = ((bf16[8,2,24,2048]{3,2,1,0:T(8,128)(2,1)}), bf16[8,2,24,2048]{3,2,1,0:T(8,128)(2,1)}, u32[]{:S(2)}, u32[]{:S(2)}) async-start(bf16[8,2,24,2048]{3,2,1,0:T(8,128)(2,1)} %bitcast.172), calls=%async_computation.5 | async-start | bytes 3145728 | tf_op jit(solution)/shard_map/all_to_all | solution.py:146
  167.0 23.6 %copy-start.5 = (f32[128,384]{1,0:T(8,128)S(1)}, f32[128,384]{1,0:T(8,128)}, u32[]{:S(2)}) copy-start(f32[128,384]{1,0:T(8,128)} %get-tuple-element.6) | copy-start | bytes 589828
  167.0 24.0 %copy-start.3 = (f32[128,2048]{1,0:T(8,128)S(1)}, f32[128,2048]{1,0:T(8,128)}, u32[]{:S(2)}) copy-start(f32[128,2048]{1,0:T(8,128)} %fusion.28) | copy-start | bytes 3145732
  191.0 19.7 %copy-start.1 = (bf16[704,2048]{1,0:T(8,128)(2,1)S(1)}, bf16[704,2048]{1,0:T(8,128)(2,1)}, u32[]{:S(2)}) copy-start(bf16[704,2048]{1,0:T(8,128)(2,1)} %param.33) | copy-start | bytes 8650756
  192.3 17.6 %all-to-all-start.7 = ((bf16[4,128,512]{2,1,0:T(8,128)(2,1)}), bf16[4,128,512]{2,1,0:T(8,128)(2,1)S(1)}, u32[]{:S(2)}, u32[]{:S(2)}) async-start(bf16[4,128,512]{2,1,0:T(8,128)(2,1)} %bitcast.176), calls=%async_computation.7 | async-start | bytes 1048576 | tf_op jit(solution)/shard_map/all_to_all | solution.py:175

commit v6 on v5

--- a/solution.py
+++ b/solution.py
@@ -155,7 +155,7 @@
     wd = w_down.reshape(experts_dev, groups_dev, hidden, model_width)
     gate_proj = jnp.einsum("nlsd,lgdf->lgnsf", arrived, wg, preferred_element_type=jnp.float32)
     up_proj = jnp.einsum("nlsd,lgdf->lgnsf", arrived, wu, preferred_element_type=jnp.float32)
-    hidden_act = (jax.nn.silu(gate_proj) * up_proj).astype(jnp.bfloat16)
+    hidden_act = lax.optimization_barrier((jax.nn.silu(gate_proj) * up_proj).astype(jnp.bfloat16))
     expert_out = jnp.einsum(
         "lgnsf,lgfd->nlsd", hidden_act, wd, preferred_element_type=jnp.float32
     ).astype(jnp.bfloat16)

time: 212 us -> 211 us (level)
    dot_general x0 -> x1, matrix products: none -> 8.63 us  [body(): jnp.einsum('nlsd,lgdf->lgnsf', arrived, wg, preferred_element_type=jnp.fl...]
    dot_general x1, matrix products: 15.5 us -> 6.93 us  [body(): jnp.einsum('lgnsf,lgfd->nlsd', hidden_act, wd, preferred_element_type=jnp...]
where the time goes in v6:
time: 211 us; the launch traced here: 209 us
  waiting for transfers between devices  58.1 us (28%)
  matrix products  42.7 us (20%)
  local copies, waits for them, and re-layouts  33.3 us (16%)
  starting transfers between devices  31.9 us (15%)
  blocking collectives  23.5 us (11%)
  other arithmetic  18.7 us (9%)
    all_to_all x1, blocking collectives, body(): lax.all_to_all(expert_out, 'row', 0, 0, tiled=True)  23.5 us
    all_to_all x1, waiting for transfers between devices, body(): lax.all_to_all(product.reshape(row_count, rows_here, requests, heads_here...  14 us
    all_to_all x1, waiting for transfers between devices, body(): lax.all_to_all(ffn_chunks, 'col', 0, 0, tiled=True).astype(jnp.float32)  13.4 us
    all_to_all x1, waiting for transfers between devices, body(): arrived = lax.all_to_all(outgoing, 'row', 0, 0, tiled=True)  12.7 us
    all_to_all x1, waiting for transfers between devices, body(): lax.all_to_all(jnp.broadcast_to(queries[None], (row_count,) + queries.sha...  9.38 us
    dot_general x1, matrix products, body(): jnp.einsum('nlsd,lgdf->lgnsf', arrived, wg, preferred_element_type=jnp.fl...  8.63 us
    dot_general x1, matrix products, body(): jnp.einsum('nlsd,lgdf->lgnsf', arrived, wu, preferred_element_type=jnp.fl...  7.06 us
    dot_general x1, matrix products, body(): jnp.einsum('lgnsf,lgfd->nlsd', hidden_act, wd, preferred_element_type=jnp...  6.93 us
  transfers between devices with their start and end apart: 7, of which 6 were waited for; matrix products, arithmetic and copies ran while one was open for 19% of the time, Pallas kernels for 0%

profile of v6, /device:TPU:0, one launch (start us, length us, event | category | flops | bytes accessed | tf_op | source)
XLA Modules:
  0.0 209.3 jit_solution(17692043970948548626)
XLA Ops:
  0.7 1.1 copy.85
  1.8 1.1 broadcast_in_dim.35
  2.9 5.3 %all-to-all-start = ((bf16[8,64,2,512]{3,1,2,0:T(8,128)(2,1)}), bf16[8,64,2,512]{3,1,2,0:T(8,128)(2,1)}, u32[]{:S(2)}, u32[]{:S(2)}) async-start(bf16[8,64,2,512]{3,1,2,0:T(8,128)(2,1)} %broadcast_in_dim.35), calls=%async_computation | async-start | bytes 2097152 | tf_op jit(solution)/shard_map/all_to_all | solution.py:49
  8.2 1.3 pad_maximum_fusion
  9.5 1.4 pad_maximum_fusion.1
  10.9 2.0 reshape.275
  12.9 1.0 reshape.276
  14.3 9.4 %all-to-all-done = bf16[8,64,2,512]{3,1,2,0:T(8,128)(2,1)} async-done(((bf16[8,64,2,512]{3,1,2,0:T(8,128)(2,1)}), bf16[8,64,2,512]{3,1,2,0:T(8,128)(2,1)}, u32[]{:S(2)}, u32[]{:S(2)}) %all-to-all-start) | async-done | bytes 1048608 | tf_op jit(solution)/shard_map/all_to_all | solution.py:49
  23.7 2.4 %copy.86 = bf16[8,64,2,512]{3,1,0,2:T(8,128)(2,1)} copy(bf16[8,64,2,512]{3,1,2,0:T(8,128)(2,1)} %all-to-all-done) | data formatting | bytes 2097152 | tf_op jit(solution)/shard_map/all_to_all | solution.py:49
  26.1 2.2 %reshape.250 = bf16[512,2,4,128]{3,2,0,1:T(4,128)(2,1)} reshape(bf16[8,64,2,512]{3,1,0,2:T(8,128)(2,1)} %copy.86) | data formatting | bytes 2097152 | tf_op jit(solution)/shard_map/reshape | solution.py:53
  28.2 2.0 fusion
  30.3 1.6 copy-done.4
  34.9 1.6 reshape.278
  36.5 3.3 %all-to-all-start.1 = ((f32[8,1,1024]{2,1,0:T(1,128)}), f32[8,1,1024]{2,1,0:T(1,128)S(1)}, u32[]{:S(2)}, u32[]{:S(2)}) async-start(f32[8,1,1024]{2,1,0:T(1,128)} %reshape.278), calls=%async_computation.1 | async-start | bytes 65536 | tf_op jit(solution)/shard_map/all_to_all | solution.py:80
  39.9 3.9 %fusion.24 = bf16[512,2,4,128]{0,3,2,1:T(8,128)(2,1)} fusion(f32[2,4,192,512]{3,2,1,0:T(8,128)} %copy-done.4, f32[2,4,512]{2,1,0:T(4,128)S(1)} %get-tuple-element.8, pred[2,512,192]{1,2,0:T(8,128)(4,1)S(1)} %broadcast_or_fusion, bf16[192,2,4,128]{3,2,1,0:T(4,128)(2,1)S(1)} %copy-done.7), kind=kOutput, calls=%fused_computation.31 | convolution fusion | flops 205783040 | bytes 4800512 | tf_op jit(solution)/shard_map/rhij,jrhd->irhd/dot_general | solution.py:70
  43.8 2.3 %copy.93 = bf16[512,2,4,128]{3,0,2,1:T(8,128)(2,1)} copy(bf16[512,2,4,128]{0,3,2,1:T(8,128)(2,1)} %fusion.24) | data formatting | bytes 2097152 | tf_op jit(solution)/shard_map/convert_element_type | solution.py:75
  46.1 2.4 %copy.94 = bf16[8,64,2,4,128]{4,1,3,2,0:T(8,128)(2,1)} copy(bf16[8,64,2,4,128]{4,1,0,3,2:T(8,128)(2,1)} %bitcast.161) | data formatting | bytes 2097152 | tf_op jit(solution)/shard_map/reshape | solution.py:78
  48.4 4.2 %all-to-all-start.2 = ((bf16[8,64,2,4,128]{4,1,3,2,0:T(8,128)(2,1)}), bf16[8,64,2,4,128]{4,1,3,2,0:T(8,128)(2,1)}, u32[]{:S(2)}, u32[]{:S(2)}) async-start(bf16[8,64,2,4,128]{4,1,3,2,0:T(8,128)(2,1)} %copy.94), calls=%async_computation.2 | async-start | bytes 2097152 | tf_op jit(solution)/shard_map/all_to_all | solution.py:77
  54.1 14.0 %all-to-all-done.2 = bf16[8,64,2,4,128]{4,1,3,2,0:T(8,128)(2,1)} async-done(((bf16[8,64,2,4,128]{4,1,3,2,0:T(8,128)(2,1)}), bf16[8,64,2,4,128]{4,1,3,2,0:T(8,128)(2,1)}, u32[]{:S(2)}, u32[]{:S(2)}) %all-to-all-start.2) | async-done | bytes 1048608 | tf_op jit(solution)/shard_map/all_to_all | solution.py:77
  68.1 1.8 multiply_reduce_fusion
  69.9 2.1 fusion.4
  72.5 1.1 reshape.255
  73.7 1.9 copy.96
  75.6 5.3 %all-to-all-start.3 = ((bf16[4,128,512]{2,1,0:T(8,128)(2,1)}), bf16[4,128,512]{2,1,0:T(8,128)(2,1)S(1)}, u32[]{:S(2)}, u32[]{:S(2)}) async-start(bf16[4,128,512]{2,1,0:T(8,128)(2,1)} %copy.96), calls=%async_computation.3 | async-start | bytes 1048576 | tf_op jit(solution)/shard_map/all_to_all | solution.py:103
  82.9 4.4 %reduce-window.6 = s32[64,6,128]{2,0,1:T(8,128)} reduce-window(s32[64,6,128]{2,0,1:T(8,128)} %fusion.43, s32[]{:T(128)} %constant.32.clone.1), window={size=1x1x128 pad=0_0x0_0x127_0}, to_apply=%region_6.7 | reduce-window | flops 6242304 | bytes 393220 | tf_op jit(solution)/shard_map/reduce-window
  87.3 2.0 reshape.248
  89.3 3.1 %all-to-all-done.3 = bf16[4,128,512]{2,1,0:T(8,128)(2,1)S(1)} async-done(((bf16[4,128,512]{2,1,0:T(8,128)(2,1)}), bf16[4,128,512]{2,1,0:T(8,128)(2,1)S(1)}, u32[]{:S(2)}, u32[]{:S(2)}) %all-to-all-start.3) | async-done | bytes 524320 | tf_op jit(solution)/shard_map/all_to_all | solution.py:103
  92.5 0.9 add_convert_fusion
  93.6 0.9 broadcast_in_dim.69
  94.4 3.5 %all-to-all-start.4 = ((bf16[4,128,512]{1,2,0:T(8,128)(2,1)}), bf16[4,128,512]{1,2,0:T(8,128)(2,1)S(1)}, u32[]{:S(2)}, u32[]{:S(2)}) async-start(bf16[4,128,512]{1,2,0:T(8,128)(2,1)} %broadcast_in_dim.69), calls=%async_computation.4 | async-start | bytes 1048576 | tf_op jit(solution)/shard_map/all_to_all | solution.py:109
  97.9 1.2 slice_reduce_fusion
  99.1 1.1 fusion.42
  101.0 1.6 add_select_fusion.2
  102.6 0.9 copy.102
  103.5 1.0 select_reduce_fusion
  104.5 5.5 %all-to-all-done.4 = bf16[4,128,512]{1,2,0:T(8,128)(2,1)S(1)} async-done(((bf16[4,128,512]{1,2,0:T(8,128)(2,1)}), bf16[4,128,512]{1,2,0:T(8,128)(2,1)S(1)}, u32[]{:S(2)}, u32[]{:S(2)}) %all-to-all-start.4) | async-done | bytes 524320 | tf_op jit(solution)/shard_map/all_to_all | solution.py:109
  110.8 1.4 fusion.30
  112.2 2.6 %convolution_convert_fusion = bf16[384,2048]{1,0:T(8,128)(2,1)} fusion(bf16[128,2048]{0,1:T(8,128)(2,1)S(1)} %fusion.30, bf16[128,384]{1,0:T(8,128)(2,1)} %get-tuple-element.7), kind=kOutput, calls=%fused_computation.3 | convolution fusion | flops 202113024 | bytes 2195456 | tf_op jit(solution)/shard_map/dot_general | solution.py:142
  114.8 6.8 %all-to-all-start.5 = ((bf16[8,2,24,2048]{3,2,1,0:T(8,128)(2,1)}), bf16[8,2,24,2048]{3,2,1,0:T(8,128)(2,1)}, u32[]{:S(2)}, u32[]{:S(2)}) async-start(bf16[8,2,24,2048]{3,2,1,0:T(8,128)(2,1)} %bitcast.160), calls=%async_computation.5 | async-start | bytes 3145728 | tf_op jit(solution)/shard_map/all_to_all | solution.py:146
  121.7 3.5 %fusion.65 = f32[128,704]{0,1:T(8,128)} fusion(bf16[2048,704]{0,1:T(8,128)(2,1)} %param.31, bf16[128,2048]{0,1:T(8,128)(2,1)S(1)} %fusion.30), kind=kOutput, calls=%fused_computation.114 | convolution fusion | flops 369098752 | bytes 3768320 | tf_op jit(solution)/shard_map/dot_general | solution.py:147
  125.1 5.0 %fusion.28 = f32[128,2048]{1,0:T(8,128)} fusion(bf16[704,2048]{1,0:T(8,128)(2,1)S(1)} %copy-done, bf16[2048,704]{0,1:T(8,128)(2,1)} %param.32, bf16[128,2048]{0,1:T(8,128)(2,1)S(1)} %fusion.30, f32[128,704]{0,1:T(8,128)} %fusion.65), kind=kOutput, calls=%fused_computation.37 | convolution fusion | flops 738738176 | bytes 7700480 | tf_op jit(solution)/shard_map/dot_general | solution.py:150
  130.1 12.7 %all-to-all-done.5 = bf16[8,2,24,2048]{3,2,1,0:T(8,128)(2,1)} async-done(((bf16[8,2,24,2048]{3,2,1,0:T(8,128)(2,1)}), bf16[8,2,24,2048]{3,2,1,0:T(8,128)(2,1)}, u32[]{:S(2)}, u32[]{:S(2)}) %all-to-all-start.5) | async-done | bytes 1572896 | tf_op jit(solution)/shard_map/all_to_all | solution.py:146
  142.8 7.1 %fusion.21 = f32[2,8,24,4,352]{4,2,3,1,0:T(8,128)S(1)} fusion(bf16[2,4,2048,352,1]{2,3,1,4,0:T(8,128)(2,1)} %bitcast.173, bf16[8,2,24,2048]{3,2,1,0:T(8,128)(2,1)} %all-to-all-done.5), kind=kOutput, calls=%fused_computation.28 | convolution fusion | flops 2214592512 | bytes 15269888 | tf_op jit(solution)/shard_map/nlsd,lgdf->lgnsf/dot_general | solution.py:157
  149.9 8.6 %fusion.5 = bf16[2,4,8,24,352]{4,3,1,2,0:T(8,128)(2,1)S(1)} fusion(f32[2,8,24,4,352]{4,2,3,1,0:T(8,128)S(1)} %fusion.21, bf16[2,4,2048,352,1]{2,3,1,4,0:T(8,128)(2,1)} %bitcast.174, bf16[8,2,24,2048]{3,2,1,0:T(8,128)(2,1)} %all-to-all-done.5), kind=kOutput, calls=%fused_computation.12 | convolution fusion | flops 2217836544 | bytes 16351232 | tf_op jit(solution)/shard_map/nlsd,lgdf->lgnsf/dot_general | solution.py:156
  158.5 6.9 %fusion.1 = bf16[8,2,24,2048]{3,2,0,1:T(8,128)(2,1)S(1)} fusion(bf16[2,4,8,24,352]{4,3,1,2,0:T(8,128)(2,1)S(1)} %fusion.5, bf16[2,4,352,2048,1]{3,2,1,4,0:T(8,128)(2,1)} %bitcast.159), kind=kOutput, calls=%fused_computation.5 | convolution fusion | flops 2215378944 | bytes 14188544 | tf_op jit(solution)/shard_map/lgnsf,lgfd->nlsd/dot_general | solution.py:159
  165.6 23.5 %all_to_all.40 = bf16[8,2,24,2048]{3,2,1,0:T(8,128)(2,1)S(1)} all-to-all(bf16[8,2,24,2048]{3,2,1,0:T(8,128)(2,1)S(1)} %copy.108), channel_id=1, replica_groups=mesh['row'=8,'col'=4] {'row'}, dimensions={0} | all-to-all | bytes 3145728 | tf_op jit(solution)/shard_map/all_to_all | solution.py:162
  190.9 3.5 %all-to-all-start.7 = ((bf16[4,128,512]{2,1,0:T(8,128)(2,1)}), bf16[4,128,512]{2,1,0:T(8,128)(2,1)S(1)}, u32[]{:S(2)}, u32[]{:S(2)}) async-start(bf16[4,128,512]{2,1,0:T(8,128)(2,1)} %bitcast.164), calls=%async_computation.7 | async-start | bytes 1048576 | tf_op jit(solution)/shard_map/all_to_all | solution.py:175
  195.1 13.4 %all-to-all-done.7 = bf16[4,128,512]{2,1,0:T(8,128)(2,1)S(1)} async-done(((bf16[4,128,512]{2,1,0:T(8,128)(2,1)}), bf16[4,128,512]{2,1,0:T(8,128)(2,1)S(1)}, u32[]{:S(2)}, u32[]{:S(2)}) %all-to-all-start.7) | async-done | bytes 524320 | tf_op jit(solution)/shard_map/all_to_all | solution.py:175
  (68 shorter events, 12.5 us)
Async XLA Ops:
  0.6 124.5 %copy-start = (bf16[704,2048]{1,0:T(8,128)(2,1)S(1)}, bf16[704,2048]{1,0:T(8,128)(2,1)}, u32[]{:S(2)}) copy-start(bf16[704,2048]{1,0:T(8,128)(2,1)} %param.33) | copy-start | bytes 8650756
  0.6 7.6 %copy-start.9 = (bf16[128,2,512]{2,1,0:T(2,128)(2,1)S(1)}, bf16[128,2,512]{2,1,0:T(2,128)(2,1)}, u32[]{:S(2)}) copy-start(bf16[128,2,512]{2,1,0:T(2,128)(2,1)} %param.20) | copy-start | bytes 786436
  0.7 7.6 %copy-start.11 = (bf16[64,2,512]{2,1,0:T(2,128)(2,1)S(1)}, bf16[64,2,512]{2,1,0:T(2,128)(2,1)}, u32[]{:S(2)}) copy-start(bf16[64,2,512]{2,1,0:T(2,128)(2,1)} %param.18) | copy-start | bytes 393220
  0.7 8.8 %copy-start.10 = (bf16[128,2,512]{2,1,0:T(2,128)(2,1)S(1)}, bf16[128,2,512]{2,1,0:T(2,128)(2,1)}, u32[]{:S(2)}) copy-start(bf16[128,2,512]{2,1,0:T(2,128)(2,1)} %param.21) | copy-start | bytes 786436
  2.9 11.0 %copy-start.13 = (s32[2]{0:T(128)S(1)}, s32[2]{0:T(128)}, u32[]{:S(2)}) copy-start(s32[2]{0:T(128)} %param.22) | copy-start | bytes 28
  2.9 20.8 %all-to-all-start = ((bf16[8,64,2,512]{3,1,2,0:T(8,128)(2,1)}), bf16[8,64,2,512]{3,1,2,0:T(8,128)(2,1)}, u32[]{:S(2)}, u32[]{:S(2)}) async-start(bf16[8,64,2,512]{3,1,2,0:T(8,128)(2,1)} %broadcast_in_dim.35), calls=%async_computation | async-start | bytes 2097152 | tf_op jit(solution)/shard_map/all_to_all | solution.py:49
  13.9 14.3 %copy-start.8 = (bf16[192,2,4,128]{3,2,1,0:T(4,128)(2,1)S(1)}, bf16[192,2,4,128]{3,2,1,0:T(4,128)(2,1)}, u32[]{:S(2)}) copy-start(bf16[192,2,4,128]{3,2,1,0:T(4,128)(2,1)} %reshape.275) | copy-start | bytes 1179652
  30.3 1.7 copy-start.4
  30.3 9.6 %copy-start.7 = (bf16[192,2,4,128]{3,2,1,0:T(4,128)(2,1)S(1)}, bf16[192,2,4,128]{3,2,1,0:T(4,128)(2,1)}, u32[]{:S(2)}) copy-start(bf16[192,2,4,128]{3,2,1,0:T(4,128)(2,1)} %reshape.276) | copy-start | bytes 1179652
  36.5 11.9 %all-to-all-start.1 = ((f32[8,1,1024]{2,1,0:T(1,128)}), f32[8,1,1024]{2,1,0:T(1,128)S(1)}, u32[]{:S(2)}, u32[]{:S(2)}) async-start(f32[8,1,1024]{2,1,0:T(1,128)} %reshape.278), calls=%async_computation.1 | async-start | bytes 65536 | tf_op jit(solution)/shard_map/all_to_all | solution.py:80
  48.4 19.7 %all-to-all-start.2 = ((bf16[8,64,2,4,128]{4,1,3,2,0:T(8,128)(2,1)}), bf16[8,64,2,4,128]{4,1,3,2,0:T(8,128)(2,1)}, u32[]{:S(2)}, u32[]{:S(2)}) async-start(bf16[8,64,2,4,128]{4,1,3,2,0:T(8,128)(2,1)} %copy.94), calls=%async_computation.2 | async-start | bytes 2097152 | tf_op jit(solution)/shard_map/all_to_all | solution.py:77
  71.9 8.9 %copy-start.12 = (s32[64,2,6]{0,1,2:T(2,128)S(1)}, s32[64,2,6]{0,1,2:T(2,128)}, u32[]{:S(2)}) copy-start(s32[64,2,6]{0,1,2:T(2,128)} %param.26) | copy-start | bytes 9220
  75.6 16.8 %all-to-all-start.3 = ((bf16[4,128,512]{2,1,0:T(8,128)(2,1)}), bf16[4,128,512]{2,1,0:T(8,128)(2,1)S(1)}, u32[]{:S(2)}, u32[]{:S(2)}) async-start(bf16[4,128,512]{2,1,0:T(8,128)(2,1)} %copy.96), calls=%async_computation.3 | async-start | bytes 1048576 | tf_op jit(solution)/shard_map/all_to_all | solution.py:103
  81.0 11.4 %copy-start.6 = (s32[64,2,6]{2,1,0:T(2,128)}, s32[64,2,6]{2,1,0:T(2,128)S(1)}, u32[]{:S(2)}) copy-start(s32[64,2,6]{2,1,0:T(2,128)S(1)} %copy.98) | copy-start | bytes 9220
  94.4 15.6 %all-to-all-start.4 = ((bf16[4,128,512]{1,2,0:T(8,128)(2,1)}), bf16[4,128,512]{1,2,0:T(8,128)(2,1)S(1)}, u32[]{:S(2)}, u32[]{:S(2)}) async-start(bf16[4,128,512]{1,2,0:T(8,128)(2,1)} %broadcast_in_dim.69), calls=%async_computation.4 | async-start | bytes 1048576 | tf_op jit(solution)/shard_map/all_to_all | solution.py:109
  110.0 0.8 copy-start.2
  114.8 28.0 %all-to-all-start.5 = ((bf16[8,2,24,2048]{3,2,1,0:T(8,128)(2,1)}), bf16[8,2,24,2048]{3,2,1,0:T(8,128)(2,1)}, u32[]{:S(2)}, u32[]{:S(2)}) async-start(bf16[8,2,24,2048]{3,2,1,0:T(8,128)(2,1)} %bitcast.160), calls=%async_computation.5 | async-start | bytes 3145728 | tf_op jit(solution)/shard_map/all_to_all | solution.py:146
  165.6 23.6 %copy-start.5 = (f32[128,384]{1,0:T(8,128)S(1)}, f32[128,384]{1,0:T(8,128)}, u32[]{:S(2)}) copy-start(f32[128,384]{1,0:T(8,128)} %get-tuple-element.6) | copy-start | bytes 589828
  165.6 24.0 %copy-start.3 = (f32[128,2048]{1,0:T(8,128)S(1)}, f32[128,2048]{1,0:T(8,128)}, u32[]{:S(2)}) copy-start(f32[128,2048]{1,0:T(8,128)} %fusion.28) | copy-start | bytes 3145732
  189.6 19.7 %copy-start.1 = (bf16[704,2048]{1,0:T(8,128)(2,1)S(1)}, bf16[704,2048]{1,0:T(8,128)(2,1)}, u32[]{:S(2)}) copy-start(bf16[704,2048]{1,0:T(8,128)(2,1)} %param.33) | copy-start | bytes 8650756
  190.9 17.6 %all-to-all-start.7 = ((bf16[4,128,512]{2,1,0:T(8,128)(2,1)}), bf16[4,128,512]{2,1,0:T(8,128)(2,1)S(1)}, u32[]{:S(2)}, u32[]{:S(2)}) async-start(bf16[4,128,512]{2,1,0:T(8,128)(2,1)} %bitcast.164), calls=%async_computation.7 | async-start | bytes 1048576 | tf_op jit(solution)/shard_map/all_to_all | solution.py:175

commit v7 on v6

--- a/solution.py
+++ b/solution.py
@@ -40,42 +40,54 @@
     row_index = lax.axis_index("row")
     row_count = lax.axis_size("row")
     score_scale = 1.0 / math.sqrt(HD)
-    keys_here = jnp.concatenate([cache_keys, new_keys], axis=0).reshape(
-        block_rows, requests, heads_here, HD
-    )
-    values_here = jnp.concatenate([cache_values, new_values], axis=0).reshape(
-        block_rows, requests, heads_here, HD
+    key_pad = -(-block_rows // 128) * 128
+    width_here = heads_here * HD
+    keys_here = jnp.concatenate([cache_keys, new_keys], axis=0)
+    values_here = jnp.concatenate([cache_values, new_values], axis=0)
+    head_of_lane = jnp.arange(width_here, dtype=jnp.int32) // HD
+    head_of_col = jnp.arange(heads_here * key_pad, dtype=jnp.int32) // key_pad
+    block_mask = head_of_lane[:, None] == head_of_col[None, :]
+    keys_t = jnp.pad(keys_here.transpose(1, 2, 0), ((0, 0), (0, 0), (0, key_pad - block_rows)))
+    keys_block = jnp.where(
+        block_mask[None], jnp.tile(keys_t, (1, 1, heads_here)), jnp.zeros((), keys_here.dtype)
+    )
+    values_t = jnp.pad(values_here.transpose(1, 0, 2), ((0, 0), (0, key_pad - block_rows), (0, 0)))
+    values_block = jnp.where(
+        block_mask.T[None], jnp.tile(values_t, (1, heads_here, 1)), jnp.zeros((), values_here.dtype)
     )
     all_queries = lax.all_to_all(
         jnp.broadcast_to(queries[None], (row_count,) + queries.shape), "row", 0, 0, tiled=True
     )
     query_count = row_count * rows_here
-    query_heads = all_queries.reshape(query_count, requests, heads_here, HD)
+    query_rows = all_queries.reshape(query_count, requests, width_here)
     query_pos = jnp.arange(query_count, dtype=jnp.int32)
-    offset_rows = jnp.arange(block_rows, dtype=jnp.int32)
+    offset_rows = jnp.arange(key_pad, dtype=jnp.int32)
     in_cache = offset_rows < cache_rows
+    in_block = offset_rows < block_rows
     cache_pos = row_index * cache_rows + offset_rows
     new_pos = row_index * rows_here + offset_rows - cache_rows
     cache_ok = in_cache[None, :] & (cache_pos[None, :] < cached_len[:, None])
-    new_ok = jnp.logical_not(in_cache)[None, :] & (new_pos[None, :] <= query_pos[:, None])
-    allowed = cache_ok[:, None, None, :] | new_ok[None, None, :, :]
+    new_ok = (
+        jnp.logical_not(in_cache) & in_block
+    )[None, :] & (new_pos[None, :] <= query_pos[:, None])
+    allowed = cache_ok[:, None, None, :] | new_ok[None, :, None, :]
     scores = (
-        jnp.einsum("irhd,jrhd->rhij", query_heads, keys_here, preferred_element_type=jnp.float32)
+        jnp.einsum("irk,rkc->ric", query_rows, keys_block, preferred_element_type=jnp.float32)
         * score_scale
-    )
+    ).reshape(requests, query_count, heads_here, key_pad)
     masked = jnp.where(allowed, scores, -1e30)
     block_max = jnp.max(masked, axis=-1)
     weights_now = jnp.where(allowed, jnp.exp(masked - block_max[..., None]), 0.0)
     block_sum = jnp.sum(weights_now, axis=-1)
     product = jnp.einsum(
-        "rhij,jrhd->irhd",
-        weights_now.astype(jnp.bfloat16),
-        values_here,
+        "ric,rck->irk",
+        weights_now.astype(jnp.bfloat16).reshape(requests, query_count, heads_here * key_pad),
+        values_block,
         preferred_element_type=jnp.float32,
     ).astype(jnp.bfloat16)
-    stats = jnp.stack([block_max, block_sum], axis=-1).transpose(2, 0, 1, 3)
+    stats = jnp.stack([block_max, block_sum], axis=-1).transpose(1, 0, 2, 3)
     product_back = lax.all_to_all(
-        product.reshape(row_count, rows_here, requests, heads_here, HD), "row", 0, 0, tiled=True
+        product.reshape(row_count, rows_here, requests, width_here), "row", 0, 0, tiled=True
     )
     stats_back = lax.all_to_all(
         stats.reshape(row_count, rows_here, requests, heads_here, 2), "row", 0, 0, tiled=True
@@ -84,11 +96,16 @@
     row_top = jnp.max(part_max, axis=0)
     rescale = jnp.exp(part_max - row_top[None])
     row_total = jnp.sum(rescale * stats_back[..., 1], axis=0)
-    summed = jnp.sum(rescale[..., None] * product_back.astype(jnp.float32), axis=0)
-    attended = (summed / row_total[..., None]).astype(jnp.bfloat16)
-    head_weights = out_weight.reshape(heads_here, HD, model_width)
+    lane_scale = jnp.broadcast_to(
+        rescale[..., None], rescale.shape + (HD,)
+    ).reshape(row_count, rows_here, requests, width_here)
+    summed = jnp.sum(lane_scale * product_back.astype(jnp.float32), axis=0)
+    lane_total = jnp.broadcast_to(row_total[..., None], row_total.shape + (HD,)).reshape(
+        rows_here, requests, width_here
+    )
+    attended = (summed / lane_total).astype(jnp.bfloat16)
     attn_part = jnp.einsum(
-        "irhd,hde->ire", attended, head_weights, preferred_element_type=jnp.float32
+        "irk,ke->ire", attended, out_weight, preferred_element_type=jnp.float32
     )
     col_index = lax.axis_index("col")
     col_count = lax.axis_size("col")

time: 211 us -> 202 us (0.957)
  waiting for transfers between devices: 58.1 us -> 43.5 us
  other arithmetic: 18.7 us -> 28.2 us
  matrix products: 42.7 us -> 40 us
    all_to_all x1, waiting for transfers between devices: 14 us -> 7.81 us  [body(): lax.all_to_all(product.reshape(row_count, rows_here, requests, width_here...]
    all_to_all x1, waiting for transfers between devices: 9.38 us -> 3.44 us  [body(): lax.all_to_all(jnp.broadcast_to(queries[None], (row_count,) + queries.sha...]
    transpose x1 -> x3, other arithmetic: 0.65 us -> 4.54 us  [the longest x1 2.29 us: body(): values_here.transpose(1, 0, 2)]
    all_to_all x1, waiting for transfers between devices: 5.53 us -> 2.07 us  [body(): lax.all_to_all(jnp.broadcast_to(mixed_slice[None], (col_count, token_coun...]
    select_n x0 -> x4, other arithmetic: none -> 3.32 us  [the longest x1 1.68 us: body(): jnp.where(block_mask.T[None], jnp.tile(values_t, (1, heads_here, 1)), jnp...]
    reshape x4 -> x3, local copies, waits for them, and re-layouts: 7.51 us -> 4.33 us  [the longest x1 3.11 us: body(): lane_scale = jnp.broadcast_to(rescale[..., None], rescale.shape + (HD,))....]
    concatenate x2 -> x0, other arithmetic: 2.67 us -> none  [the longest x1 1.42 us: body(): jnp.concatenate([cache_values, new_values], axis=0)]
    broadcast_in_dim x0 -> x3, local copies, waits for them, and re-layouts: none -> 2.66 us  [the longest x2 2.46 us: body(): jnp.broadcast_to(rescale[..., None], rescale.shape + (HD,))]
  transfers between devices with their start and end apart: 7 -> 7, of which waited for: 6 -> 7; matrix products, arithmetic and copies ran while one was open for 19% -> 25% of each run, Pallas kernels for 0% -> 0%
where the time goes in v7:
time: 202 us; the launch traced here: 200 us
  waiting for transfers between devices  43.5 us (22%)
  matrix products  40 us (20%)
  starting transfers between devices  32.3 us (16%)
  local copies, waits for them, and re-layouts  31.8 us (16%)
  other arithmetic  28.2 us (14%)
  blocking collectives  23.5 us (12%)
    all_to_all x1, blocking collectives, body(): lax.all_to_all(expert_out, 'row', 0, 0, tiled=True)  23.5 us
    all_to_all x1, waiting for transfers between devices, body(): lax.all_to_all(ffn_chunks, 'col', 0, 0, tiled=True).astype(jnp.float32)  13.4 us
    all_to_all x1, waiting for transfers between devices, body(): arrived = lax.all_to_all(outgoing, 'row', 0, 0, tiled=True)  12.7 us
    dot_general x1, matrix products, body(): jnp.einsum('nlsd,lgdf->lgnsf', arrived, wg, preferred_element_type=jnp.fl...  8.63 us
    all_to_all x1, waiting for transfers between devices, body(): lax.all_to_all(product.reshape(row_count, rows_here, requests, width_here...  7.81 us
    unnamed x31, local copies, waits for them, and re-layouts  7.52 us
    all_to_all x1, starting transfers between devices, body(): arrived = lax.all_to_all(outgoing, 'row', 0, 0, tiled=True)  7.1 us
    dot_general x1, matrix products, body(): jnp.einsum('nlsd,lgdf->lgnsf', arrived, wu, preferred_element_type=jnp.fl...  7.05 us
  transfers between devices with their start and end apart: 7, of which 7 were waited for; matrix products, arithmetic and copies ran while one was open for 25% of the time, Pallas kernels for 0%

profile of v7, /device:TPU:0, one launch (start us, length us, event | category | flops | bytes accessed | tf_op | source)
XLA Modules:
  0.0 200.4 jit_solution(3350363863916445739)
XLA Ops:
  0.6 1.1 copy.88
  1.7 1.1 broadcast_in_dim.111
  2.9 5.2 %all-to-all-start = ((bf16[8,64,2,512]{3,1,2,0:T(8,128)(2,1)}), bf16[8,64,2,512]{3,1,2,0:T(8,128)(2,1)}, u32[]{:S(2)}, u32[]{:S(2)}) async-start(bf16[8,64,2,512]{3,1,2,0:T(8,128)(2,1)} %broadcast_in_dim.111), calls=%async_computation | async-start | bytes 2097152 | tf_op jit(solution)/shard_map/all_to_all | solution.py:58
  8.1 1.2 broadcast_compare_fusion.1
  9.6 2.2 %maximum_bitcast_fusion = bf16[2,512,192]{1,0,2:T(2,128)(2,1)} fusion(bf16[64,2,512]{2,1,0:T(2,128)(2,1)S(1)} %copy-done.9, bf16[128,2,512]{2,1,0:T(2,128)(2,1)} %param.20), kind=kLoop, calls=%fused_computation.46 | loop fusion | flops 196608 | bytes 786432 | tf_op jit(solution)/shard_map/transpose | solution.py:50
  11.8 2.3 %maximum_bitcast_fusion.1 = bf16[2,192,512]{2,0,1:T(2,128)(2,1)} fusion(bf16[64,2,512]{2,1,0:T(2,128)(2,1)} %param.19, bf16[128,2,512]{2,1,0:T(2,128)(2,1)} %param.21), kind=kLoop, calls=%fused_computation.47 | loop fusion | flops 196608 | bytes 786432 | tf_op jit(solution)/shard_map/transpose | solution.py:54
  14.1 1.1 copy.127
  15.2 1.0 copy.128
  16.3 1.6 bitcast_select_fusion.3
  18.0 1.7 bitcast_select_fusion.2
  20.1 3.4 %all-to-all-done = bf16[8,64,2,512]{3,1,2,0:T(8,128)(2,1)} async-done(((bf16[8,64,2,512]{3,1,2,0:T(8,128)(2,1)}), bf16[8,64,2,512]{3,1,2,0:T(8,128)(2,1)}, u32[]{:S(2)}, u32[]{:S(2)}) %all-to-all-start) | async-done | bytes 1048608 | tf_op jit(solution)/shard_map/all_to_all | solution.py:58
  23.5 1.4 copy.89
  25.4 1.5 select_reduce_fusion.1
  27.0 1.1 select_reduce_fusion
  28.0 2.6 %fusion.2 = bf16[2,512,1024]{1,2,0:T(8,128)(2,1)} fusion(f32[2,1024,512]{2,1,0:T(8,128)S(1)} %get-tuple-element.9, f32[2,512,4]{1,2,0:T(4,128)S(1)} %get-tuple-element.8, pred[2,512,256]{1,2,0:T(8,128)(4,1)S(1)} %broadcast_or_fusion), kind=kLoop, calls=%fused_computation.4 | loop fusion | flops 5242880 | bytes 6569984 | tf_op jit(solution)/shard_map/convert_element_type | solution.py:84
  31.6 3.3 %all-to-all-start.1 = ((f32[8,1,1024]{2,1,0:T(1,128)}), f32[8,1,1024]{2,1,0:T(1,128)S(1)}, u32[]{:S(2)}, u32[]{:S(2)}) async-start(f32[8,1,1024]{2,1,0:T(1,128)} %reshape.370), calls=%async_computation.1 | async-start | bytes 65536 | tf_op jit(solution)/shard_map/all_to_all | solution.py:92
  34.9 3.5 %convolution_convert_fusion.2 = bf16[2,512,512]{1,2,0:T(8,128)(2,1)S(1)} fusion(bf16[2,1024,512]{2,1,0:T(8,128)(2,1)} %bitcast_select_fusion.2, bf16[2,512,1024]{1,2,0:T(8,128)(2,1)} %fusion.2), kind=kOutput, calls=%fused_computation.25 | convolution fusion | flops 1074266112 | bytes 5242880 | tf_op jit(solution)/shard_map/ric,rck->irk/dot_general | solution.py:82
  38.4 1.1 copy.95
  39.7 4.4 %all-to-all-start.2 = ((bf16[8,64,2,512]{3,1,2,0:T(8,128)(2,1)}), bf16[8,64,2,512]{3,1,2,0:T(8,128)(2,1)}, u32[]{:S(2)}, u32[]{:S(2)}) async-start(bf16[8,64,2,512]{3,1,2,0:T(8,128)(2,1)} %copy.95), calls=%async_computation.2 | async-start | bytes 2097152 | tf_op jit(solution)/shard_map/all_to_all | solution.py:89
  45.7 2.2 %broadcast_in_dim.115 = f32[8,64,2,4,128]{4,3,1,2,0:T(4,128)} broadcast(f32[8,64,2,4]{3,1,2,0:T(8,128)S(1)} %copy.92), dimensions={0,1,2,3} | broadcast | bytes 2113536 | tf_op jit(solution)/shard_map/broadcast_in_dim | solution.py:99
  48.0 3.1 %reshape.347 = f32[8,64,2,512]{3,1,2,0:T(8,128)} reshape(f32[8,64,2,4,128]{4,3,1,2,0:T(4,128)} %broadcast_in_dim.115) | data formatting | bytes 4194304 | tf_op jit(solution)/shard_map/reshape | solution.py:101
  51.5 7.8 %all-to-all-done.2 = bf16[8,64,2,512]{3,1,2,0:T(8,128)(2,1)} async-done(((bf16[8,64,2,512]{3,1,2,0:T(8,128)(2,1)}), bf16[8,64,2,512]{3,1,2,0:T(8,128)(2,1)}, u32[]{:S(2)}, u32[]{:S(2)}) %all-to-all-start.2) | async-done | bytes 1048608 | tf_op jit(solution)/shard_map/all_to_all | solution.py:89
  59.3 2.4 %multiply_reduce_fusion = f32[64,2,512]{2,0,1:T(8,128)S(1)} fusion(f32[8,64,2,512]{3,1,2,0:T(8,128)} %reshape.347, bf16[8,64,2,512]{3,1,2,0:T(8,128)(2,1)} %all-to-all-done.2), kind=kLoop, calls=%fused_computation.24 | loop fusion | flops 1507328 | bytes 3407872 | tf_op jit(solution)/shard_map/reduce_sum | solution.py:102
  62.9 1.1 reshape.350
  64.0 1.9 copy.99
  66.0 5.3 %all-to-all-start.3 = ((bf16[4,128,512]{2,1,0:T(8,128)(2,1)}), bf16[4,128,512]{2,1,0:T(8,128)(2,1)S(1)}, u32[]{:S(2)}, u32[]{:S(2)}) async-start(bf16[4,128,512]{2,1,0:T(8,128)(2,1)} %copy.99), calls=%async_computation.3 | async-start | bytes 1048576 | tf_op jit(solution)/shard_map/all_to_all | solution.py:120
  71.2 2.0 %reshape.343 = bf16[128,2048]{1,0:T(8,128)(2,1)} reshape(bf16[64,2,2048]{2,1,0:T(2,128)(2,1)} %param.23) | data formatting | bytes 1048576 | tf_op jit(solution)/shard_map/reshape | solution.py:123
  74.3 4.4 %reduce-window.6 = s32[64,6,128]{2,0,1:T(8,128)} reduce-window(s32[64,6,128]{2,0,1:T(8,128)} %fusion.26, s32[]{:T(128)} %constant.85.clone.1), window={size=1x1x128 pad=0_0x0_0x127_0}, to_apply=%region_6.7 | reduce-window | flops 6242304 | bytes 393220 | tf_op jit(solution)/shard_map/reduce-window
  78.6 4.0 %all-to-all-done.3 = bf16[4,128,512]{2,1,0:T(8,128)(2,1)S(1)} async-done(((bf16[4,128,512]{2,1,0:T(8,128)(2,1)}), bf16[4,128,512]{2,1,0:T(8,128)(2,1)S(1)}, u32[]{:S(2)}, u32[]{:S(2)}) %all-to-all-start.3) | async-done | bytes 524320 | tf_op jit(solution)/shard_map/all_to_all | solution.py:120
  84.7 3.5 %all-to-all-start.4 = ((bf16[4,128,512]{1,2,0:T(8,128)(2,1)}), bf16[4,128,512]{1,2,0:T(8,128)(2,1)S(1)}, u32[]{:S(2)}, u32[]{:S(2)}) async-start(bf16[4,128,512]{1,2,0:T(8,128)(2,1)} %broadcast_in_dim.125), calls=%async_computation.4 | async-start | bytes 1048576 | tf_op jit(solution)/shard_map/all_to_all | solution.py:126
  88.2 1.2 slice_reduce_fusion
  90.4 1.1 fusion.25
  92.2 1.6 add_select_fusion.2
  94.7 1.4 copy.106
  97.1 1.0 select_reduce_fusion.2
  98.1 2.1 %all-to-all-done.4 = bf16[4,128,512]{1,2,0:T(8,128)(2,1)S(1)} async-done(((bf16[4,128,512]{1,2,0:T(8,128)(2,1)}), bf16[4,128,512]{1,2,0:T(8,128)(2,1)S(1)}, u32[]{:S(2)}, u32[]{:S(2)}) %all-to-all-start.4) | async-done | bytes 524320 | tf_op jit(solution)/shard_map/all_to_all | solution.py:126
  100.9 1.4 fusion.17
  102.3 2.6 %convolution_convert_fusion = bf16[384,2048]{1,0:T(8,128)(2,1)} fusion(bf16[128,2048]{0,1:T(8,128)(2,1)S(1)} %fusion.17, bf16[128,384]{1,0:T(8,128)(2,1)} %get-tuple-element.7), kind=kOutput, calls=%fused_computation.8 | convolution fusion | flops 202113024 | bytes 2195456 | tf_op jit(solution)/shard_map/dot_general | solution.py:159
  105.0 7.1 %all-to-all-start.5 = ((bf16[8,2,24,2048]{3,2,1,0:T(8,128)(2,1)}), bf16[8,2,24,2048]{3,2,1,0:T(8,128)(2,1)}, u32[]{:S(2)}, u32[]{:S(2)}) async-start(bf16[8,2,24,2048]{3,2,1,0:T(8,128)(2,1)} %bitcast.175), calls=%async_computation.5 | async-start | bytes 3145728 | tf_op jit(solution)/shard_map/all_to_all | solution.py:163
  112.1 3.5 %fusion.49 = f32[128,704]{0,1:T(8,128)} fusion(bf16[2048,704]{0,1:T(8,128)(2,1)} %param.31, bf16[128,2048]{0,1:T(8,128)(2,1)S(1)} %fusion.17), kind=kOutput, calls=%fused_computation.119 | convolution fusion | flops 369098752 | bytes 3768320 | tf_op jit(solution)/shard_map/dot_general | solution.py:164
  115.5 5.0 %fusion.15 = f32[128,2048]{1,0:T(8,128)} fusion(bf16[704,2048]{1,0:T(8,128)(2,1)S(1)} %copy-done, bf16[2048,704]{0,1:T(8,128)(2,1)} %param.32, bf16[128,2048]{0,1:T(8,128)(2,1)S(1)} %fusion.17, f32[128,704]{0,1:T(8,128)} %fusion.49), kind=kOutput, calls=%fused_computation.34 | convolution fusion | flops 738738176 | bytes 7700480 | tf_op jit(solution)/shard_map/dot_general | solution.py:167
  120.5 12.7 %all-to-all-done.5 = bf16[8,2,24,2048]{3,2,1,0:T(8,128)(2,1)} async-done(((bf16[8,2,24,2048]{3,2,1,0:T(8,128)(2,1)}), bf16[8,2,24,2048]{3,2,1,0:T(8,128)(2,1)}, u32[]{:S(2)}, u32[]{:S(2)}) %all-to-all-start.5) | async-done | bytes 1572896 | tf_op jit(solution)/shard_map/all_to_all | solution.py:163
  133.2 7.1 %fusion.11 = f32[2,8,24,4,352]{4,2,3,1,0:T(8,128)S(1)} fusion(bf16[2,4,2048,352,1]{2,3,1,4,0:T(8,128)(2,1)} %bitcast.188, bf16[8,2,24,2048]{3,2,1,0:T(8,128)(2,1)} %all-to-all-done.5), kind=kOutput, calls=%fused_computation.26 | convolution fusion | flops 2214592512 | bytes 15269888 | tf_op jit(solution)/shard_map/nlsd,lgdf->lgnsf/dot_general | solution.py:174
  140.3 8.6 %fusion.6 = bf16[2,4,8,24,352]{4,3,1,2,0:T(8,128)(2,1)S(1)} fusion(f32[2,8,24,4,352]{4,2,3,1,0:T(8,128)S(1)} %fusion.11, bf16[2,4,2048,352,1]{2,3,1,4,0:T(8,128)(2,1)} %bitcast.189, bf16[8,2,24,2048]{3,2,1,0:T(8,128)(2,1)} %all-to-all-done.5), kind=kOutput, calls=%fused_computation.15 | convolution fusion | flops 2217836544 | bytes 16351232 | tf_op jit(solution)/shard_map/nlsd,lgdf->lgnsf/dot_general | solution.py:173
  148.9 6.9 %fusion.3 = bf16[8,2,24,2048]{3,2,0,1:T(8,128)(2,1)S(1)} fusion(bf16[2,4,8,24,352]{4,3,1,2,0:T(8,128)(2,1)S(1)} %fusion.6, bf16[2,4,352,2048,1]{3,2,1,4,0:T(8,128)(2,1)} %bitcast.174), kind=kOutput, calls=%fused_computation.9 | convolution fusion | flops 2215378944 | bytes 14188544 | tf_op jit(solution)/shard_map/lgnsf,lgfd->nlsd/dot_general | solution.py:176
  156.0 23.5 %all_to_all.40 = bf16[8,2,24,2048]{3,2,1,0:T(8,128)(2,1)S(1)} all-to-all(bf16[8,2,24,2048]{3,2,1,0:T(8,128)(2,1)S(1)} %copy.111), channel_id=1, replica_groups=mesh['row'=8,'col'=4] {'row'}, dimensions={0} | all-to-all | bytes 3145728 | tf_op jit(solution)/shard_map/all_to_all | solution.py:179
  182.0 3.5 %all-to-all-start.7 = ((bf16[4,128,512]{2,1,0:T(8,128)(2,1)}), bf16[4,128,512]{2,1,0:T(8,128)(2,1)S(1)}, u32[]{:S(2)}, u32[]{:S(2)}) async-start(bf16[4,128,512]{2,1,0:T(8,128)(2,1)} %bitcast.178), calls=%async_computation.7 | async-start | bytes 1048576 | tf_op jit(solution)/shard_map/all_to_all | solution.py:192
  186.2 13.4 %all-to-all-done.7 = bf16[4,128,512]{2,1,0:T(8,128)(2,1)S(1)} async-done(((bf16[4,128,512]{2,1,0:T(8,128)(2,1)}), bf16[4,128,512]{2,1,0:T(8,128)(2,1)S(1)}, u32[]{:S(2)}, u32[]{:S(2)}) %all-to-all-start.7) | async-done | bytes 524320 | tf_op jit(solution)/shard_map/all_to_all | solution.py:192
  (77 shorter events, 17.0 us)
Async XLA Ops:
  0.6 114.9 %copy-start = (bf16[704,2048]{1,0:T(8,128)(2,1)S(1)}, bf16[704,2048]{1,0:T(8,128)(2,1)}, u32[]{:S(2)}) copy-start(bf16[704,2048]{1,0:T(8,128)(2,1)} %param.33) | copy-start | bytes 8650756
  1.7 7.9 %copy-start.9 = (bf16[64,2,512]{2,1,0:T(2,128)(2,1)S(1)}, bf16[64,2,512]{2,1,0:T(2,128)(2,1)}, u32[]{:S(2)}) copy-start(bf16[64,2,512]{2,1,0:T(2,128)(2,1)} %param.18) | copy-start | bytes 393220
  2.9 20.7 %all-to-all-start = ((bf16[8,64,2,512]{3,1,2,0:T(8,128)(2,1)}), bf16[8,64,2,512]{3,1,2,0:T(8,128)(2,1)}, u32[]{:S(2)}, u32[]{:S(2)}) async-start(bf16[8,64,2,512]{3,1,2,0:T(8,128)(2,1)} %broadcast_in_dim.111), calls=%async_computation | async-start | bytes 2097152 | tf_op jit(solution)/shard_map/all_to_all | solution.py:58
  14.1 2.2 %copy-start.6 = (pred[512,1024]{0,1:T(8,128)(4,1)S(1)}, pred[512,1024]{0,1:T(8,128)(4,1)}, u32[]{:S(2)}) copy-start(pred[512,1024]{0,1:T(8,128)(4,1)} %broadcast_compare_fusion.1) | copy-start | bytes 1572868
  18.0 1.7 copy-start.11
  23.5 1.9 copy-start.2
  31.6 8.1 %all-to-all-start.1 = ((f32[8,1,1024]{2,1,0:T(1,128)}), f32[8,1,1024]{2,1,0:T(1,128)S(1)}, u32[]{:S(2)}, u32[]{:S(2)}) async-start(f32[8,1,1024]{2,1,0:T(1,128)} %reshape.370), calls=%async_computation.1 | async-start | bytes 65536 | tf_op jit(solution)/shard_map/all_to_all | solution.py:92
  39.7 19.7 %all-to-all-start.2 = ((bf16[8,64,2,512]{3,1,2,0:T(8,128)(2,1)}), bf16[8,64,2,512]{3,1,2,0:T(8,128)(2,1)}, u32[]{:S(2)}, u32[]{:S(2)}) async-start(bf16[8,64,2,512]{3,1,2,0:T(8,128)(2,1)} %copy.95), calls=%async_computation.2 | async-start | bytes 2097152 | tf_op jit(solution)/shard_map/all_to_all | solution.py:89
  59.3 2.5 %copy-start.5 = (bf16[512,2048]{1,0:T(8,128)(2,1)S(1)}, bf16[512,2048]{1,0:T(8,128)(2,1)}, u32[]{:S(2)}) copy-start(bf16[512,2048]{1,0:T(8,128)(2,1)} %param.24) | copy-start | bytes 6291460
  62.9 10.4 %copy-start.10 = (s32[64,2,6]{0,1,2:T(2,128)S(1)}, s32[64,2,6]{0,1,2:T(2,128)}, u32[]{:S(2)}) copy-start(s32[64,2,6]{0,1,2:T(2,128)} %param.26) | copy-start | bytes 9220
  66.0 16.7 %all-to-all-start.3 = ((bf16[4,128,512]{2,1,0:T(8,128)(2,1)}), bf16[4,128,512]{2,1,0:T(8,128)(2,1)S(1)}, u32[]{:S(2)}, u32[]{:S(2)}) async-start(bf16[4,128,512]{2,1,0:T(8,128)(2,1)} %copy.99), calls=%async_computation.3 | async-start | bytes 1048576 | tf_op jit(solution)/shard_map/all_to_all | solution.py:120
  73.4 9.3 %copy-start.8 = (s32[64,2,6]{2,1,0:T(2,128)}, s32[64,2,6]{2,1,0:T(2,128)S(1)}, u32[]{:S(2)}) copy-start(s32[64,2,6]{2,1,0:T(2,128)S(1)} %copy.101) | copy-start | bytes 9220
  84.7 15.5 %all-to-all-start.4 = ((bf16[4,128,512]{1,2,0:T(8,128)(2,1)}), bf16[4,128,512]{1,2,0:T(8,128)(2,1)S(1)}, u32[]{:S(2)}, u32[]{:S(2)}) async-start(bf16[4,128,512]{1,2,0:T(8,128)(2,1)} %broadcast_in_dim.125), calls=%async_computation.4 | async-start | bytes 1048576 | tf_op jit(solution)/shard_map/all_to_all | solution.py:126
  100.1 0.8 copy-start.3
  105.0 28.2 %all-to-all-start.5 = ((bf16[8,2,24,2048]{3,2,1,0:T(8,128)(2,1)}), bf16[8,2,24,2048]{3,2,1,0:T(8,128)(2,1)}, u32[]{:S(2)}, u32[]{:S(2)}) async-start(bf16[8,2,24,2048]{3,2,1,0:T(8,128)(2,1)} %bitcast.175), calls=%async_computation.5 | async-start | bytes 3145728 | tf_op jit(solution)/shard_map/all_to_all | solution.py:163
  156.0 23.6 %copy-start.7 = (f32[128,384]{1,0:T(8,128)S(1)}, f32[128,384]{1,0:T(8,128)}, u32[]{:S(2)}) copy-start(f32[128,384]{1,0:T(8,128)} %get-tuple-element.6) | copy-start | bytes 589828
  179.5 1.2 copy-start.4
  180.7 19.6 %copy-start.1 = (bf16[704,2048]{1,0:T(8,128)(2,1)S(1)}, bf16[704,2048]{1,0:T(8,128)(2,1)}, u32[]{:S(2)}) copy-start(bf16[704,2048]{1,0:T(8,128)(2,1)} %param.33) | copy-start | bytes 8650756
  182.0 17.6 %all-to-all-start.7 = ((bf16[4,128,512]{2,1,0:T(8,128)(2,1)}), bf16[4,128,512]{2,1,0:T(8,128)(2,1)S(1)}, u32[]{:S(2)}, u32[]{:S(2)}) async-start(bf16[4,128,512]{2,1,0:T(8,128)(2,1)} %bitcast.178), calls=%async_computation.7 | async-start | bytes 1048576 | tf_op jit(solution)/shard_map/all_to_all | solution.py:192

commit v8 on v7

--- a/solution.py
+++ b/solution.py
@@ -104,18 +104,16 @@
         rows_here, requests, width_here
     )
     attended = (summed / lane_total).astype(jnp.bfloat16)
-    attn_part = jnp.einsum(
-        "irk,ke->ire", attended, out_weight, preferred_element_type=jnp.float32
-    )
     col_index = lax.axis_index("col")
     col_count = lax.axis_size("col")
     col_width = model_width // col_count
     token_count = rows_here * requests
-    attn_chunks = (
-        attn_part.astype(jnp.bfloat16)
-        .reshape(token_count, col_count, col_width)
-        .transpose(1, 0, 2)
-    )
+    attn_chunks = jnp.einsum(
+        "tk,kcw->ctw",
+        attended.reshape(token_count, width_here),
+        out_weight.reshape(width_here, col_count, col_width),
+        preferred_element_type=jnp.float32,
+    ).astype(jnp.bfloat16)
     attn_summed = jnp.sum(
         lax.all_to_all(attn_chunks, "col", 0, 0, tiled=True).astype(jnp.float32), axis=0
     )

time: 202 us -> 201 us (level)
  local copies, waits for them, and re-layouts: 31.8 us -> 28.2 us
  matrix products: 40 us -> 42.4 us
    dot_general x1, matrix products: 0.45 us -> 2.83 us  [body(): jnp.einsum('tk,kcw->ctw', attended.reshape(token_count, width_here), out_...]
    unnamed x31 -> x29, local copies, waits for them, and re-layouts: 7.52 us -> 7.35 us
where the time goes in v8:
time: 201 us; the launch traced here: 199 us
  waiting for transfers between devices  43.9 us (22%)
  matrix products  42.4 us (21%)
  starting transfers between devices  31.9 us (16%)
  local copies, waits for them, and re-layouts  28.2 us (14%)
  other arithmetic  28.1 us (14%)
  blocking collectives  23.5 us (12%)
    all_to_all x1, blocking collectives, body(): lax.all_to_all(expert_out, 'row', 0, 0, tiled=True)  23.5 us
    all_to_all x1, waiting for transfers between devices, body(): lax.all_to_all(ffn_chunks, 'col', 0, 0, tiled=True).astype(jnp.float32)  13.4 us
    all_to_all x1, waiting for transfers between devices, body(): arrived = lax.all_to_all(outgoing, 'row', 0, 0, tiled=True)  12.7 us
    dot_general x1, matrix products, body(): jnp.einsum('nlsd,lgdf->lgnsf', arrived, wg, preferred_element_type=jnp.fl...  8.63 us
    all_to_all x1, waiting for transfers between devices, body(): lax.all_to_all(product.reshape(row_count, rows_here, requests, width_here...  7.99 us
    unnamed x29, local copies, waits for them, and re-layouts  7.35 us
    dot_general x1, matrix products, body(): jnp.einsum('nlsd,lgdf->lgnsf', arrived, wu, preferred_element_type=jnp.fl...  7.06 us
    dot_general x1, matrix products, body(): jnp.einsum('lgnsf,lgfd->nlsd', hidden_act, wd, preferred_element_type=jnp...  6.93 us
  transfers between devices with their start and end apart: 7, of which 7 were waited for; matrix products, arithmetic and copies ran while one was open for 25% of the time, Pallas kernels for 0%

profile of v8, /device:TPU:0, one launch (start us, length us, event | category | flops | bytes accessed | tf_op | source)
XLA Modules:
  0.0 199.1 jit_solution(18252322113991907537)
XLA Ops:
  0.6 1.1 copy.88
  1.7 1.1 broadcast_in_dim.111
  2.9 5.2 %all-to-all-start = ((bf16[8,64,2,512]{3,1,2,0:T(8,128)(2,1)}), bf16[8,64,2,512]{3,1,2,0:T(8,128)(2,1)}, u32[]{:S(2)}, u32[]{:S(2)}) async-start(bf16[8,64,2,512]{3,1,2,0:T(8,128)(2,1)} %broadcast_in_dim.111), calls=%async_computation | async-start | bytes 2097152 | tf_op jit(solution)/shard_map/all_to_all | solution.py:58
  8.1 1.2 broadcast_compare_fusion.1
  9.6 2.2 %maximum_bitcast_fusion = bf16[2,512,192]{1,0,2:T(2,128)(2,1)} fusion(bf16[64,2,512]{2,1,0:T(2,128)(2,1)S(1)} %copy-done.8, bf16[128,2,512]{2,1,0:T(2,128)(2,1)} %param.20), kind=kLoop, calls=%fused_computation.49 | loop fusion | flops 196608 | bytes 786432 | tf_op jit(solution)/shard_map/transpose | solution.py:50
  11.8 2.3 %maximum_bitcast_fusion.1 = bf16[2,192,512]{2,0,1:T(2,128)(2,1)} fusion(bf16[64,2,512]{2,1,0:T(2,128)(2,1)} %param.19, bf16[128,2,512]{2,1,0:T(2,128)(2,1)} %param.21), kind=kLoop, calls=%fused_computation.50 | loop fusion | flops 196608 | bytes 786432 | tf_op jit(solution)/shard_map/transpose | solution.py:54
  14.1 1.1 copy.127
  15.2 1.0 copy.128
  16.3 1.6 bitcast_select_fusion.3
  18.0 1.7 bitcast_select_fusion.2
  20.1 3.4 %all-to-all-done = bf16[8,64,2,512]{3,1,2,0:T(8,128)(2,1)} async-done(((bf16[8,64,2,512]{3,1,2,0:T(8,128)(2,1)}), bf16[8,64,2,512]{3,1,2,0:T(8,128)(2,1)}, u32[]{:S(2)}, u32[]{:S(2)}) %all-to-all-start) | async-done | bytes 1048608 | tf_op jit(solution)/shard_map/all_to_all | solution.py:58
  23.5 1.4 copy.89
  25.4 1.5 select_reduce_fusion.1
  27.0 1.1 select_reduce_fusion
  28.0 2.6 %fusion.2 = bf16[2,512,1024]{1,2,0:T(8,128)(2,1)} fusion(f32[2,1024,512]{2,1,0:T(8,128)S(1)} %get-tuple-element.9, f32[2,512,4]{1,2,0:T(4,128)S(1)} %get-tuple-element.8, pred[2,512,256]{1,2,0:T(8,128)(4,1)S(1)} %broadcast_or_fusion), kind=kLoop, calls=%fused_computation.4 | loop fusion | flops 5242880 | bytes 6569984 | tf_op jit(solution)/shard_map/convert_element_type | solution.py:84
  31.6 3.3 %all-to-all-start.1 = ((f32[8,1,1024]{2,1,0:T(1,128)}), f32[8,1,1024]{2,1,0:T(1,128)S(1)}, u32[]{:S(2)}, u32[]{:S(2)}) async-start(f32[8,1,1024]{2,1,0:T(1,128)} %reshape.388), calls=%async_computation.1 | async-start | bytes 65536 | tf_op jit(solution)/shard_map/all_to_all | solution.py:92
  34.9 3.5 %convolution_convert_fusion.1 = bf16[2,512,512]{1,2,0:T(8,128)(2,1)S(1)} fusion(bf16[2,1024,512]{2,1,0:T(8,128)(2,1)} %bitcast_select_fusion.2, bf16[2,512,1024]{1,2,0:T(8,128)(2,1)} %fusion.2), kind=kOutput, calls=%fused_computation.26 | convolution fusion | flops 1074266112 | bytes 5242880 | tf_op jit(solution)/shard_map/ric,rck->irk/dot_general | solution.py:82
  38.4 1.1 copy.95
  39.7 4.2 %all-to-all-start.2 = ((bf16[8,64,2,512]{3,1,2,0:T(8,128)(2,1)}), bf16[8,64,2,512]{3,1,2,0:T(8,128)(2,1)}, u32[]{:S(2)}, u32[]{:S(2)}) async-start(bf16[8,64,2,512]{3,1,2,0:T(8,128)(2,1)} %copy.95), calls=%async_computation.2 | async-start | bytes 2097152 | tf_op jit(solution)/shard_map/all_to_all | solution.py:89
  45.6 2.2 %broadcast_in_dim.115 = f32[8,64,2,4,128]{4,3,1,2,0:T(4,128)} broadcast(f32[8,64,2,4]{3,1,2,0:T(8,128)S(1)} %copy.92), dimensions={0,1,2,3} | broadcast | bytes 2113536 | tf_op jit(solution)/shard_map/broadcast_in_dim | solution.py:99
  47.8 3.1 %reshape.364 = f32[8,64,2,512]{3,1,2,0:T(8,128)} reshape(f32[8,64,2,4,128]{4,3,1,2,0:T(4,128)} %broadcast_in_dim.115) | data formatting | bytes 4194304 | tf_op jit(solution)/shard_map/reshape | solution.py:101
  51.3 8.0 %all-to-all-done.2 = bf16[8,64,2,512]{3,1,2,0:T(8,128)(2,1)} async-done(((bf16[8,64,2,512]{3,1,2,0:T(8,128)(2,1)}), bf16[8,64,2,512]{3,1,2,0:T(8,128)(2,1)}, u32[]{:S(2)}, u32[]{:S(2)}) %all-to-all-start.2) | async-done | bytes 1048608 | tf_op jit(solution)/shard_map/all_to_all | solution.py:89
  59.3 2.2 %multiply_reduce_fusion = f32[64,2,512]{2,0,1:T(8,128)S(1)} fusion(f32[8,64,2,512]{3,1,2,0:T(8,128)} %reshape.364, bf16[8,64,2,512]{3,1,2,0:T(8,128)(2,1)} %all-to-all-done.2), kind=kLoop, calls=%fused_computation.25 | loop fusion | flops 1507328 | bytes 3407872 | tf_op jit(solution)/shard_map/reduce_sum | solution.py:102
  61.8 2.8 %fusion.19 = bf16[4,128,512]{2,1,0:T(8,128)(2,1)} fusion(bf16[128,512,1]{1,0,2:T(8,128)(2,1)S(1)} %reshape.379, bf16[64,4,8,512]{3,2,1,0:T(8,128)(2,1)} %bitcast.196), kind=kOutput, calls=%fused_computation.31 | convolution fusion | flops 268697600 | bytes 2752512 | tf_op jit(solution)/shard_map/tk,kcw->ctw/dot_general | solution.py:111
  64.7 5.3 %all-to-all-start.3 = ((bf16[4,128,512]{2,1,0:T(8,128)(2,1)}), bf16[4,128,512]{2,1,0:T(8,128)(2,1)S(1)}, u32[]{:S(2)}, u32[]{:S(2)}) async-start(bf16[4,128,512]{2,1,0:T(8,128)(2,1)} %fusion.19), calls=%async_computation.3 | async-start | bytes 1048576 | tf_op jit(solution)/shard_map/all_to_all | solution.py:118
  70.0 2.0 %reshape.360 = bf16[128,2048]{1,0:T(8,128)(2,1)} reshape(bf16[64,2,2048]{2,1,0:T(2,128)(2,1)} %param.23) | data formatting | bytes 1048576 | tf_op jit(solution)/shard_map/reshape | solution.py:121
  73.0 4.4 %reduce-window.6 = s32[64,6,128]{2,0,1:T(8,128)} reduce-window(s32[64,6,128]{2,0,1:T(8,128)} %fusion.34, s32[]{:T(128)} %constant.85.clone.1), window={size=1x1x128 pad=0_0x0_0x127_0}, to_apply=%region_6.7 | reduce-window | flops 6242304 | bytes 393220 | tf_op jit(solution)/shard_map/reduce-window
  77.4 4.1 %all-to-all-done.3 = bf16[4,128,512]{2,1,0:T(8,128)(2,1)S(1)} async-done(((bf16[4,128,512]{2,1,0:T(8,128)(2,1)}), bf16[4,128,512]{2,1,0:T(8,128)(2,1)S(1)}, u32[]{:S(2)}, u32[]{:S(2)}) %all-to-all-start.3) | async-done | bytes 524320 | tf_op jit(solution)/shard_map/all_to_all | solution.py:118
  83.5 3.5 %all-to-all-start.4 = ((bf16[4,128,512]{1,2,0:T(8,128)(2,1)}), bf16[4,128,512]{1,2,0:T(8,128)(2,1)S(1)}, u32[]{:S(2)}, u32[]{:S(2)}) async-start(bf16[4,128,512]{1,2,0:T(8,128)(2,1)} %broadcast_in_dim.125), calls=%async_computation.4 | async-start | bytes 1048576 | tf_op jit(solution)/shard_map/all_to_all | solution.py:124
  87.0 1.2 slice_reduce_fusion
  88.2 1.0 eq.72
  89.2 1.1 fusion.33
  91.0 1.6 add_select_fusion.2
  93.5 1.4 copy.106
  95.9 1.0 select_reduce_fusion.2
  96.9 2.2 %all-to-all-done.4 = bf16[4,128,512]{1,2,0:T(8,128)(2,1)S(1)} async-done(((bf16[4,128,512]{1,2,0:T(8,128)(2,1)}), bf16[4,128,512]{1,2,0:T(8,128)(2,1)S(1)}, u32[]{:S(2)}, u32[]{:S(2)}) %all-to-all-start.4) | async-done | bytes 524320 | tf_op jit(solution)/shard_map/all_to_all | solution.py:124
  99.8 1.4 fusion.25
  101.2 2.6 %convolution_convert_fusion = bf16[384,2048]{1,0:T(8,128)(2,1)} fusion(bf16[128,2048]{0,1:T(8,128)(2,1)S(1)} %fusion.25, bf16[128,384]{1,0:T(8,128)(2,1)} %get-tuple-element.7), kind=kOutput, calls=%fused_computation.8 | convolution fusion | flops 202113024 | bytes 2195456 | tf_op jit(solution)/shard_map/dot_general | solution.py:157
  103.9 6.9 %all-to-all-start.5 = ((bf16[8,2,24,2048]{3,2,1,0:T(8,128)(2,1)}), bf16[8,2,24,2048]{3,2,1,0:T(8,128)(2,1)}, u32[]{:S(2)}, u32[]{:S(2)}) async-start(bf16[8,2,24,2048]{3,2,1,0:T(8,128)(2,1)} %bitcast.182), calls=%async_computation.5 | async-start | bytes 3145728 | tf_op jit(solution)/shard_map/all_to_all | solution.py:161
  110.8 3.5 %fusion.57 = f32[128,704]{0,1:T(8,128)} fusion(bf16[2048,704]{0,1:T(8,128)(2,1)} %param.31, bf16[128,2048]{0,1:T(8,128)(2,1)S(1)} %fusion.25), kind=kOutput, calls=%fused_computation.122 | convolution fusion | flops 369098752 | bytes 3768320 | tf_op jit(solution)/shard_map/dot_general | solution.py:162
  114.2 5.0 %fusion.23 = f32[128,2048]{1,0:T(8,128)} fusion(bf16[704,2048]{1,0:T(8,128)(2,1)S(1)} %copy-done, bf16[2048,704]{0,1:T(8,128)(2,1)} %param.32, bf16[128,2048]{0,1:T(8,128)(2,1)S(1)} %fusion.25, f32[128,704]{0,1:T(8,128)} %fusion.57), kind=kOutput, calls=%fused_computation.37 | convolution fusion | flops 738738176 | bytes 7700480 | tf_op jit(solution)/shard_map/dot_general | solution.py:165
  119.2 12.7 %all-to-all-done.5 = bf16[8,2,24,2048]{3,2,1,0:T(8,128)(2,1)} async-done(((bf16[8,2,24,2048]{3,2,1,0:T(8,128)(2,1)}), bf16[8,2,24,2048]{3,2,1,0:T(8,128)(2,1)}, u32[]{:S(2)}, u32[]{:S(2)}) %all-to-all-start.5) | async-done | bytes 1572896 | tf_op jit(solution)/shard_map/all_to_all | solution.py:161
  131.9 7.1 %fusion.13 = f32[2,8,24,4,352]{4,2,3,1,0:T(8,128)S(1)} fusion(bf16[2,4,2048,352,1]{2,3,1,4,0:T(8,128)(2,1)} %bitcast.194, bf16[8,2,24,2048]{3,2,1,0:T(8,128)(2,1)} %all-to-all-done.5), kind=kOutput, calls=%fused_computation.27 | convolution fusion | flops 2214592512 | bytes 15269888 | tf_op jit(solution)/shard_map/nlsd,lgdf->lgnsf/dot_general | solution.py:172
  139.0 8.6 %fusion.6 = bf16[2,4,8,24,352]{4,3,1,2,0:T(8,128)(2,1)S(1)} fusion(f32[2,8,24,4,352]{4,2,3,1,0:T(8,128)S(1)} %fusion.13, bf16[2,4,2048,352,1]{2,3,1,4,0:T(8,128)(2,1)} %bitcast.195, bf16[8,2,24,2048]{3,2,1,0:T(8,128)(2,1)} %all-to-all-done.5), kind=kOutput, calls=%fused_computation.14 | convolution fusion | flops 2217836544 | bytes 16351232 | tf_op jit(solution)/shard_map/nlsd,lgdf->lgnsf/dot_general | solution.py:171
  147.6 6.9 %fusion.3 = bf16[8,2,24,2048]{3,2,0,1:T(8,128)(2,1)S(1)} fusion(bf16[2,4,8,24,352]{4,3,1,2,0:T(8,128)(2,1)S(1)} %fusion.6, bf16[2,4,352,2048,1]{3,2,1,4,0:T(8,128)(2,1)} %bitcast.181), kind=kOutput, calls=%fused_computation.9 | convolution fusion | flops 2215378944 | bytes 14188544 | tf_op jit(solution)/shard_map/lgnsf,lgfd->nlsd/dot_general | solution.py:174
  154.7 23.5 %all_to_all.40 = bf16[8,2,24,2048]{3,2,1,0:T(8,128)(2,1)S(1)} all-to-all(bf16[8,2,24,2048]{3,2,1,0:T(8,128)(2,1)S(1)} %copy.111), channel_id=1, replica_groups=mesh['row'=8,'col'=4] {'row'}, dimensions={0} | all-to-all | bytes 3145728 | tf_op jit(solution)/shard_map/all_to_all | solution.py:177
  180.7 3.5 %all-to-all-start.7 = ((bf16[4,128,512]{2,1,0:T(8,128)(2,1)}), bf16[4,128,512]{2,1,0:T(8,128)(2,1)S(1)}, u32[]{:S(2)}, u32[]{:S(2)}) async-start(bf16[4,128,512]{2,1,0:T(8,128)(2,1)} %bitcast.185), calls=%async_computation.7 | async-start | bytes 1048576 | tf_op jit(solution)/shard_map/all_to_all | solution.py:190
  184.9 13.4 %all-to-all-done.7 = bf16[4,128,512]{2,1,0:T(8,128)(2,1)S(1)} async-done(((bf16[4,128,512]{2,1,0:T(8,128)(2,1)}), bf16[4,128,512]{2,1,0:T(8,128)(2,1)S(1)}, u32[]{:S(2)}, u32[]{:S(2)}) %all-to-all-start.7) | async-done | bytes 524320 | tf_op jit(solution)/shard_map/all_to_all | solution.py:190
  (75 shorter events, 15.1 us)
Async XLA Ops:
  0.6 113.6 %copy-start = (bf16[704,2048]{1,0:T(8,128)(2,1)S(1)}, bf16[704,2048]{1,0:T(8,128)(2,1)}, u32[]{:S(2)}) copy-start(bf16[704,2048]{1,0:T(8,128)(2,1)} %param.33) | copy-start | bytes 8650756
  1.7 7.9 %copy-start.8 = (bf16[64,2,512]{2,1,0:T(2,128)(2,1)S(1)}, bf16[64,2,512]{2,1,0:T(2,128)(2,1)}, u32[]{:S(2)}) copy-start(bf16[64,2,512]{2,1,0:T(2,128)(2,1)} %param.18) | copy-start | bytes 393220
  2.9 20.7 %all-to-all-start = ((bf16[8,64,2,512]{3,1,2,0:T(8,128)(2,1)}), bf16[8,64,2,512]{3,1,2,0:T(8,128)(2,1)}, u32[]{:S(2)}, u32[]{:S(2)}) async-start(bf16[8,64,2,512]{3,1,2,0:T(8,128)(2,1)} %broadcast_in_dim.111), calls=%async_computation | async-start | bytes 2097152 | tf_op jit(solution)/shard_map/all_to_all | solution.py:58
  14.1 2.2 %copy-start.5 = (pred[512,1024]{0,1:T(8,128)(4,1)S(1)}, pred[512,1024]{0,1:T(8,128)(4,1)}, u32[]{:S(2)}) copy-start(pred[512,1024]{0,1:T(8,128)(4,1)} %broadcast_compare_fusion.1) | copy-start | bytes 1572868
  18.0 1.7 copy-start.10
  23.5 1.9 copy-start.2
  31.6 8.1 %all-to-all-start.1 = ((f32[8,1,1024]{2,1,0:T(1,128)}), f32[8,1,1024]{2,1,0:T(1,128)S(1)}, u32[]{:S(2)}, u32[]{:S(2)}) async-start(f32[8,1,1024]{2,1,0:T(1,128)} %reshape.388), calls=%async_computation.1 | async-start | bytes 65536 | tf_op jit(solution)/shard_map/all_to_all | solution.py:92
  39.7 19.7 %all-to-all-start.2 = ((bf16[8,64,2,512]{3,1,2,0:T(8,128)(2,1)}), bf16[8,64,2,512]{3,1,2,0:T(8,128)(2,1)}, u32[]{:S(2)}, u32[]{:S(2)}) async-start(bf16[8,64,2,512]{3,1,2,0:T(8,128)(2,1)} %copy.95), calls=%async_computation.2 | async-start | bytes 2097152 | tf_op jit(solution)/shard_map/all_to_all | solution.py:89
  61.8 10.2 %copy-start.9 = (s32[64,2,6]{0,1,2:T(2,128)S(1)}, s32[64,2,6]{0,1,2:T(2,128)}, u32[]{:S(2)}) copy-start(s32[64,2,6]{0,1,2:T(2,128)} %param.26) | copy-start | bytes 9220
  64.7 16.8 %all-to-all-start.3 = ((bf16[4,128,512]{2,1,0:T(8,128)(2,1)}), bf16[4,128,512]{2,1,0:T(8,128)(2,1)S(1)}, u32[]{:S(2)}, u32[]{:S(2)}) async-start(bf16[4,128,512]{2,1,0:T(8,128)(2,1)} %fusion.19), calls=%async_computation.3 | async-start | bytes 1048576 | tf_op jit(solution)/shard_map/all_to_all | solution.py:118
  72.1 9.4 %copy-start.7 = (s32[64,2,6]{2,1,0:T(2,128)}, s32[64,2,6]{2,1,0:T(2,128)S(1)}, u32[]{:S(2)}) copy-start(s32[64,2,6]{2,1,0:T(2,128)S(1)} %copy.101) | copy-start | bytes 9220
  83.5 15.6 %all-to-all-start.4 = ((bf16[4,128,512]{1,2,0:T(8,128)(2,1)}), bf16[4,128,512]{1,2,0:T(8,128)(2,1)S(1)}, u32[]{:S(2)}, u32[]{:S(2)}) async-start(bf16[4,128,512]{1,2,0:T(8,128)(2,1)} %broadcast_in_dim.125), calls=%async_computation.4 | async-start | bytes 1048576 | tf_op jit(solution)/shard_map/all_to_all | solution.py:124
  99.1 0.8 copy-start.3
  103.9 28.0 %all-to-all-start.5 = ((bf16[8,2,24,2048]{3,2,1,0:T(8,128)(2,1)}), bf16[8,2,24,2048]{3,2,1,0:T(8,128)(2,1)}, u32[]{:S(2)}, u32[]{:S(2)}) async-start(bf16[8,2,24,2048]{3,2,1,0:T(8,128)(2,1)} %bitcast.182), calls=%async_computation.5 | async-start | bytes 3145728 | tf_op jit(solution)/shard_map/all_to_all | solution.py:161
  154.7 23.6 %copy-start.6 = (f32[128,384]{1,0:T(8,128)S(1)}, f32[128,384]{1,0:T(8,128)}, u32[]{:S(2)}) copy-start(f32[128,384]{1,0:T(8,128)} %get-tuple-element.6) | copy-start | bytes 589828
  178.2 1.2 copy-start.4
  179.4 19.6 %copy-start.1 = (bf16[704,2048]{1,0:T(8,128)(2,1)S(1)}, bf16[704,2048]{1,0:T(8,128)(2,1)}, u32[]{:S(2)}) copy-start(bf16[704,2048]{1,0:T(8,128)(2,1)} %param.33) | copy-start | bytes 8650756
  180.7 17.6 %all-to-all-start.7 = ((bf16[4,128,512]{2,1,0:T(8,128)(2,1)}), bf16[4,128,512]{2,1,0:T(8,128)(2,1)S(1)}, u32[]{:S(2)}, u32[]{:S(2)}) async-start(bf16[4,128,512]{2,1,0:T(8,128)(2,1)} %bitcast.185), calls=%async_computation.7 | async-start | bytes 1048576 | tf_op jit(solution)/shard_map/all_to_all | solution.py:190

commit v9 on v8

--- a/solution.py
+++ b/solution.py
@@ -168,18 +168,32 @@
     wg = w_gate.reshape(experts_dev, groups_dev, model_width, hidden)
     wu = w_up.reshape(experts_dev, groups_dev, model_width, hidden)
     wd = w_down.reshape(experts_dev, groups_dev, hidden, model_width)
-    gate_proj = jnp.einsum("nlsd,lgdf->lgnsf", arrived, wg, preferred_element_type=jnp.float32)
-    up_proj = jnp.einsum("nlsd,lgdf->lgnsf", arrived, wu, preferred_element_type=jnp.float32)
-    hidden_act = lax.optimization_barrier((jax.nn.silu(gate_proj) * up_proj).astype(jnp.bfloat16))
-    expert_out = jnp.einsum(
-        "lgnsf,lgfd->nlsd", hidden_act, wd, preferred_element_type=jnp.float32
-    ).astype(jnp.bfloat16)
-    returned = lax.all_to_all(expert_out, "row", 0, 0, tiled=True).reshape(slots, model_width)
-    combine_hi = combine.astype(jnp.bfloat16)
-    combine_lo = (combine - combine_hi.astype(jnp.float32)).astype(jnp.bfloat16)
-    routed = jnp.dot(combine_hi, returned, preferred_element_type=jnp.float32) + jnp.dot(
-        combine_lo, returned, preferred_element_type=jnp.float32
-    )
+    combine_hi = combine.astype(jnp.bfloat16).reshape(token_count, row_count, experts_dev, CAP)
+    combine_lo = (combine - combine_hi.reshape(token_count, slots).astype(jnp.float32)).astype(
+        jnp.bfloat16
+    ).reshape(token_count, row_count, experts_dev, CAP)
+    routed = jnp.zeros((token_count, model_width), jnp.float32)
+    for chunk in range(experts_dev):
+        rows_in = arrived[:, chunk].reshape(row_count * CAP, model_width)
+        gate_proj = jnp.einsum(
+            "td,gdf->gtf", rows_in, wg[chunk], preferred_element_type=jnp.float32
+        )
+        up_proj = jnp.einsum("td,gdf->gtf", rows_in, wu[chunk], preferred_element_type=jnp.float32)
+        hidden_act = lax.optimization_barrier(
+            (jax.nn.silu(gate_proj) * up_proj).astype(jnp.bfloat16)
+        )
+        expert_out = jnp.einsum(
+            "gtf,gfd->td", hidden_act, wd[chunk], preferred_element_type=jnp.float32
+        ).astype(jnp.bfloat16)
+        returned = lax.all_to_all(
+            expert_out.reshape(row_count, CAP, model_width), "row", 0, 0, tiled=True
+        ).reshape(row_count * CAP, model_width)
+        pick_hi = combine_hi[:, :, chunk].reshape(token_count, row_count * CAP)
+        pick_lo = combine_lo[:, :, chunk].reshape(token_count, row_count * CAP)
+        routed = routed + (
+            jnp.dot(pick_hi, returned, preferred_element_type=jnp.float32)
+            + jnp.dot(pick_lo, returned, preferred_element_type=jnp.float32)
+        )
     ffn_chunks = (
         (routed + shared_part)
         .astype(jnp.bfloat16)

time: 201 us -> 199 us (0.990)
  blocking collectives: 23.5 us -> 0 us
  waiting for transfers between devices: 43.9 us -> 51.6 us
  starting transfers between devices: 31.9 us -> 39.2 us
  local copies, waits for them, and re-layouts: 28.2 us -> 31.8 us
  matrix products: 42.4 us -> 44.9 us
    all_to_all x1 -> x0, blocking collectives: 23.5 us -> none  [body(): lax.all_to_all(expert_out, 'row', 0, 0, tiled=True)]
    all_to_all x0 -> x2, waiting for transfers between devices: none -> 11.5 us  [body(): lax.all_to_all(expert_out.reshape(row_count, CAP, model_width), 'row', 0,...]
    all_to_all x0 -> x2, starting transfers between devices: none -> 7.34 us  [body(): lax.all_to_all(expert_out.reshape(row_count, CAP, model_width), 'row', 0,...]
    dot_general x5 -> x10, matrix products: 23.5 us -> 26 us  [the longest x2 9.57 us: body(): jnp.einsum('td,gdf->gtf', rows_in, wu[chunk], preferred_element_type=jnp....]
    all_to_all x1, waiting for transfers between devices: 13.4 us -> 11.2 us  [body(): lax.all_to_all(ffn_chunks, 'col', 0, 0, tiled=True).astype(jnp.float32)]
    unnamed x29 -> x47, local copies, waits for them, and re-layouts: 7.35 us -> 7.77 us
  transfers between devices with their start and end apart: 7 -> 9, of which waited for: 7 -> 9; matrix products, arithmetic and copies ran while one was open for 25% -> 33% of each run, Pallas kernels for 0% -> 0%
where the time goes in v9:
time: 199 us; the launch traced here: 197 us
  waiting for transfers between devices  51.6 us (26%)
  matrix products  44.9 us (23%)
  starting transfers between devices  39.2 us (20%)
  local copies, waits for them, and re-layouts  31.8 us (16%)
  other arithmetic  28.1 us (14%)
    all_to_all x2, waiting for transfers between devices, body(): lax.all_to_all(expert_out.reshape(row_count, CAP, model_width), 'row', 0,...  11.5 us
    all_to_all x1, waiting for transfers between devices, body(): lax.all_to_all(ffn_chunks, 'col', 0, 0, tiled=True).astype(jnp.float32)  11.2 us
    all_to_all x1, waiting for transfers between devices, body(): arrived = lax.all_to_all(outgoing, 'row', 0, 0, tiled=True)  11 us
    dot_general x2, matrix products, body(): jnp.einsum('td,gdf->gtf', rows_in, wu[chunk], preferred_element_type=jnp....  9.57 us
    dot_general x2, matrix products, body(): jnp.einsum('td,gdf->gtf', rows_in, wg[chunk], preferred_element_type=jnp....  9.53 us
    all_to_all x1, waiting for transfers between devices, body(): lax.all_to_all(product.reshape(row_count, rows_here, requests, width_here...  8.02 us
    unnamed x47, local copies, waits for them, and re-layouts  7.77 us
    all_to_all x2, starting transfers between devices, body(): lax.all_to_all(expert_out.reshape(row_count, CAP, model_width), 'row', 0,...  7.34 us
  transfers between devices with their start and end apart: 9, of which 9 were waited for; matrix products, arithmetic and copies ran while one was open for 33% of the time, Pallas kernels for 0%

profile of v9, /device:TPU:0, one launch (start us, length us, event | category | flops | bytes accessed | tf_op | source)
XLA Modules:
  0.0 196.9 jit_solution(16434323037658222765)
XLA Ops:
  1.7 1.1 broadcast_in_dim.111
  2.8 5.2 %all-to-all-start = ((bf16[8,64,2,512]{3,1,2,0:T(8,128)(2,1)}), bf16[8,64,2,512]{3,1,2,0:T(8,128)(2,1)}, u32[]{:S(2)}, u32[]{:S(2)}) async-start(bf16[8,64,2,512]{3,1,2,0:T(8,128)(2,1)} %broadcast_in_dim.111), calls=%async_computation | async-start | bytes 2097152 | tf_op jit(solution)/shard_map/all_to_all | solution.py:58
  8.0 1.2 broadcast_compare_fusion.1
  9.6 2.2 %maximum_bitcast_fusion = bf16[2,512,192]{1,0,2:T(2,128)(2,1)} fusion(bf16[64,2,512]{2,1,0:T(2,128)(2,1)S(1)} %copy-done.11, bf16[128,2,512]{2,1,0:T(2,128)(2,1)} %param.20), kind=kLoop, calls=%fused_computation.63 | loop fusion | flops 196608 | bytes 786432 | tf_op jit(solution)/shard_map/transpose | solution.py:50
  11.8 2.3 %maximum_bitcast_fusion.1 = bf16[2,192,512]{2,0,1:T(2,128)(2,1)} fusion(bf16[64,2,512]{2,1,0:T(2,128)(2,1)} %param.19, bf16[128,2,512]{2,1,0:T(2,128)(2,1)} %param.21), kind=kLoop, calls=%fused_computation.64 | loop fusion | flops 196608 | bytes 786432 | tf_op jit(solution)/shard_map/transpose | solution.py:54
  16.3 1.6 bitcast_select_fusion.3
  18.0 1.7 bitcast_select_fusion.2
  20.1 3.5 %all-to-all-done = bf16[8,64,2,512]{3,1,2,0:T(8,128)(2,1)} async-done(((bf16[8,64,2,512]{3,1,2,0:T(8,128)(2,1)}), bf16[8,64,2,512]{3,1,2,0:T(8,128)(2,1)}, u32[]{:S(2)}, u32[]{:S(2)}) %all-to-all-start) | async-done | bytes 1048608 | tf_op jit(solution)/shard_map/all_to_all | solution.py:58
  23.5 1.4 copy.80
  25.4 1.5 select_reduce_fusion.1
  28.0 2.6 %fusion.14 = bf16[2,512,1024]{1,2,0:T(8,128)(2,1)} fusion(f32[2,1024,512]{2,1,0:T(8,128)S(1)} %get-tuple-element.17, f32[2,512,4]{1,2,0:T(4,128)S(1)} %get-tuple-element.16, pred[2,512,256]{1,2,0:T(8,128)(4,1)S(1)} %broadcast_or_fusion), kind=kLoop, calls=%fused_computation.16 | loop fusion | flops 5242880 | bytes 6569984 | tf_op jit(solution)/shard_map/convert_element_type | solution.py:84
  31.6 3.3 %all-to-all-start.1 = ((f32[8,1,1024]{2,1,0:T(1,128)}), f32[8,1,1024]{2,1,0:T(1,128)S(1)}, u32[]{:S(2)}, u32[]{:S(2)}) async-start(f32[8,1,1024]{2,1,0:T(1,128)} %reshape.405), calls=%async_computation.1 | async-start | bytes 65536 | tf_op jit(solution)/shard_map/all_to_all | solution.py:92
  34.9 3.5 %convolution_convert_fusion.1 = bf16[2,512,512]{1,2,0:T(8,128)(2,1)S(1)} fusion(bf16[2,1024,512]{2,1,0:T(8,128)(2,1)} %bitcast_select_fusion.2, bf16[2,512,1024]{1,2,0:T(8,128)(2,1)} %fusion.14), kind=kOutput, calls=%fused_computation.35 | convolution fusion | flops 1074266112 | bytes 5242880 | tf_op jit(solution)/shard_map/ric,rck->irk/dot_general | solution.py:82
  39.7 4.2 %all-to-all-start.2 = ((bf16[8,64,2,512]{3,1,2,0:T(8,128)(2,1)}), bf16[8,64,2,512]{3,1,2,0:T(8,128)(2,1)}, u32[]{:S(2)}, u32[]{:S(2)}) async-start(bf16[8,64,2,512]{3,1,2,0:T(8,128)(2,1)} %copy.86), calls=%async_computation.2 | async-start | bytes 2097152 | tf_op jit(solution)/shard_map/all_to_all | solution.py:89
  45.6 2.2 %broadcast_in_dim.115 = f32[8,64,2,4,128]{4,3,1,2,0:T(4,128)} broadcast(f32[8,64,2,4]{3,1,2,0:T(8,128)S(1)} %copy.83), dimensions={0,1,2,3} | broadcast | bytes 2113536 | tf_op jit(solution)/shard_map/broadcast_in_dim | solution.py:99
  47.8 3.1 %reshape.383 = f32[8,64,2,512]{3,1,2,0:T(8,128)} reshape(f32[8,64,2,4,128]{4,3,1,2,0:T(4,128)} %broadcast_in_dim.115) | data formatting | bytes 4194304 | tf_op jit(solution)/shard_map/reshape | solution.py:101
  51.3 8.0 %all-to-all-done.2 = bf16[8,64,2,512]{3,1,2,0:T(8,128)(2,1)} async-done(((bf16[8,64,2,512]{3,1,2,0:T(8,128)(2,1)}), bf16[8,64,2,512]{3,1,2,0:T(8,128)(2,1)}, u32[]{:S(2)}, u32[]{:S(2)}) %all-to-all-start.2) | async-done | bytes 1048608 | tf_op jit(solution)/shard_map/all_to_all | solution.py:89
  59.3 2.2 %multiply_reduce_fusion = f32[64,2,512]{2,0,1:T(8,128)S(1)} fusion(f32[8,64,2,512]{3,1,2,0:T(8,128)} %reshape.383, bf16[8,64,2,512]{3,1,2,0:T(8,128)(2,1)} %all-to-all-done.2), kind=kLoop, calls=%fused_computation.34 | loop fusion | flops 1507328 | bytes 3407872 | tf_op jit(solution)/shard_map/reduce_sum | solution.py:102
  61.8 2.8 %fusion.60 = bf16[4,128,512]{2,1,0:T(8,128)(2,1)} fusion(bf16[128,512,1]{1,0,2:T(8,128)(2,1)S(1)} %reshape.398, bf16[64,4,8,512]{3,2,1,0:T(8,128)(2,1)} %bitcast.207), kind=kOutput, calls=%fused_computation.45 | convolution fusion | flops 268697600 | bytes 2752512 | tf_op jit(solution)/shard_map/tk,kcw->ctw/dot_general | solution.py:111
  64.7 5.3 %all-to-all-start.3 = ((bf16[4,128,512]{2,1,0:T(8,128)(2,1)}), bf16[4,128,512]{2,1,0:T(8,128)(2,1)S(1)}, u32[]{:S(2)}, u32[]{:S(2)}) async-start(bf16[4,128,512]{2,1,0:T(8,128)(2,1)} %fusion.60), calls=%async_computation.3 | async-start | bytes 1048576 | tf_op jit(solution)/shard_map/all_to_all | solution.py:118
  70.0 2.0 %reshape.379 = bf16[128,2048]{1,0:T(8,128)(2,1)} reshape(bf16[64,2,2048]{2,1,0:T(2,128)(2,1)} %param.23) | data formatting | bytes 1048576 | tf_op jit(solution)/shard_map/reshape | solution.py:121
  73.0 4.4 %reduce-window.6 = s32[64,6,128]{2,0,1:T(8,128)} reduce-window(s32[64,6,128]{2,0,1:T(8,128)} %fusion.75, s32[]{:T(128)} %constant.86.clone.1), window={size=1x1x128 pad=0_0x0_0x127_0}, to_apply=%region_6.7 | reduce-window | flops 6242304 | bytes 393220 | tf_op jit(solution)/shard_map/reduce-window
  77.4 4.1 %all-to-all-done.3 = bf16[4,128,512]{2,1,0:T(8,128)(2,1)S(1)} async-done(((bf16[4,128,512]{2,1,0:T(8,128)(2,1)}), bf16[4,128,512]{2,1,0:T(8,128)(2,1)S(1)}, u32[]{:S(2)}, u32[]{:S(2)}) %all-to-all-start.3) | async-done | bytes 524320 | tf_op jit(solution)/shard_map/all_to_all | solution.py:118
  83.5 3.5 %all-to-all-start.4 = ((bf16[4,128,512]{1,2,0:T(8,128)(2,1)}), bf16[4,128,512]{1,2,0:T(8,128)(2,1)S(1)}, u32[]{:S(2)}, u32[]{:S(2)}) async-start(bf16[4,128,512]{1,2,0:T(8,128)(2,1)} %broadcast_in_dim.125), calls=%async_computation.4 | async-start | bytes 1048576 | tf_op jit(solution)/shard_map/all_to_all | solution.py:124
  87.0 1.2 slice_reduce_fusion
  91.0 1.6 add_select_fusion.2
  93.5 1.4 copy.97
  96.9 2.2 %all-to-all-done.4 = bf16[4,128,512]{1,2,0:T(8,128)(2,1)S(1)} async-done(((bf16[4,128,512]{1,2,0:T(8,128)(2,1)}), bf16[4,128,512]{1,2,0:T(8,128)(2,1)S(1)}, u32[]{:S(2)}, u32[]{:S(2)}) %all-to-all-start.4) | async-done | bytes 524320 | tf_op jit(solution)/shard_map/all_to_all | solution.py:124
  99.9 1.4 fusion.66
  101.3 2.6 %convolution_convert_fusion = bf16[384,2048]{1,0:T(8,128)(2,1)} fusion(bf16[128,2048]{0,1:T(8,128)(2,1)S(1)} %fusion.66, bf16[128,384]{1,0:T(8,128)(2,1)} %get-tuple-element.7), kind=kOutput, calls=%fused_computation.19 | convolution fusion | flops 202113024 | bytes 2195456 | tf_op jit(solution)/shard_map/dot_general | solution.py:157
  103.9 6.9 %all-to-all-start.5 = ((bf16[8,2,24,2048]{3,2,1,0:T(8,128)(2,1)}), bf16[8,2,24,2048]{3,2,1,0:T(8,128)(2,1)}, u32[]{:S(2)}, u32[]{:S(2)}) async-start(bf16[8,2,24,2048]{3,2,1,0:T(8,128)(2,1)} %bitcast.182), calls=%async_computation.5 | async-start | bytes 3145728 | tf_op jit(solution)/shard_map/all_to_all | solution.py:161
  110.8 1.7 copy.99
  112.6 3.5 %fusion.100 = f32[128,704]{0,1:T(8,128)} fusion(bf16[2048,704]{0,1:T(8,128)(2,1)} %param.31, bf16[128,2048]{0,1:T(8,128)(2,1)S(1)} %fusion.66), kind=kOutput, calls=%fused_computation.138 | convolution fusion | flops 369098752 | bytes 3768320 | tf_op jit(solution)/shard_map/dot_general | solution.py:162
  116.0 5.0 %fusion.64 = f32[128,2048]{1,0:T(8,128)} fusion(bf16[704,2048]{1,0:T(8,128)(2,1)S(1)} %copy-done, bf16[2048,704]{0,1:T(8,128)(2,1)} %param.32, bf16[128,2048]{0,1:T(8,128)(2,1)S(1)} %fusion.66, f32[128,704]{0,1:T(8,128)} %fusion.100), kind=kOutput, calls=%fused_computation.51 | convolution fusion | flops 738738176 | bytes 7700480 | tf_op jit(solution)/shard_map/dot_general | solution.py:165
  121.0 11.0 %all-to-all-done.5 = bf16[8,2,24,2048]{3,2,1,0:T(8,128)(2,1)} async-done(((bf16[8,2,24,2048]{3,2,1,0:T(8,128)(2,1)}), bf16[8,2,24,2048]{3,2,1,0:T(8,128)(2,1)}, u32[]{:S(2)}, u32[]{:S(2)}) %all-to-all-start.5) | async-done | bytes 1572896 | tf_op jit(solution)/shard_map/all_to_all | solution.py:161
  131.9 1.5 fusion.95
  133.5 4.8 %fusion.39 = f32[4,192,352]{2,1,0:T(8,128)S(1)} fusion(bf16[192,2048,1]{1,0,2:T(8,128)(2,1)S(1)} %bitcast.191, bf16[8,2048,352]{1,2,0:T(8,128)(2,1)} %param.28), kind=kOutput, calls=%fused_computation.38 | convolution fusion | flops 1107296256 | bytes 7634944 | tf_op jit(solution)/shard_map/td,gdf->gtf/dot_general | solution.py:178
  138.3 4.8 %fusion.54 = bf16[4,192,352]{2,1,0:T(8,128)(2,1)S(1)} fusion(bf16[192,2048,1]{1,0,2:T(8,128)(2,1)S(1)} %bitcast.192, bf16[8,2048,352]{1,2,0:T(8,128)(2,1)} %param.29, f32[4,192,352]{2,1,0:T(8,128)S(1)} %fusion.39), kind=kOutput, calls=%fused_computation.43 | convolution fusion | flops 1108918272 | bytes 8175616 | tf_op jit(solution)/shard_map/td,gdf->gtf/dot_general | solution.py:181
  143.1 2.3 %fusion.21 = bf16[192,2048]{1,0:T(8,128)(2,1)} fusion(bf16[4,192,352]{2,1,0:T(8,128)(2,1)S(1)} %fusion.54, bf16[8,352,2048]{2,1,0:T(8,128)(2,1)S(1)} %bitcast.204), kind=kOutput, calls=%fused_computation.22 | convolution fusion | flops 1107689472 | bytes 7143424 | tf_op jit(solution)/shard_map/gtf,gfd->td/dot_general | solution.py:185
  145.4 3.8 %all-to-all-start.7 = ((bf16[8,24,2048]{2,1,0:T(8,128)(2,1)}), bf16[8,24,2048]{2,1,0:T(8,128)(2,1)S(1)}, u32[]{:S(2)}, u32[]{:S(2)}) async-start(bf16[8,24,2048]{2,1,0:T(8,128)(2,1)} %bitcast.40), calls=%async_computation.7 | async-start | bytes 1572864 | tf_op jit(solution)/shard_map/all_to_all | solution.py:188
  149.2 4.8 %fusion.33 = f32[4,192,352]{2,1,0:T(8,128)S(1)} fusion(bf16[192,2048,1]{1,0,2:T(8,128)(2,1)S(1)} %bitcast.189, bf16[8,2048,352]{1,2,0:T(8,128)(2,1)} %param.28), kind=kOutput, calls=%fused_computation.36 | convolution fusion | flops 1107296256 | bytes 7634944 | tf_op jit(solution)/shard_map/td,gdf->gtf/dot_general | solution.py:178
  154.0 4.8 %fusion.51 = bf16[4,192,352]{2,1,0:T(8,128)(2,1)S(1)} fusion(bf16[192,2048,1]{1,0,2:T(8,128)(2,1)S(1)} %bitcast.190, bf16[8,2048,352]{1,2,0:T(8,128)(2,1)} %param.29, f32[4,192,352]{2,1,0:T(8,128)S(1)} %fusion.33), kind=kOutput, calls=%fused_computation.42 | convolution fusion | flops 1108918272 | bytes 8175616 | tf_op jit(solution)/shard_map/td,gdf->gtf/dot_general | solution.py:181
  158.9 2.3 %fusion.24 = bf16[192,2048]{1,0:T(8,128)(2,1)} fusion(bf16[4,192,352]{2,1,0:T(8,128)(2,1)S(1)} %fusion.51, bf16[8,352,2048]{2,1,0:T(8,128)(2,1)S(1)} %bitcast.206), kind=kOutput, calls=%fused_computation.23 | convolution fusion | flops 1107689472 | bytes 7143424 | tf_op jit(solution)/shard_map/gtf,gfd->td/dot_general | solution.py:185
  161.5 3.6 %all-to-all-start.6 = ((bf16[8,24,2048]{2,1,0:T(8,128)(2,1)}), bf16[8,24,2048]{2,1,0:T(8,128)(2,1)S(1)}, u32[]{:S(2)}, u32[]{:S(2)}) async-start(bf16[8,24,2048]{2,1,0:T(8,128)(2,1)} %bitcast.30), calls=%async_computation.6 | async-start | bytes 1572864 | tf_op jit(solution)/shard_map/all_to_all | solution.py:188
  165.2 1.3 fusion.99
  166.5 11.2 %all-to-all-done.6 = bf16[8,24,2048]{2,1,0:T(8,128)(2,1)S(1)} async-done(((bf16[8,24,2048]{2,1,0:T(8,128)(2,1)}), bf16[8,24,2048]{2,1,0:T(8,128)(2,1)S(1)}, u32[]{:S(2)}, u32[]{:S(2)}) %all-to-all-start.6) | async-done | bytes 786464 | tf_op jit(solution)/shard_map/all_to_all | solution.py:188
  180.7 3.5 %all-to-all-start.8 = ((bf16[4,128,512]{2,1,0:T(8,128)(2,1)}), bf16[4,128,512]{2,1,0:T(8,128)(2,1)S(1)}, u32[]{:S(2)}, u32[]{:S(2)}) async-start(bf16[4,128,512]{2,1,0:T(8,128)(2,1)} %bitcast.185), calls=%async_computation.8 | async-start | bytes 1048576 | tf_op jit(solution)/shard_map/all_to_all | solution.py:204
  184.8 11.2 %all-to-all-done.8 = bf16[4,128,512]{2,1,0:T(8,128)(2,1)S(1)} async-done(((bf16[4,128,512]{2,1,0:T(8,128)(2,1)}), bf16[4,128,512]{2,1,0:T(8,128)(2,1)S(1)}, u32[]{:S(2)}, u32[]{:S(2)}) %all-to-all-start.8) | async-done | bytes 524320 | tf_op jit(solution)/shard_map/all_to_all | solution.py:204
  (106 shorter events, 24.4 us)
Async XLA Ops:
  0.6 115.4 %copy-start = (bf16[704,2048]{1,0:T(8,128)(2,1)S(1)}, bf16[704,2048]{1,0:T(8,128)(2,1)}, u32[]{:S(2)}) copy-start(bf16[704,2048]{1,0:T(8,128)(2,1)} %param.33) | copy-start | bytes 8650756
  1.7 7.9 %copy-start.11 = (bf16[64,2,512]{2,1,0:T(2,128)(2,1)S(1)}, bf16[64,2,512]{2,1,0:T(2,128)(2,1)}, u32[]{:S(2)}) copy-start(bf16[64,2,512]{2,1,0:T(2,128)(2,1)} %param.18) | copy-start | bytes 393220
  2.8 20.7 %all-to-all-start = ((bf16[8,64,2,512]{3,1,2,0:T(8,128)(2,1)}), bf16[8,64,2,512]{3,1,2,0:T(8,128)(2,1)}, u32[]{:S(2)}, u32[]{:S(2)}) async-start(bf16[8,64,2,512]{3,1,2,0:T(8,128)(2,1)} %broadcast_in_dim.111), calls=%async_computation | async-start | bytes 2097152 | tf_op jit(solution)/shard_map/all_to_all | solution.py:58
  14.1 2.2 %copy-start.8 = (pred[512,1024]{0,1:T(8,128)(4,1)S(1)}, pred[512,1024]{0,1:T(8,128)(4,1)}, u32[]{:S(2)}) copy-start(pred[512,1024]{0,1:T(8,128)(4,1)} %broadcast_compare_fusion.1) | copy-start | bytes 1572868
  17.9 1.7 copy-start.13
  23.5 1.9 copy-start.2
  31.6 8.1 %all-to-all-start.1 = ((f32[8,1,1024]{2,1,0:T(1,128)}), f32[8,1,1024]{2,1,0:T(1,128)S(1)}, u32[]{:S(2)}, u32[]{:S(2)}) async-start(f32[8,1,1024]{2,1,0:T(1,128)} %reshape.405), calls=%async_computation.1 | async-start | bytes 65536 | tf_op jit(solution)/shard_map/all_to_all | solution.py:92
  39.7 19.7 %all-to-all-start.2 = ((bf16[8,64,2,512]{3,1,2,0:T(8,128)(2,1)}), bf16[8,64,2,512]{3,1,2,0:T(8,128)(2,1)}, u32[]{:S(2)}, u32[]{:S(2)}) async-start(bf16[8,64,2,512]{3,1,2,0:T(8,128)(2,1)} %copy.86), calls=%async_computation.2 | async-start | bytes 2097152 | tf_op jit(solution)/shard_map/all_to_all | solution.py:89
  61.8 10.2 %copy-start.12 = (s32[64,2,6]{0,1,2:T(2,128)S(1)}, s32[64,2,6]{0,1,2:T(2,128)}, u32[]{:S(2)}) copy-start(s32[64,2,6]{0,1,2:T(2,128)} %param.26) | copy-start | bytes 9220
  64.7 16.8 %all-to-all-start.3 = ((bf16[4,128,512]{2,1,0:T(8,128)(2,1)}), bf16[4,128,512]{2,1,0:T(8,128)(2,1)S(1)}, u32[]{:S(2)}, u32[]{:S(2)}) async-start(bf16[4,128,512]{2,1,0:T(8,128)(2,1)} %fusion.60), calls=%async_computation.3 | async-start | bytes 1048576 | tf_op jit(solution)/shard_map/all_to_all | solution.py:118
  72.1 9.4 %copy-start.9 = (s32[64,2,6]{2,1,0:T(2,128)}, s32[64,2,6]{2,1,0:T(2,128)S(1)}, u32[]{:S(2)}) copy-start(s32[64,2,6]{2,1,0:T(2,128)S(1)} %copy.92) | copy-start | bytes 9220
  83.5 15.6 %all-to-all-start.4 = ((bf16[4,128,512]{1,2,0:T(8,128)(2,1)}), bf16[4,128,512]{1,2,0:T(8,128)(2,1)S(1)}, u32[]{:S(2)}, u32[]{:S(2)}) async-start(bf16[4,128,512]{1,2,0:T(8,128)(2,1)} %broadcast_in_dim.125), calls=%async_computation.4 | async-start | bytes 1048576 | tf_op jit(solution)/shard_map/all_to_all | solution.py:124
  99.1 0.8 copy-start.5
  103.9 28.0 %all-to-all-start.5 = ((bf16[8,2,24,2048]{3,2,1,0:T(8,128)(2,1)}), bf16[8,2,24,2048]{3,2,1,0:T(8,128)(2,1)}, u32[]{:S(2)}, u32[]{:S(2)}) async-start(bf16[8,2,24,2048]{3,2,1,0:T(8,128)(2,1)} %bitcast.182), calls=%async_computation.5 | async-start | bytes 3145728 | tf_op jit(solution)/shard_map/all_to_all | solution.py:161
  133.5 9.6 %slice-start = ((s8[11534336]{0:T(1024)(128)(4,1)}), s8[4194304]{0:T(1024)(128)(4,1)S(1)}, s32[]{:S(2)}) async-start(s8[11534336]{0:T(1024)(128)(4,1)} %bitcast.203), calls=%async_computation.9 | async-start | bytes 8388608
  133.5 9.6 %slice-start.1 = ((s8[11534336]{0:T(1024)(128)(4,1)}), s8[4194304]{0:T(1024)(128)(4,1)S(1)}, s32[]{:S(2)}) async-start(s8[11534336]{0:T(1024)(128)(4,1)} %bitcast.203), calls=%async_computation.10 | async-start | bytes 8388608
  138.3 4.8 %slice-start.2 = ((s8[11534336]{0:T(1024)(128)(4,1)}), s8[3145728]{0:T(1024)(128)(4,1)S(1)}, s32[]{:S(2)}) async-start(s8[11534336]{0:T(1024)(128)(4,1)} %bitcast.203), calls=%async_computation.11 | async-start | bytes 6291456
  145.4 16.1 %all-to-all-start.7 = ((bf16[8,24,2048]{2,1,0:T(8,128)(2,1)}), bf16[8,24,2048]{2,1,0:T(8,128)(2,1)S(1)}, u32[]{:S(2)}, u32[]{:S(2)}) async-start(bf16[8,24,2048]{2,1,0:T(8,128)(2,1)} %bitcast.40), calls=%async_computation.7 | async-start | bytes 1572864 | tf_op jit(solution)/shard_map/all_to_all | solution.py:188
  149.2 9.6 %slice-start.3 = ((s8[11534336]{0:T(1024)(128)(4,1)}), s8[4194304]{0:T(1024)(128)(4,1)S(1)}, s32[]{:S(2)}) async-start(s8[11534336]{0:T(1024)(128)(4,1)} %bitcast.205), calls=%async_computation.12 | async-start | bytes 8388608
  149.2 9.6 %slice-start.4 = ((s8[11534336]{0:T(1024)(128)(4,1)}), s8[4194304]{0:T(1024)(128)(4,1)S(1)}, s32[]{:S(2)}) async-start(s8[11534336]{0:T(1024)(128)(4,1)} %bitcast.205), calls=%async_computation.13 | async-start | bytes 8388608
  154.0 4.8 %slice-start.5 = ((s8[11534336]{0:T(1024)(128)(4,1)}), s8[3145728]{0:T(1024)(128)(4,1)S(1)}, s32[]{:S(2)}) async-start(s8[11534336]{0:T(1024)(128)(4,1)} %bitcast.205), calls=%async_computation.14 | async-start | bytes 6291456
  158.8 6.2 %copy-start.10 = (f32[128,384]{0,1:T(8,128)S(1)}, f32[128,384]{0,1:T(8,128)}, u32[]{:S(2)}) copy-start(f32[128,384]{0,1:T(8,128)} %copy.99) | copy-start | bytes 589828
  161.5 5.0 %copy-start.3 = (bf16[8,24,2048]{2,1,0:T(8,128)(2,1)}, bf16[8,24,2048]{2,1,0:T(8,128)(2,1)S(1)}, u32[]{:S(2)}) copy-start(bf16[8,24,2048]{2,1,0:T(8,128)(2,1)S(1)} %all-to-all-done.7) | copy-start | bytes 2359300
  161.5 16.2 %all-to-all-start.6 = ((bf16[8,24,2048]{2,1,0:T(8,128)(2,1)}), bf16[8,24,2048]{2,1,0:T(8,128)(2,1)S(1)}, u32[]{:S(2)}, u32[]{:S(2)}) async-start(bf16[8,24,2048]{2,1,0:T(8,128)(2,1)} %bitcast.30), calls=%async_computation.6 | async-start | bytes 1572864 | tf_op jit(solution)/shard_map/all_to_all | solution.py:188
  177.7 1.1 copy-start.4
  177.7 1.5 copy-start.6
  177.7 1.8 copy-start.7
  179.5 17.4 %copy-start.1 = (bf16[704,2048]{1,0:T(8,128)(2,1)S(1)}, bf16[704,2048]{1,0:T(8,128)(2,1)}, u32[]{:S(2)}) copy-start(bf16[704,2048]{1,0:T(8,128)(2,1)} %param.33) | copy-start | bytes 8650756
  180.7 15.4 %all-to-all-start.8 = ((bf16[4,128,512]{2,1,0:T(8,128)(2,1)}), bf16[4,128,512]{2,1,0:T(8,128)(2,1)S(1)}, u32[]{:S(2)}, u32[]{:S(2)}) async-start(bf16[4,128,512]{2,1,0:T(8,128)(2,1)} %bitcast.185), calls=%async_computation.8 | async-start | bytes 1048576 | tf_op jit(solution)/shard_map/all_to_all | solution.py:204

commit v10 on v9

--- a/solution.py
+++ b/solution.py
@@ -86,11 +86,28 @@
         preferred_element_type=jnp.float32,
     ).astype(jnp.bfloat16)
     stats = jnp.stack([block_max, block_sum], axis=-1).transpose(1, 0, 2, 3)
-    product_back = lax.all_to_all(
-        product.reshape(row_count, rows_here, requests, width_here), "row", 0, 0, tiled=True
-    )
-    stats_back = lax.all_to_all(
-        stats.reshape(row_count, rows_here, requests, heads_here, 2), "row", 0, 0, tiled=True
+    stats_flat = stats.reshape(row_count, rows_here * requests * heads_here * 2)
+    stats_hi = lax.reduce_precision(stats_flat, exponent_bits=8, mantissa_bits=7)
+    stats_rest = stats_flat - stats_hi
+    stats_mid = lax.reduce_precision(stats_rest, exponent_bits=8, mantissa_bits=7)
+    stats_lo = stats_rest - stats_mid
+    stat_rows = (
+        jnp.stack([stats_hi, stats_mid, stats_lo], axis=1)
+        .astype(jnp.bfloat16)
+        .reshape(row_count, -1, width_here)
+    )
+    packed = jnp.concatenate(
+        [product.reshape(row_count, rows_here * requests, width_here), stat_rows], axis=1
+    )
+    packed_back = lax.all_to_all(packed, "row", 0, 0, tiled=True)
+    product_back = packed_back[:, : rows_here * requests].reshape(
+        row_count, rows_here, requests, width_here
+    )
+    stats_parts = (
+        packed_back[:, rows_here * requests :].astype(jnp.float32).reshape(row_count, 3, -1)
+    )
+    stats_back = (stats_parts[:, 0] + stats_parts[:, 1] + stats_parts[:, 2]).reshape(
+        row_count, rows_here, requests, heads_here, 2
     )
     part_max = stats_back[..., 0]
     row_top = jnp.max(part_max, axis=0)
@@ -168,10 +185,16 @@
     wg = w_gate.reshape(experts_dev, groups_dev, model_width, hidden)
     wu = w_up.reshape(experts_dev, groups_dev, model_width, hidden)
     wd = w_down.reshape(experts_dev, groups_dev, hidden, model_width)
-    combine_hi = combine.astype(jnp.bfloat16).reshape(token_count, row_count, experts_dev, CAP)
-    combine_lo = (combine - combine_hi.reshape(token_count, slots).astype(jnp.float32)).astype(
-        jnp.bfloat16
-    ).reshape(token_count, row_count, experts_dev, CAP)
+    combine_hi = (
+        lax.reduce_precision(combine, exponent_bits=8, mantissa_bits=7)
+        .astype(jnp.bfloat16)
+        .reshape(token_count, row_count, experts_dev, CAP)
+    )
+    combine_lo = (
+        (combine - lax.reduce_precision(combine, exponent_bits=8, mantissa_bits=7))
+        .astype(jnp.bfloat16)
+        .reshape(token_count, row_count, experts_dev, CAP)
+    )
     routed = jnp.zeros((token_count, model_width), jnp.float32)
     for chunk in range(experts_dev):
         rows_in = arrived[:, chunk].reshape(row_count * CAP, model_width)

time: 199 us -> 222 us (1.12)
  blocking collectives: 0 us -> 18.5 us
  local copies, waits for them, and re-layouts: 31.8 us -> 46.3 us
  starting transfers between devices: 39.2 us -> 29 us
  waiting for transfers between devices: 51.6 us -> 48.1 us
  other arithmetic: 28.1 us -> 31.5 us
    all_to_all x0 -> x1, blocking collectives: none -> 18.5 us  [body(): packed_back = lax.all_to_all(packed, 'row', 0, 0, tiled=True)]
    all_to_all x2 -> x0, waiting for transfers between devices: 8.16 us -> none  [the longest x1 8.02 us: body(): lax.all_to_all(product.reshape(row_count, rows_here, requests, width_here...]
    all_to_all x2 -> x0, starting transfers between devices: 7.58 us -> none  [the longest x1 4.24 us: body(): lax.all_to_all(product.reshape(row_count, rows_here, requests, width_here...]
    broadcast_in_dim x2 -> x3, local copies, waits for them, and re-layouts: 2.46 us -> 7.9 us  [body(): jnp.broadcast_to(rescale[..., None], rescale.shape + (HD,))]
    all_to_all x1, waiting for transfers between devices: 4.11 us -> 7 us  [body(): lax.all_to_all(attn_chunks, 'col', 0, 0, tiled=True).astype(jnp.float32)]
    all_to_all x1, starting transfers between devices: 6.88 us -> 4.5 us  [body(): arrived = lax.all_to_all(outgoing, 'row', 0, 0, tiled=True)]
    slice x1 -> x2, local copies, waits for them, and re-layouts: 1.2 us -> 3.57 us  [the longest x1 2.37 us: body(): row_total = jnp.sum(rescale * stats_back[..., 1], axis=0)]
    reshape x5 -> x3, local copies, waits for them, and re-layouts: 4.43 us -> 5.96 us  [the longest x1 3.62 us: body(): stats_flat = stats.reshape(row_count, rows_here * requests * heads_here * 2)]
  transfers between devices with their start and end apart: 9 -> 7, of which waited for: 9 -> 7; matrix products, arithmetic and copies ran while one was open for 33% -> 24% of each run, Pallas kernels for 0% -> 0%
where the time goes in v10:
time: 222 us; the launch traced here: 219 us
  waiting for transfers between devices  48.1 us (22%)
  local copies, waits for them, and re-layouts  46.3 us (21%)
  matrix products  44.9 us (20%)
  other arithmetic  31.5 us (14%)
  starting transfers between devices  29 us (13%)
  blocking collectives  18.5 us (8%)
    all_to_all x1, blocking collectives, body(): packed_back = lax.all_to_all(packed, 'row', 0, 0, tiled=True)  18.5 us
    all_to_all x2, waiting for transfers between devices, body(): lax.all_to_all(expert_out.reshape(row_count, CAP, model_width), 'row', 0,...  11.8 us
    all_to_all x1, waiting for transfers between devices, body(): lax.all_to_all(ffn_chunks, 'col', 0, 0, tiled=True).astype(jnp.float32)  11.2 us
    all_to_all x1, waiting for transfers between devices, body(): arrived = lax.all_to_all(outgoing, 'row', 0, 0, tiled=True)  10.6 us
    dot_general x2, matrix products, body(): jnp.einsum('td,gdf->gtf', rows_in, wu[chunk], preferred_element_type=jnp....  9.57 us
    dot_general x2, matrix products, body(): jnp.einsum('td,gdf->gtf', rows_in, wg[chunk], preferred_element_type=jnp....  9.52 us
    unnamed x47, local copies, waits for them, and re-layouts  7.94 us
    broadcast_in_dim x3, local copies, waits for them, and re-layouts, body(): jnp.broadcast_to(rescale[..., None], rescale.shape + (HD,))  7.9 us
  transfers between devices with their start and end apart: 7, of which 7 were waited for; matrix products, arithmetic and copies ran while one was open for 24% of the time, Pallas kernels for 0%

profile of v10, /device:TPU:0, one launch (start us, length us, event | category | flops | bytes accessed | tf_op | source)
XLA Modules:
  0.0 219.4 jit_solution(14313763513627079688)
XLA Ops:
  2.8 5.2 %all-to-all-start = ((bf16[8,64,2,512]{3,1,2,0:T(8,128)(2,1)}), bf16[8,64,2,512]{3,1,2,0:T(8,128)(2,1)}, u32[]{:S(2)}, u32[]{:S(2)}) async-start(bf16[8,64,2,512]{3,1,2,0:T(8,128)(2,1)} %broadcast_in_dim.118), calls=%async_computation | async-start | bytes 2097152 | tf_op jit(solution)/shard_map/all_to_all | solution.py:58
  9.6 2.2 %maximum_bitcast_fusion.1 = bf16[2,512,192]{1,0,2:T(2,128)(2,1)} fusion(bf16[64,2,512]{2,1,0:T(2,128)(2,1)S(1)} %copy-done.12, bf16[128,2,512]{2,1,0:T(2,128)(2,1)} %param.20), kind=kLoop, calls=%fused_computation.66 | loop fusion | flops 196608 | bytes 786432 | tf_op jit(solution)/shard_map/transpose | solution.py:50
  11.8 2.3 %maximum_bitcast_fusion = bf16[2,192,512]{2,0,1:T(2,128)(2,1)} fusion(bf16[64,2,512]{2,1,0:T(2,128)(2,1)} %param.19, bf16[128,2,512]{2,1,0:T(2,128)(2,1)} %param.21), kind=kLoop, calls=%fused_computation.65 | loop fusion | flops 196608 | bytes 786432 | tf_op jit(solution)/shard_map/transpose | solution.py:54
  16.3 1.6 bitcast_select_fusion.2
  18.0 1.7 bitcast_select_fusion.3
  20.1 3.4 %all-to-all-done = bf16[8,64,2,512]{3,1,2,0:T(8,128)(2,1)} async-done(((bf16[8,64,2,512]{3,1,2,0:T(8,128)(2,1)}), bf16[8,64,2,512]{3,1,2,0:T(8,128)(2,1)}, u32[]{:S(2)}, u32[]{:S(2)}) %all-to-all-start) | async-done | bytes 1048608 | tf_op jit(solution)/shard_map/all_to_all | solution.py:58
  23.5 1.4 copy.84
  25.4 1.5 select_reduce_fusion.1
  28.0 2.6 %fusion.14 = bf16[2,512,1024]{1,2,0:T(8,128)(2,1)} fusion(f32[2,1024,512]{2,1,0:T(8,128)S(1)} %get-tuple-element.22, f32[2,512,4]{1,2,0:T(4,128)S(1)} %get-tuple-element.21, pred[2,512,256]{1,2,0:T(8,128)(4,1)S(1)} %broadcast_or_fusion), kind=kLoop, calls=%fused_computation.16 | loop fusion | flops 5242880 | bytes 6569984 | tf_op jit(solution)/shard_map/convert_element_type | solution.py:84
  30.6 1.8 copy.87
  32.4 3.6 %reshape.432 = f32[8,1,1024]{2,0,1:T(8,128)S(1)} reshape(f32[512,2,4,2]{3,2,1,0:T(4,128)} %copy.87) | data formatting | bytes 65536 | tf_op jit(solution)/shard_map/reshape | solution.py:89
  36.2 3.5 %fusion.45 = bf16[512,2,512]{2,0,1:T(8,128)(2,1)S(1)} fusion(bf16[2,1024,512]{2,1,0:T(8,128)(2,1)} %bitcast_select_fusion.3, bf16[2,512,1024]{1,2,0:T(8,128)(2,1)} %fusion.14), kind=kOutput, calls=%fused_computation.40 | convolution fusion | flops 1074266112 | bytes 5242880 | tf_op jit(solution)/shard_map/ric,rck->irk/dot_general | solution.py:82
  39.7 2.1 copy.86
  41.7 2.3 %reshape.431 = bf16[8,128,512]{2,1,0:T(8,128)(2,1)} reshape(bf16[512,2,512]{2,1,0:T(2,128)(2,1)} %copy.86) | data formatting | bytes 2097152 | tf_op jit(solution)/shard_map/reshape | solution.py:100
  45.3 18.5 %all_to_all.40 = bf16[8,134,512]{2,1,0:T(8,128)(2,1)S(1)} all-to-all(bf16[8,134,512]{2,1,0:T(8,128)(2,1)S(1)} %pad_maximum_fusion), channel_id=1, replica_groups=mesh['row'=8,'col'=4] {'row'}, dimensions={0} | all-to-all | bytes 2195456 | tf_op jit(solution)/shard_map/all_to_all | solution.py:102
  65.9 2.4 %fusion.94 = (f32[8,64,2,4,1]{0,4,3,2,1:T(1,128)}, f32[8,64,2,4,1]{0,4,3,2,1:T(1,128)S(1)}) fusion(f32[8,64,2,4,2]{0,4,3,2,1:T(2,128)} %bitcast.161), kind=kLoop, calls=%fused_computation.139 | loop fusion | bytes 65536 | tf_op jit(solution)/shard_map/slice | solution.py:115
  68.8 1.6 copy.91
  70.4 3.2 %broadcast_in_dim.125 = f32[8,64,2,4,128]{4,3,2,1,0:T(4,128)} broadcast(f32[8,64,2,4]{3,2,1,0:T(2,128)} %copy.91), dimensions={0,1,2,3} | broadcast | bytes 2113536 | tf_op jit(solution)/shard_map/broadcast_in_dim | solution.py:116
  73.6 3.1 %broadcast_in_dim.126 = f32[8,128,512]{2,1,0:T(8,128)} reshape(f32[8,64,2,4,128]{4,3,2,1,0:T(4,128)} %broadcast_in_dim.125) | data formatting | bytes 4194304 | tf_op jit(solution)/shard_map/broadcast_in_dim | solution.py:116
  76.7 2.9 %multiply_reduce_fusion = f32[128,512]{1,0:T(8,128)} fusion(f32[8,128,512]{2,1,0:T(8,128)} %broadcast_in_dim.126, bf16[8,134,512]{2,1,0:T(8,128)(2,1)} %copy-done.6), kind=kLoop, calls=%fused_computation.34 | loop fusion | flops 1507328 | bytes 3407872 | tf_op jit(solution)/shard_map/reduce_sum | solution.py:119
  82.3 2.8 %fusion.61 = bf16[4,128,512]{2,1,0:T(8,128)(2,1)} fusion(bf16[128,512,1]{1,0,2:T(8,128)(2,1)S(1)} %reshape.449, bf16[64,4,8,512]{3,2,1,0:T(8,128)(2,1)} %bitcast.181), kind=kOutput, calls=%fused_computation.46 | convolution fusion | flops 268697600 | bytes 2752512 | tf_op jit(solution)/shard_map/tk,kcw->ctw/dot_general | solution.py:128
  85.1 5.3 %all-to-all-start.2 = ((bf16[4,128,512]{2,1,0:T(8,128)(2,1)}), bf16[4,128,512]{2,1,0:T(8,128)(2,1)S(1)}, u32[]{:S(2)}, u32[]{:S(2)}) async-start(bf16[4,128,512]{2,1,0:T(8,128)(2,1)} %fusion.61), calls=%async_computation.2 | async-start | bytes 1048576 | tf_op jit(solution)/shard_map/all_to_all | solution.py:135
  90.4 2.0 reshape.428
  93.4 4.4 %reduce-window.6 = s32[64,6,128]{2,0,1:T(8,128)} reduce-window(s32[64,6,128]{2,0,1:T(8,128)} %fusion.77, s32[]{:T(128)} %constant.86.clone.1), window={size=1x1x128 pad=0_0x0_0x127_0}, to_apply=%region_6.7 | reduce-window | flops 6242304 | bytes 393220 | tf_op jit(solution)/shard_map/reduce-window
  97.8 7.0 %all-to-all-done.2 = bf16[4,128,512]{2,1,0:T(8,128)(2,1)S(1)} async-done(((bf16[4,128,512]{2,1,0:T(8,128)(2,1)}), bf16[4,128,512]{2,1,0:T(8,128)(2,1)S(1)}, u32[]{:S(2)}, u32[]{:S(2)}) %all-to-all-start.2) | async-done | bytes 524320 | tf_op jit(solution)/shard_map/all_to_all | solution.py:135
  106.8 3.5 %all-to-all-start.3 = ((bf16[4,128,512]{1,2,0:T(8,128)(2,1)}), bf16[4,128,512]{1,2,0:T(8,128)(2,1)S(1)}, u32[]{:S(2)}, u32[]{:S(2)}) async-start(bf16[4,128,512]{1,2,0:T(8,128)(2,1)} %broadcast_in_dim.131), calls=%async_computation.3 | async-start | bytes 1048576 | tf_op jit(solution)/shard_map/all_to_all | solution.py:141
  114.4 1.6 add_select_fusion.2
  116.9 1.4 copy.98
  120.2 4.0 %all-to-all-done.3 = bf16[4,128,512]{1,2,0:T(8,128)(2,1)S(1)} async-done(((bf16[4,128,512]{1,2,0:T(8,128)(2,1)}), bf16[4,128,512]{1,2,0:T(8,128)(2,1)S(1)}, u32[]{:S(2)}, u32[]{:S(2)}) %all-to-all-start.3) | async-done | bytes 524320 | tf_op jit(solution)/shard_map/all_to_all | solution.py:141
  125.1 1.4 fusion.67
  126.5 2.7 %convolution_convert_fusion = bf16[384,2048]{1,0:T(8,128)(2,1)} fusion(bf16[128,2048]{0,1:T(8,128)(2,1)S(1)} %fusion.67, bf16[128,384]{1,0:T(8,128)(2,1)} %get-tuple-element.7), kind=kOutput, calls=%fused_computation.19 | convolution fusion | flops 202113024 | bytes 2195456 | tf_op jit(solution)/shard_map/dot_general | solution.py:174
  129.1 4.5 %all-to-all-start.4 = ((bf16[8,2,24,2048]{3,2,1,0:T(8,128)(2,1)}), bf16[8,2,24,2048]{3,2,1,0:T(8,128)(2,1)}, u32[]{:S(2)}, u32[]{:S(2)}) async-start(bf16[8,2,24,2048]{3,2,1,0:T(8,128)(2,1)} %bitcast.154), calls=%async_computation.4 | async-start | bytes 3145728 | tf_op jit(solution)/shard_map/all_to_all | solution.py:178
  133.6 1.8 copy.100
  135.4 3.4 %fusion.99 = f32[128,704]{0,1:T(8,128)} fusion(bf16[2048,704]{0,1:T(8,128)(2,1)} %param.31, bf16[128,2048]{0,1:T(8,128)(2,1)S(1)} %fusion.67), kind=kOutput, calls=%fused_computation.144 | convolution fusion | flops 369098752 | bytes 3768320 | tf_op jit(solution)/shard_map/dot_general | solution.py:179
  138.9 5.0 %fusion.65 = f32[128,2048]{1,0:T(8,128)} fusion(bf16[704,2048]{1,0:T(8,128)(2,1)S(1)} %copy-done, bf16[2048,704]{0,1:T(8,128)(2,1)} %param.32, bf16[128,2048]{0,1:T(8,128)(2,1)S(1)} %fusion.67, f32[128,704]{0,1:T(8,128)} %fusion.99), kind=kOutput, calls=%fused_computation.52 | convolution fusion | flops 738738176 | bytes 7700480 | tf_op jit(solution)/shard_map/dot_general | solution.py:182
  143.8 10.6 %all-to-all-done.4 = bf16[8,2,24,2048]{3,2,1,0:T(8,128)(2,1)} async-done(((bf16[8,2,24,2048]{3,2,1,0:T(8,128)(2,1)}), bf16[8,2,24,2048]{3,2,1,0:T(8,128)(2,1)}, u32[]{:S(2)}, u32[]{:S(2)}) %all-to-all-start.4) | async-done | bytes 1572896 | tf_op jit(solution)/shard_map/all_to_all | solution.py:178
  154.5 1.5 fusion.93
  156.0 4.8 %fusion.39 = f32[4,192,352]{2,1,0:T(8,128)S(1)} fusion(bf16[192,2048,1]{1,0,2:T(8,128)(2,1)S(1)} %bitcast.167, bf16[8,2048,352]{1,2,0:T(8,128)(2,1)} %param.28), kind=kOutput, calls=%fused_computation.38 | convolution fusion | flops 1107296256 | bytes 7634944 | tf_op jit(solution)/shard_map/td,gdf->gtf/dot_general | solution.py:201
  160.8 4.8 %fusion.55 = bf16[4,192,352]{2,1,0:T(8,128)(2,1)S(1)} fusion(bf16[192,2048,1]{1,0,2:T(8,128)(2,1)S(1)} %bitcast.168, bf16[8,2048,352]{1,2,0:T(8,128)(2,1)} %param.29, f32[4,192,352]{2,1,0:T(8,128)S(1)} %fusion.39), kind=kOutput, calls=%fused_computation.44 | convolution fusion | flops 1108918272 | bytes 8175616 | tf_op jit(solution)/shard_map/td,gdf->gtf/dot_general | solution.py:204
  165.6 2.3 %fusion.21 = bf16[192,2048]{1,0:T(8,128)(2,1)} fusion(bf16[4,192,352]{2,1,0:T(8,128)(2,1)S(1)} %fusion.55, bf16[8,352,2048]{2,1,0:T(8,128)(2,1)S(1)} %bitcast.178), kind=kOutput, calls=%fused_computation.22 | convolution fusion | flops 1107689472 | bytes 7143424 | tf_op jit(solution)/shard_map/gtf,gfd->td/dot_general | solution.py:208
  168.0 3.5 %all-to-all-start.6 = ((bf16[8,24,2048]{2,1,0:T(8,128)(2,1)}), bf16[8,24,2048]{2,1,0:T(8,128)(2,1)S(1)}, u32[]{:S(2)}, u32[]{:S(2)}) async-start(bf16[8,24,2048]{2,1,0:T(8,128)(2,1)} %bitcast.42), calls=%async_computation.6 | async-start | bytes 1572864 | tf_op jit(solution)/shard_map/all_to_all | solution.py:211
  171.5 4.8 %fusion.33 = f32[4,192,352]{2,1,0:T(8,128)S(1)} fusion(bf16[192,2048,1]{1,0,2:T(8,128)(2,1)S(1)} %bitcast.165, bf16[8,2048,352]{1,2,0:T(8,128)(2,1)} %param.28), kind=kOutput, calls=%fused_computation.36 | convolution fusion | flops 1107296256 | bytes 7634944 | tf_op jit(solution)/shard_map/td,gdf->gtf/dot_general | solution.py:201
  176.3 4.8 %fusion.52 = bf16[4,192,352]{2,1,0:T(8,128)(2,1)S(1)} fusion(bf16[192,2048,1]{1,0,2:T(8,128)(2,1)S(1)} %bitcast.166, bf16[8,2048,352]{1,2,0:T(8,128)(2,1)} %param.29, f32[4,192,352]{2,1,0:T(8,128)S(1)} %fusion.33), kind=kOutput, calls=%fused_computation.43 | convolution fusion | flops 1108918272 | bytes 8175616 | tf_op jit(solution)/shard_map/td,gdf->gtf/dot_general | solution.py:204
  181.1 2.3 %fusion.24 = bf16[192,2048]{1,0:T(8,128)(2,1)} fusion(bf16[4,192,352]{2,1,0:T(8,128)(2,1)S(1)} %fusion.52, bf16[8,352,2048]{2,1,0:T(8,128)(2,1)S(1)} %bitcast.180), kind=kOutput, calls=%fused_computation.23 | convolution fusion | flops 1107689472 | bytes 7143424 | tf_op jit(solution)/shard_map/gtf,gfd->td/dot_general | solution.py:208
  184.0 3.6 %all-to-all-start.5 = ((bf16[8,24,2048]{2,1,0:T(8,128)(2,1)}), bf16[8,24,2048]{2,1,0:T(8,128)(2,1)S(1)}, u32[]{:S(2)}, u32[]{:S(2)}) async-start(bf16[8,24,2048]{2,1,0:T(8,128)(2,1)} %bitcast.32), calls=%async_computation.5 | async-start | bytes 1572864 | tf_op jit(solution)/shard_map/all_to_all | solution.py:211
  189.0 11.2 %all-to-all-done.5 = bf16[8,24,2048]{2,1,0:T(8,128)(2,1)S(1)} async-done(((bf16[8,24,2048]{2,1,0:T(8,128)(2,1)}), bf16[8,24,2048]{2,1,0:T(8,128)(2,1)S(1)}, u32[]{:S(2)}, u32[]{:S(2)}) %all-to-all-start.5) | async-done | bytes 786464 | tf_op jit(solution)/shard_map/all_to_all | solution.py:211
  203.2 3.5 %all-to-all-start.7 = ((bf16[4,128,512]{2,1,0:T(8,128)(2,1)}), bf16[4,128,512]{2,1,0:T(8,128)(2,1)S(1)}, u32[]{:S(2)}, u32[]{:S(2)}) async-start(bf16[4,128,512]{2,1,0:T(8,128)(2,1)} %bitcast.160), calls=%async_computation.7 | async-start | bytes 1048576 | tf_op jit(solution)/shard_map/all_to_all | solution.py:227
  207.3 11.2 %all-to-all-done.7 = bf16[4,128,512]{2,1,0:T(8,128)(2,1)S(1)} async-done(((bf16[4,128,512]{2,1,0:T(8,128)(2,1)}), bf16[4,128,512]{2,1,0:T(8,128)(2,1)S(1)}, u32[]{:S(2)}, u32[]{:S(2)}) %all-to-all-start.7) | async-done | bytes 524320 | tf_op jit(solution)/shard_map/all_to_all | solution.py:227
  (107 shorter events, 31.6 us)
Async XLA Ops:
  0.6 138.2 %copy-start = (bf16[704,2048]{1,0:T(8,128)(2,1)S(1)}, bf16[704,2048]{1,0:T(8,128)(2,1)}, u32[]{:S(2)}) copy-start(bf16[704,2048]{1,0:T(8,128)(2,1)} %param.33) | copy-start | bytes 8650756
  1.7 7.8 %copy-start.12 = (bf16[64,2,512]{2,1,0:T(2,128)(2,1)S(1)}, bf16[64,2,512]{2,1,0:T(2,128)(2,1)}, u32[]{:S(2)}) copy-start(bf16[64,2,512]{2,1,0:T(2,128)(2,1)} %param.18) | copy-start | bytes 393220
  2.8 20.7 %all-to-all-start = ((bf16[8,64,2,512]{3,1,2,0:T(8,128)(2,1)}), bf16[8,64,2,512]{3,1,2,0:T(8,128)(2,1)}, u32[]{:S(2)}, u32[]{:S(2)}) async-start(bf16[8,64,2,512]{3,1,2,0:T(8,128)(2,1)} %broadcast_in_dim.118), calls=%async_computation | async-start | bytes 2097152 | tf_op jit(solution)/shard_map/all_to_all | solution.py:58
  14.1 2.2 %copy-start.9 = (pred[512,1024]{0,1:T(8,128)(4,1)S(1)}, pred[512,1024]{0,1:T(8,128)(4,1)}, u32[]{:S(2)}) copy-start(pred[512,1024]{0,1:T(8,128)(4,1)} %broadcast_compare_fusion) | copy-start | bytes 1572868
  18.0 1.7 copy-start.14
  23.5 1.9 copy-start.2
  63.8 1.0 copy-start.6
  82.3 10.2 %copy-start.13 = (s32[64,2,6]{0,1,2:T(2,128)S(1)}, s32[64,2,6]{0,1,2:T(2,128)}, u32[]{:S(2)}) copy-start(s32[64,2,6]{0,1,2:T(2,128)} %param.26) | copy-start | bytes 9220
  85.1 19.7 %all-to-all-start.2 = ((bf16[4,128,512]{2,1,0:T(8,128)(2,1)}), bf16[4,128,512]{2,1,0:T(8,128)(2,1)S(1)}, u32[]{:S(2)}, u32[]{:S(2)}) async-start(bf16[4,128,512]{2,1,0:T(8,128)(2,1)} %fusion.61), calls=%async_computation.2 | async-start | bytes 1048576 | tf_op jit(solution)/shard_map/all_to_all | solution.py:135
  92.6 12.3 %copy-start.10 = (s32[64,2,6]{2,1,0:T(2,128)}, s32[64,2,6]{2,1,0:T(2,128)S(1)}, u32[]{:S(2)}) copy-start(s32[64,2,6]{2,1,0:T(2,128)S(1)} %copy.93) | copy-start | bytes 9220
  106.8 17.4 %all-to-all-start.3 = ((bf16[4,128,512]{1,2,0:T(8,128)(2,1)}), bf16[4,128,512]{1,2,0:T(8,128)(2,1)S(1)}, u32[]{:S(2)}, u32[]{:S(2)}) async-start(bf16[4,128,512]{1,2,0:T(8,128)(2,1)} %broadcast_in_dim.131), calls=%async_computation.3 | async-start | bytes 1048576 | tf_op jit(solution)/shard_map/all_to_all | solution.py:141
  124.3 0.8 copy-start.5
  129.1 25.3 %all-to-all-start.4 = ((bf16[8,2,24,2048]{3,2,1,0:T(8,128)(2,1)}), bf16[8,2,24,2048]{3,2,1,0:T(8,128)(2,1)}, u32[]{:S(2)}, u32[]{:S(2)}) async-start(bf16[8,2,24,2048]{3,2,1,0:T(8,128)(2,1)} %bitcast.154), calls=%async_computation.4 | async-start | bytes 3145728 | tf_op jit(solution)/shard_map/all_to_all | solution.py:178
  156.0 9.6 %slice-start = ((s8[11534336]{0:T(1024)(128)(4,1)}), s8[4194304]{0:T(1024)(128)(4,1)S(1)}, s32[]{:S(2)}) async-start(s8[11534336]{0:T(1024)(128)(4,1)} %bitcast.177), calls=%async_computation.8 | async-start | bytes 8388608
  156.0 9.6 %slice-start.1 = ((s8[11534336]{0:T(1024)(128)(4,1)}), s8[4194304]{0:T(1024)(128)(4,1)S(1)}, s32[]{:S(2)}) async-start(s8[11534336]{0:T(1024)(128)(4,1)} %bitcast.177), calls=%async_computation.9 | async-start | bytes 8388608
  160.8 4.8 %slice-start.2 = ((s8[11534336]{0:T(1024)(128)(4,1)}), s8[3145728]{0:T(1024)(128)(4,1)S(1)}, s32[]{:S(2)}) async-start(s8[11534336]{0:T(1024)(128)(4,1)} %bitcast.177), calls=%async_computation.10 | async-start | bytes 6291456
  168.0 16.1 %all-to-all-start.6 = ((bf16[8,24,2048]{2,1,0:T(8,128)(2,1)}), bf16[8,24,2048]{2,1,0:T(8,128)(2,1)S(1)}, u32[]{:S(2)}, u32[]{:S(2)}) async-start(bf16[8,24,2048]{2,1,0:T(8,128)(2,1)} %bitcast.42), calls=%async_computation.6 | async-start | bytes 1572864 | tf_op jit(solution)/shard_map/all_to_all | solution.py:211
  171.5 9.6 %slice-start.3 = ((s8[11534336]{0:T(1024)(128)(4,1)}), s8[4194304]{0:T(1024)(128)(4,1)S(1)}, s32[]{:S(2)}) async-start(s8[11534336]{0:T(1024)(128)(4,1)} %bitcast.179), calls=%async_computation.11 | async-start | bytes 8388608
  171.5 9.6 %slice-start.4 = ((s8[11534336]{0:T(1024)(128)(4,1)}), s8[4194304]{0:T(1024)(128)(4,1)S(1)}, s32[]{:S(2)}) async-start(s8[11534336]{0:T(1024)(128)(4,1)} %bitcast.179), calls=%async_computation.12 | async-start | bytes 8388608
  176.3 4.8 %slice-start.5 = ((s8[11534336]{0:T(1024)(128)(4,1)}), s8[3145728]{0:T(1024)(128)(4,1)S(1)}, s32[]{:S(2)}) async-start(s8[11534336]{0:T(1024)(128)(4,1)} %bitcast.179), calls=%async_computation.13 | async-start | bytes 6291456
  181.1 6.5 %copy-start.11 = (f32[128,384]{0,1:T(8,128)S(1)}, f32[128,384]{0,1:T(8,128)}, u32[]{:S(2)}) copy-start(f32[128,384]{0,1:T(8,128)} %copy.100) | copy-start | bytes 589828
  184.0 5.0 %copy-start.3 = (bf16[8,24,2048]{2,1,0:T(8,128)(2,1)}, bf16[8,24,2048]{2,1,0:T(8,128)(2,1)S(1)}, u32[]{:S(2)}) copy-start(bf16[8,24,2048]{2,1,0:T(8,128)(2,1)S(1)} %all-to-all-done.6) | copy-start | bytes 2359300
  184.0 16.2 %all-to-all-start.5 = ((bf16[8,24,2048]{2,1,0:T(8,128)(2,1)}), bf16[8,24,2048]{2,1,0:T(8,128)(2,1)S(1)}, u32[]{:S(2)}, u32[]{:S(2)}) async-start(bf16[8,24,2048]{2,1,0:T(8,128)(2,1)} %bitcast.32), calls=%async_computation.5 | async-start | bytes 1572864 | tf_op jit(solution)/shard_map/all_to_all | solution.py:211
  200.2 1.1 copy-start.4
  200.2 1.5 copy-start.7
  200.2 1.8 copy-start.8
  202.0 17.4 %copy-start.1 = (bf16[704,2048]{1,0:T(8,128)(2,1)S(1)}, bf16[704,2048]{1,0:T(8,128)(2,1)}, u32[]{:S(2)}) copy-start(bf16[704,2048]{1,0:T(8,128)(2,1)} %param.33) | copy-start | bytes 8650756
  203.2 15.4 %all-to-all-start.7 = ((bf16[4,128,512]{2,1,0:T(8,128)(2,1)}), bf16[4,128,512]{2,1,0:T(8,128)(2,1)S(1)}, u32[]{:S(2)}, u32[]{:S(2)}) async-start(bf16[4,128,512]{2,1,0:T(8,128)(2,1)} %bitcast.160), calls=%async_computation.7 | async-start | bytes 1048576 | tf_op jit(solution)/shard_map/all_to_all | solution.py:227

commit v11 on v9

--- a/solution.py
+++ b/solution.py
@@ -147,7 +147,7 @@
     dest_row = chosen // experts_per_row
     local_expert = chosen - (dest_row * col_count + col_index) * entries_here // GROUPS
     valid = (local_expert >= 0) & (local_expert < experts_dev)
-    place = (dest_row * experts_dev + local_expert) * CAP + slot_index
+    place = (local_expert * row_count + dest_row) * CAP + slot_index
     place = jnp.where(valid, place, -1).reshape(token_count, TOPK)
     hit = place[:, :, None] == jnp.arange(slots, dtype=jnp.int32)[None, None, :]
     dispatch = jnp.sum(hit.astype(jnp.float32), axis=1).astype(jnp.bfloat16)
@@ -157,24 +157,27 @@
     outgoing = lax.dot_general(
         dispatch, tokens, (((0,), (0,)), ((), ())), preferred_element_type=jnp.float32
     ).astype(jnp.bfloat16)
-    outgoing = outgoing.reshape(row_count, experts_dev, CAP, model_width)
-    arrived = lax.all_to_all(outgoing, "row", 0, 0, tiled=True)
+    outgoing = outgoing.reshape(experts_dev, row_count, CAP, model_width)
+    arrived = [
+        lax.all_to_all(outgoing[chunk], "row", 0, 0, tiled=True) for chunk in range(experts_dev)
+    ]
     shared_g = jnp.dot(tokens, shared_gate, preferred_element_type=jnp.float32)
     shared_u = jnp.dot(tokens, shared_up, preferred_element_type=jnp.float32)
     shared_act = (jax.nn.silu(shared_g) * shared_u).astype(jnp.bfloat16)
     shared_part = jnp.dot(shared_act, shared_down, preferred_element_type=jnp.float32)
-    arrived, shared_part = lax.optimization_barrier((arrived, shared_part))
+    first_arrived, shared_part = lax.optimization_barrier((arrived[0], shared_part))
+    arrived[0] = first_arrived
     hidden = w_gate.shape[2]
     wg = w_gate.reshape(experts_dev, groups_dev, model_width, hidden)
     wu = w_up.reshape(experts_dev, groups_dev, model_width, hidden)
     wd = w_down.reshape(experts_dev, groups_dev, hidden, model_width)
-    combine_hi = combine.astype(jnp.bfloat16).reshape(token_count, row_count, experts_dev, CAP)
+    combine_hi = combine.astype(jnp.bfloat16).reshape(token_count, experts_dev, row_count, CAP)
     combine_lo = (combine - combine_hi.reshape(token_count, slots).astype(jnp.float32)).astype(
         jnp.bfloat16
-    ).reshape(token_count, row_count, experts_dev, CAP)
+    ).reshape(token_count, experts_dev, row_count, CAP)
     routed = jnp.zeros((token_count, model_width), jnp.float32)
     for chunk in range(experts_dev):
-        rows_in = arrived[:, chunk].reshape(row_count * CAP, model_width)
+        rows_in = arrived[chunk].reshape(row_count * CAP, model_width)
         gate_proj = jnp.einsum(
             "td,gdf->gtf", rows_in, wg[chunk], preferred_element_type=jnp.float32
         )
@@ -188,8 +191,8 @@
         returned = lax.all_to_all(
             expert_out.reshape(row_count, CAP, model_width), "row", 0, 0, tiled=True
         ).reshape(row_count * CAP, model_width)
-        pick_hi = combine_hi[:, :, chunk].reshape(token_count, row_count * CAP)
-        pick_lo = combine_lo[:, :, chunk].reshape(token_count, row_count * CAP)
+        pick_hi = combine_hi[:, chunk].reshape(token_count, row_count * CAP)
+        pick_lo = combine_lo[:, chunk].reshape(token_count, row_count * CAP)
         routed = routed + (
             jnp.dot(pick_hi, returned, preferred_element_type=jnp.float32)
             + jnp.dot(pick_lo, returned, preferred_element_type=jnp.float32)

time: 199 us -> 194 us (0.975)
  waiting for transfers between devices: 51.6 us -> 43.5 us
  starting transfers between devices: 39.2 us -> 43 us
    all_to_all x1 -> x2, waiting for transfers between devices: 11 us -> 4.34 us  [body(): lax.all_to_all(outgoing[chunk], 'row', 0, 0, tiled=True)]
    all_to_all x1 -> x2, starting transfers between devices: 6.88 us -> 10.4 us  [body(): lax.all_to_all(outgoing[chunk], 'row', 0, 0, tiled=True)]
  transfers between devices with their start and end apart: 9 -> 10, of which waited for: 9 -> 10; matrix products, arithmetic and copies ran while one was open for 33% -> 41% of each run, Pallas kernels for 0% -> 0%
where the time goes in v11:
time: 194 us; the launch traced here: 192 us
  matrix products  44.3 us (23%)
  waiting for transfers between devices  43.5 us (22%)
  starting transfers between devices  43 us (22%)
  local copies, waits for them, and re-layouts  31.6 us (16%)
  other arithmetic  28.2 us (15%)
    all_to_all x2, waiting for transfers between devices, body(): lax.all_to_all(expert_out.reshape(row_count, CAP, model_width), 'row', 0,...  11.8 us
    all_to_all x1, waiting for transfers between devices, body(): lax.all_to_all(ffn_chunks, 'col', 0, 0, tiled=True).astype(jnp.float32)  11.2 us
    all_to_all x2, starting transfers between devices, body(): lax.all_to_all(outgoing[chunk], 'row', 0, 0, tiled=True)  10.4 us
    dot_general x2, matrix products, body(): jnp.einsum('td,gdf->gtf', rows_in, wu[chunk], preferred_element_type=jnp....  9.8 us
    dot_general x2, matrix products, body(): jnp.einsum('td,gdf->gtf', rows_in, wg[chunk], preferred_element_type=jnp....  9.76 us
    all_to_all x1, waiting for transfers between devices, body(): lax.all_to_all(product.reshape(row_count, rows_here, requests, width_here...  7.98 us
    unnamed x47, local copies, waits for them, and re-layouts  7.79 us
    all_to_all x2, starting transfers between devices, body(): lax.all_to_all(expert_out.reshape(row_count, CAP, model_width), 'row', 0,...  7.58 us
  transfers between devices with their start and end apart: 10, of which 10 were waited for; matrix products, arithmetic and copies ran while one was open for 41% of the time, Pallas kernels for 0%

profile of v11, /device:TPU:0, one launch (start us, length us, event | category | flops | bytes accessed | tf_op | source)
XLA Modules:
  0.0 191.8 jit_solution(4845910128527745863)
XLA Ops:
  1.7 1.1 broadcast_in_dim.111
  2.9 5.2 %all-to-all-start = ((bf16[8,64,2,512]{3,1,2,0:T(8,128)(2,1)}), bf16[8,64,2,512]{3,1,2,0:T(8,128)(2,1)}, u32[]{:S(2)}, u32[]{:S(2)}) async-start(bf16[8,64,2,512]{3,1,2,0:T(8,128)(2,1)} %broadcast_in_dim.111), calls=%async_computation | async-start | bytes 2097152 | tf_op jit(solution)/shard_map/all_to_all | solution.py:58
  8.1 1.2 broadcast_compare_fusion.1
  9.6 2.2 %maximum_bitcast_fusion = bf16[2,512,192]{1,0,2:T(2,128)(2,1)} fusion(bf16[64,2,512]{2,1,0:T(2,128)(2,1)S(1)} %copy-done.11, bf16[128,2,512]{2,1,0:T(2,128)(2,1)} %param.20), kind=kLoop, calls=%fused_computation.63 | loop fusion | flops 196608 | bytes 786432 | tf_op jit(solution)/shard_map/transpose | solution.py:50
  11.8 2.3 %maximum_bitcast_fusion.1 = bf16[2,192,512]{2,0,1:T(2,128)(2,1)} fusion(bf16[64,2,512]{2,1,0:T(2,128)(2,1)} %param.19, bf16[128,2,512]{2,1,0:T(2,128)(2,1)} %param.21), kind=kLoop, calls=%fused_computation.64 | loop fusion | flops 196608 | bytes 786432 | tf_op jit(solution)/shard_map/transpose | solution.py:54
  16.3 1.6 bitcast_select_fusion.3
  18.0 1.7 bitcast_select_fusion.2
  20.1 3.4 %all-to-all-done = bf16[8,64,2,512]{3,1,2,0:T(8,128)(2,1)} async-done(((bf16[8,64,2,512]{3,1,2,0:T(8,128)(2,1)}), bf16[8,64,2,512]{3,1,2,0:T(8,128)(2,1)}, u32[]{:S(2)}, u32[]{:S(2)}) %all-to-all-start) | async-done | bytes 1048608 | tf_op jit(solution)/shard_map/all_to_all | solution.py:58
  23.5 1.4 copy.80
  25.4 1.5 select_reduce_fusion.1
  28.0 2.6 %fusion.14 = bf16[2,512,1024]{1,2,0:T(8,128)(2,1)} fusion(f32[2,1024,512]{2,1,0:T(8,128)S(1)} %get-tuple-element.17, f32[2,512,4]{1,2,0:T(4,128)S(1)} %get-tuple-element.16, pred[2,512,256]{1,2,0:T(8,128)(4,1)S(1)} %broadcast_or_fusion), kind=kLoop, calls=%fused_computation.16 | loop fusion | flops 5242880 | bytes 6569984 | tf_op jit(solution)/shard_map/convert_element_type | solution.py:84
  31.6 3.3 %all-to-all-start.1 = ((f32[8,1,1024]{2,1,0:T(1,128)}), f32[8,1,1024]{2,1,0:T(1,128)S(1)}, u32[]{:S(2)}, u32[]{:S(2)}) async-start(f32[8,1,1024]{2,1,0:T(1,128)} %reshape.414), calls=%async_computation.1 | async-start | bytes 65536 | tf_op jit(solution)/shard_map/all_to_all | solution.py:92
  34.9 3.5 %convolution_convert_fusion.1 = bf16[2,512,512]{1,2,0:T(8,128)(2,1)S(1)} fusion(bf16[2,1024,512]{2,1,0:T(8,128)(2,1)} %bitcast_select_fusion.2, bf16[2,512,1024]{1,2,0:T(8,128)(2,1)} %fusion.14), kind=kOutput, calls=%fused_computation.35 | convolution fusion | flops 1074266112 | bytes 5242880 | tf_op jit(solution)/shard_map/ric,rck->irk/dot_general | solution.py:82
  39.7 4.2 %all-to-all-start.2 = ((bf16[8,64,2,512]{3,1,2,0:T(8,128)(2,1)}), bf16[8,64,2,512]{3,1,2,0:T(8,128)(2,1)}, u32[]{:S(2)}, u32[]{:S(2)}) async-start(bf16[8,64,2,512]{3,1,2,0:T(8,128)(2,1)} %copy.86), calls=%async_computation.2 | async-start | bytes 2097152 | tf_op jit(solution)/shard_map/all_to_all | solution.py:89
  45.6 2.2 %broadcast_in_dim.115 = f32[8,64,2,4,128]{4,3,1,2,0:T(4,128)} broadcast(f32[8,64,2,4]{3,1,2,0:T(8,128)S(1)} %copy.83), dimensions={0,1,2,3} | broadcast | bytes 2113536 | tf_op jit(solution)/shard_map/broadcast_in_dim | solution.py:99
  47.8 3.1 %reshape.391 = f32[8,64,2,512]{3,1,2,0:T(8,128)} reshape(f32[8,64,2,4,128]{4,3,1,2,0:T(4,128)} %broadcast_in_dim.115) | data formatting | bytes 4194304 | tf_op jit(solution)/shard_map/reshape | solution.py:101
  51.4 8.0 %all-to-all-done.2 = bf16[8,64,2,512]{3,1,2,0:T(8,128)(2,1)} async-done(((bf16[8,64,2,512]{3,1,2,0:T(8,128)(2,1)}), bf16[8,64,2,512]{3,1,2,0:T(8,128)(2,1)}, u32[]{:S(2)}, u32[]{:S(2)}) %all-to-all-start.2) | async-done | bytes 1048608 | tf_op jit(solution)/shard_map/all_to_all | solution.py:89
  59.4 2.2 %multiply_reduce_fusion = f32[64,2,512]{2,0,1:T(8,128)S(1)} fusion(f32[8,64,2,512]{3,1,2,0:T(8,128)} %reshape.391, bf16[8,64,2,512]{3,1,2,0:T(8,128)(2,1)} %all-to-all-done.2), kind=kLoop, calls=%fused_computation.34 | loop fusion | flops 1507328 | bytes 3407872 | tf_op jit(solution)/shard_map/reduce_sum | solution.py:102
  61.9 2.8 %fusion.60 = bf16[4,128,512]{2,1,0:T(8,128)(2,1)} fusion(bf16[128,512,1]{1,0,2:T(8,128)(2,1)S(1)} %reshape.407, bf16[64,4,8,512]{3,2,1,0:T(8,128)(2,1)} %bitcast.207), kind=kOutput, calls=%fused_computation.45 | convolution fusion | flops 268697600 | bytes 2752512 | tf_op jit(solution)/shard_map/tk,kcw->ctw/dot_general | solution.py:111
  64.7 5.3 %all-to-all-start.3 = ((bf16[4,128,512]{2,1,0:T(8,128)(2,1)}), bf16[4,128,512]{2,1,0:T(8,128)(2,1)S(1)}, u32[]{:S(2)}, u32[]{:S(2)}) async-start(bf16[4,128,512]{2,1,0:T(8,128)(2,1)} %fusion.60), calls=%async_computation.3 | async-start | bytes 1048576 | tf_op jit(solution)/shard_map/all_to_all | solution.py:118
  70.0 2.0 %reshape.387 = bf16[128,2048]{1,0:T(8,128)(2,1)} reshape(bf16[64,2,2048]{2,1,0:T(2,128)(2,1)} %param.23) | data formatting | bytes 1048576 | tf_op jit(solution)/shard_map/reshape | solution.py:121
  73.0 4.4 %reduce-window.6 = s32[64,6,128]{2,0,1:T(8,128)} reduce-window(s32[64,6,128]{2,0,1:T(8,128)} %fusion.75, s32[]{:T(128)} %constant.86.clone.1), window={size=1x1x128 pad=0_0x0_0x127_0}, to_apply=%region_6.7 | reduce-window | flops 6242304 | bytes 393220 | tf_op jit(solution)/shard_map/reduce-window
  77.4 4.1 %all-to-all-done.3 = bf16[4,128,512]{2,1,0:T(8,128)(2,1)S(1)} async-done(((bf16[4,128,512]{2,1,0:T(8,128)(2,1)}), bf16[4,128,512]{2,1,0:T(8,128)(2,1)S(1)}, u32[]{:S(2)}, u32[]{:S(2)}) %all-to-all-start.3) | async-done | bytes 524320 | tf_op jit(solution)/shard_map/all_to_all | solution.py:118
  83.5 3.5 %all-to-all-start.4 = ((bf16[4,128,512]{1,2,0:T(8,128)(2,1)}), bf16[4,128,512]{1,2,0:T(8,128)(2,1)S(1)}, u32[]{:S(2)}, u32[]{:S(2)}) async-start(bf16[4,128,512]{1,2,0:T(8,128)(2,1)} %broadcast_in_dim.125), calls=%async_computation.4 | async-start | bytes 1048576 | tf_op jit(solution)/shard_map/all_to_all | solution.py:124
  87.0 1.2 slice_reduce_fusion
  91.0 1.6 add_select_fusion.2
  93.5 1.4 copy.97
  96.9 1.7 copy.99
  99.9 1.4 fusion.66
  101.3 1.5 convolution_convert_fusion
  102.8 1.4 fusion.95
  104.1 6.9 %all-to-all-start.7 = ((bf16[8,24,2048]{2,1,0:T(8,128)(2,1)}), bf16[8,24,2048]{2,1,0:T(8,128)(2,1)}, u32[]{:S(2)}, u32[]{:S(2)}) async-start(bf16[8,24,2048]{2,1,0:T(8,128)(2,1)} %bitcast.185), calls=%async_computation.7 | async-start | bytes 1572864 | tf_op jit(solution)/shard_map/all_to_all | solution.py:162
  111.0 3.5 %fusion.100 = f32[128,704]{0,1:T(8,128)} fusion(bf16[2048,704]{0,1:T(8,128)(2,1)} %param.31, bf16[128,2048]{0,1:T(8,128)(2,1)S(1)} %fusion.66), kind=kOutput, calls=%fused_computation.138 | convolution fusion | flops 369098752 | bytes 3768320 | tf_op jit(solution)/shard_map/dot_general | solution.py:164
  114.5 5.0 %fusion.64 = f32[128,2048]{1,0:T(8,128)} fusion(bf16[704,2048]{1,0:T(8,128)(2,1)S(1)} %copy-done, bf16[2048,704]{0,1:T(8,128)(2,1)} %param.32, bf16[128,2048]{0,1:T(8,128)(2,1)S(1)} %fusion.66, f32[128,704]{0,1:T(8,128)} %fusion.100), kind=kOutput, calls=%fused_computation.51 | convolution fusion | flops 738738176 | bytes 7700480 | tf_op jit(solution)/shard_map/dot_general | solution.py:167
  119.5 4.3 %all-to-all-done.7 = bf16[8,24,2048]{2,1,0:T(8,128)(2,1)} async-done(((bf16[8,24,2048]{2,1,0:T(8,128)(2,1)}), bf16[8,24,2048]{2,1,0:T(8,128)(2,1)}, u32[]{:S(2)}, u32[]{:S(2)}) %all-to-all-start.7) | async-done | bytes 786464 | tf_op jit(solution)/shard_map/all_to_all | solution.py:162
  123.7 3.5 %all-to-all-start.5 = ((bf16[8,24,2048]{2,1,0:T(8,128)(2,1)}), bf16[8,24,2048]{2,1,0:T(8,128)(2,1)S(1)}, u32[]{:S(2)}, u32[]{:S(2)}) async-start(bf16[8,24,2048]{2,1,0:T(8,128)(2,1)} %bitcast.184), calls=%async_computation.5 | async-start | bytes 1572864 | tf_op jit(solution)/shard_map/all_to_all | solution.py:162
  127.3 5.0 %fusion.39 = f32[4,192,352]{2,1,0:T(8,128)S(1)} fusion(bf16[192,2048,1]{1,0,2:T(8,128)(2,1)} %bitcast.36, bf16[8,2048,352]{1,2,0:T(8,128)(2,1)} %param.28), kind=kOutput, calls=%fused_computation.38 | convolution fusion | flops 1107296256 | bytes 7634944 | tf_op jit(solution)/shard_map/td,gdf->gtf/dot_general | solution.py:181
  132.3 5.0 %fusion.54 = bf16[4,192,352]{2,1,0:T(8,128)(2,1)S(1)} fusion(bf16[192,2048,1]{1,0,2:T(8,128)(2,1)} %bitcast.36, bf16[8,2048,352]{1,2,0:T(8,128)(2,1)} %param.29, f32[4,192,352]{2,1,0:T(8,128)S(1)} %fusion.39), kind=kOutput, calls=%fused_computation.43 | convolution fusion | flops 1108918272 | bytes 8175616 | tf_op jit(solution)/shard_map/td,gdf->gtf/dot_general | solution.py:184
  137.4 2.3 %fusion.21 = bf16[192,2048]{1,0:T(8,128)(2,1)} fusion(bf16[4,192,352]{2,1,0:T(8,128)(2,1)S(1)} %fusion.54, bf16[8,352,2048]{2,1,0:T(8,128)(2,1)S(1)} %bitcast.204), kind=kOutput, calls=%fused_computation.22 | convolution fusion | flops 1107689472 | bytes 7143424 | tf_op jit(solution)/shard_map/gtf,gfd->td/dot_general | solution.py:188
  139.8 4.0 %all-to-all-start.8 = ((bf16[8,24,2048]{2,1,0:T(8,128)(2,1)}), bf16[8,24,2048]{2,1,0:T(8,128)(2,1)S(1)}, u32[]{:S(2)}, u32[]{:S(2)}) async-start(bf16[8,24,2048]{2,1,0:T(8,128)(2,1)} %bitcast.41), calls=%async_computation.8 | async-start | bytes 1572864 | tf_op jit(solution)/shard_map/all_to_all | solution.py:191
  143.9 4.8 %fusion.33 = f32[4,192,352]{2,1,0:T(8,128)S(1)} fusion(bf16[192,2048,1]{1,0,2:T(8,128)(2,1)S(1)} %bitcast.190, bf16[8,2048,352]{1,2,0:T(8,128)(2,1)} %param.28), kind=kOutput, calls=%fused_computation.36 | convolution fusion | flops 1107296256 | bytes 7634944 | tf_op jit(solution)/shard_map/td,gdf->gtf/dot_general | solution.py:181
  148.7 4.8 %fusion.51 = bf16[4,192,352]{2,1,0:T(8,128)(2,1)S(1)} fusion(bf16[192,2048,1]{1,0,2:T(8,128)(2,1)S(1)} %bitcast.191, bf16[8,2048,352]{1,2,0:T(8,128)(2,1)} %param.29, f32[4,192,352]{2,1,0:T(8,128)S(1)} %fusion.33), kind=kOutput, calls=%fused_computation.42 | convolution fusion | flops 1108918272 | bytes 8175616 | tf_op jit(solution)/shard_map/td,gdf->gtf/dot_general | solution.py:184
  153.5 2.3 %fusion.24 = bf16[192,2048]{1,0:T(8,128)(2,1)} fusion(bf16[4,192,352]{2,1,0:T(8,128)(2,1)S(1)} %fusion.51, bf16[8,352,2048]{2,1,0:T(8,128)(2,1)S(1)} %bitcast.206), kind=kOutput, calls=%fused_computation.23 | convolution fusion | flops 1107689472 | bytes 7143424 | tf_op jit(solution)/shard_map/gtf,gfd->td/dot_general | solution.py:188
  156.5 3.5 %all-to-all-start.6 = ((bf16[8,24,2048]{2,1,0:T(8,128)(2,1)}), bf16[8,24,2048]{2,1,0:T(8,128)(2,1)S(1)}, u32[]{:S(2)}, u32[]{:S(2)}) async-start(bf16[8,24,2048]{2,1,0:T(8,128)(2,1)} %bitcast.30), calls=%async_computation.6 | async-start | bytes 1572864 | tf_op jit(solution)/shard_map/all_to_all | solution.py:191
  160.1 1.4 fusion.99
  161.5 11.1 %all-to-all-done.6 = bf16[8,24,2048]{2,1,0:T(8,128)(2,1)S(1)} async-done(((bf16[8,24,2048]{2,1,0:T(8,128)(2,1)}), bf16[8,24,2048]{2,1,0:T(8,128)(2,1)S(1)}, u32[]{:S(2)}, u32[]{:S(2)}) %all-to-all-start.6) | async-done | bytes 786464 | tf_op jit(solution)/shard_map/all_to_all | solution.py:191
  175.6 3.5 %all-to-all-start.9 = ((bf16[4,128,512]{2,1,0:T(8,128)(2,1)}), bf16[4,128,512]{2,1,0:T(8,128)(2,1)S(1)}, u32[]{:S(2)}, u32[]{:S(2)}) async-start(bf16[4,128,512]{2,1,0:T(8,128)(2,1)} %bitcast.187), calls=%async_computation.9 | async-start | bytes 1048576 | tf_op jit(solution)/shard_map/all_to_all | solution.py:207
  179.8 11.2 %all-to-all-done.9 = bf16[4,128,512]{2,1,0:T(8,128)(2,1)S(1)} async-done(((bf16[4,128,512]{2,1,0:T(8,128)(2,1)}), bf16[4,128,512]{2,1,0:T(8,128)(2,1)S(1)}, u32[]{:S(2)}, u32[]{:S(2)}) %all-to-all-start.9) | async-done | bytes 524320 | tf_op jit(solution)/shard_map/all_to_all | solution.py:207
  (108 shorter events, 25.2 us)
Async XLA Ops:
  0.6 113.9 %copy-start = (bf16[704,2048]{1,0:T(8,128)(2,1)S(1)}, bf16[704,2048]{1,0:T(8,128)(2,1)}, u32[]{:S(2)}) copy-start(bf16[704,2048]{1,0:T(8,128)(2,1)} %param.33) | copy-start | bytes 8650756
  0.6 8.9 %copy-start.11 = (bf16[64,2,512]{2,1,0:T(2,128)(2,1)S(1)}, bf16[64,2,512]{2,1,0:T(2,128)(2,1)}, u32[]{:S(2)}) copy-start(bf16[64,2,512]{2,1,0:T(2,128)(2,1)} %param.18) | copy-start | bytes 393220
  2.9 20.7 %all-to-all-start = ((bf16[8,64,2,512]{3,1,2,0:T(8,128)(2,1)}), bf16[8,64,2,512]{3,1,2,0:T(8,128)(2,1)}, u32[]{:S(2)}, u32[]{:S(2)}) async-start(bf16[8,64,2,512]{3,1,2,0:T(8,128)(2,1)} %broadcast_in_dim.111), calls=%async_computation | async-start | bytes 2097152 | tf_op jit(solution)/shard_map/all_to_all | solution.py:58
  14.1 2.2 %copy-start.8 = (pred[512,1024]{0,1:T(8,128)(4,1)S(1)}, pred[512,1024]{0,1:T(8,128)(4,1)}, u32[]{:S(2)}) copy-start(pred[512,1024]{0,1:T(8,128)(4,1)} %broadcast_compare_fusion.1) | copy-start | bytes 1572868
  16.3 3.4 %copy-start.13 = (s32[2]{0:T(128)S(1)}, s32[2]{0:T(128)}, u32[]{:S(2)}) copy-start(s32[2]{0:T(128)} %param.22) | copy-start | bytes 28
  23.5 1.9 copy-start.2
  31.6 8.1 %all-to-all-start.1 = ((f32[8,1,1024]{2,1,0:T(1,128)}), f32[8,1,1024]{2,1,0:T(1,128)S(1)}, u32[]{:S(2)}, u32[]{:S(2)}) async-start(f32[8,1,1024]{2,1,0:T(1,128)} %reshape.414), calls=%async_computation.1 | async-start | bytes 65536 | tf_op jit(solution)/shard_map/all_to_all | solution.py:92
  39.7 19.7 %all-to-all-start.2 = ((bf16[8,64,2,512]{3,1,2,0:T(8,128)(2,1)}), bf16[8,64,2,512]{3,1,2,0:T(8,128)(2,1)}, u32[]{:S(2)}, u32[]{:S(2)}) async-start(bf16[8,64,2,512]{3,1,2,0:T(8,128)(2,1)} %copy.86), calls=%async_computation.2 | async-start | bytes 2097152 | tf_op jit(solution)/shard_map/all_to_all | solution.py:89
  61.6 10.4 %copy-start.12 = (s32[64,2,6]{0,1,2:T(2,128)S(1)}, s32[64,2,6]{0,1,2:T(2,128)}, u32[]{:S(2)}) copy-start(s32[64,2,6]{0,1,2:T(2,128)} %param.26) | copy-start | bytes 9220
  64.7 16.8 %all-to-all-start.3 = ((bf16[4,128,512]{2,1,0:T(8,128)(2,1)}), bf16[4,128,512]{2,1,0:T(8,128)(2,1)S(1)}, u32[]{:S(2)}, u32[]{:S(2)}) async-start(bf16[4,128,512]{2,1,0:T(8,128)(2,1)} %fusion.60), calls=%async_computation.3 | async-start | bytes 1048576 | tf_op jit(solution)/shard_map/all_to_all | solution.py:118
  72.1 9.4 %copy-start.9 = (s32[64,2,6]{2,1,0:T(2,128)}, s32[64,2,6]{2,1,0:T(2,128)S(1)}, u32[]{:S(2)}) copy-start(s32[64,2,6]{2,1,0:T(2,128)S(1)} %copy.92) | copy-start | bytes 9220
  83.5 15.6 %all-to-all-start.4 = ((bf16[4,128,512]{1,2,0:T(8,128)(2,1)}), bf16[4,128,512]{1,2,0:T(8,128)(2,1)S(1)}, u32[]{:S(2)}, u32[]{:S(2)}) async-start(bf16[4,128,512]{1,2,0:T(8,128)(2,1)} %broadcast_in_dim.125), calls=%async_computation.4 | async-start | bytes 1048576 | tf_op jit(solution)/shard_map/all_to_all | solution.py:124
  99.1 0.8 copy-start.5
  104.1 19.6 %all-to-all-start.7 = ((bf16[8,24,2048]{2,1,0:T(8,128)(2,1)}), bf16[8,24,2048]{2,1,0:T(8,128)(2,1)}, u32[]{:S(2)}, u32[]{:S(2)}) async-start(bf16[8,24,2048]{2,1,0:T(8,128)(2,1)} %bitcast.185), calls=%async_computation.7 | async-start | bytes 1572864 | tf_op jit(solution)/shard_map/all_to_all | solution.py:162
  123.7 16.1 %all-to-all-start.5 = ((bf16[8,24,2048]{2,1,0:T(8,128)(2,1)}), bf16[8,24,2048]{2,1,0:T(8,128)(2,1)S(1)}, u32[]{:S(2)}, u32[]{:S(2)}) async-start(bf16[8,24,2048]{2,1,0:T(8,128)(2,1)} %bitcast.184), calls=%async_computation.5 | async-start | bytes 1572864 | tf_op jit(solution)/shard_map/all_to_all | solution.py:162
  127.3 10.1 %slice-start = ((s8[11534336]{0:T(1024)(128)(4,1)}), s8[4194304]{0:T(1024)(128)(4,1)S(1)}, s32[]{:S(2)}) async-start(s8[11534336]{0:T(1024)(128)(4,1)} %bitcast.203), calls=%async_computation.10 | async-start | bytes 8388608
  127.3 10.1 %slice-start.1 = ((s8[11534336]{0:T(1024)(128)(4,1)}), s8[4194304]{0:T(1024)(128)(4,1)S(1)}, s32[]{:S(2)}) async-start(s8[11534336]{0:T(1024)(128)(4,1)} %bitcast.203), calls=%async_computation.11 | async-start | bytes 8388608
  132.3 5.1 %slice-start.2 = ((s8[11534336]{0:T(1024)(128)(4,1)}), s8[3145728]{0:T(1024)(128)(4,1)S(1)}, s32[]{:S(2)}) async-start(s8[11534336]{0:T(1024)(128)(4,1)} %bitcast.203), calls=%async_computation.12 | async-start | bytes 6291456
  139.8 16.6 %all-to-all-start.8 = ((bf16[8,24,2048]{2,1,0:T(8,128)(2,1)}), bf16[8,24,2048]{2,1,0:T(8,128)(2,1)S(1)}, u32[]{:S(2)}, u32[]{:S(2)}) async-start(bf16[8,24,2048]{2,1,0:T(8,128)(2,1)} %bitcast.41), calls=%async_computation.8 | async-start | bytes 1572864 | tf_op jit(solution)/shard_map/all_to_all | solution.py:191
  143.9 9.6 %slice-start.3 = ((s8[11534336]{0:T(1024)(128)(4,1)}), s8[4194304]{0:T(1024)(128)(4,1)S(1)}, s32[]{:S(2)}) async-start(s8[11534336]{0:T(1024)(128)(4,1)} %bitcast.205), calls=%async_computation.13 | async-start | bytes 8388608
  143.9 9.6 %slice-start.4 = ((s8[11534336]{0:T(1024)(128)(4,1)}), s8[4194304]{0:T(1024)(128)(4,1)S(1)}, s32[]{:S(2)}) async-start(s8[11534336]{0:T(1024)(128)(4,1)} %bitcast.205), calls=%async_computation.14 | async-start | bytes 8388608
  148.7 4.8 %slice-start.5 = ((s8[11534336]{0:T(1024)(128)(4,1)}), s8[3145728]{0:T(1024)(128)(4,1)S(1)}, s32[]{:S(2)}) async-start(s8[11534336]{0:T(1024)(128)(4,1)} %bitcast.205), calls=%async_computation.15 | async-start | bytes 6291456
  153.5 6.5 %copy-start.10 = (f32[128,384]{0,1:T(8,128)S(1)}, f32[128,384]{0,1:T(8,128)}, u32[]{:S(2)}) copy-start(f32[128,384]{0,1:T(8,128)} %copy.99) | copy-start | bytes 589828
  156.5 16.5 %copy-start.3 = (bf16[8,24,2048]{2,1,0:T(8,128)(2,1)}, bf16[8,24,2048]{2,1,0:T(8,128)(2,1)S(1)}, u32[]{:S(2)}) copy-start(bf16[8,24,2048]{2,1,0:T(8,128)(2,1)S(1)} %all-to-all-done.8) | copy-start | bytes 2359300
  156.5 16.1 %all-to-all-start.6 = ((bf16[8,24,2048]{2,1,0:T(8,128)(2,1)}), bf16[8,24,2048]{2,1,0:T(8,128)(2,1)S(1)}, u32[]{:S(2)}, u32[]{:S(2)}) async-start(bf16[8,24,2048]{2,1,0:T(8,128)(2,1)} %bitcast.30), calls=%async_computation.6 | async-start | bytes 1572864 | tf_op jit(solution)/shard_map/all_to_all | solution.py:191
  172.6 1.2 copy-start.6
  172.6 1.5 copy-start.7
  172.9 1.5 copy-start.4
  173.3 18.5 %copy-start.1 = (bf16[704,2048]{1,0:T(8,128)(2,1)S(1)}, bf16[704,2048]{1,0:T(8,128)(2,1)}, u32[]{:S(2)}) copy-start(bf16[704,2048]{1,0:T(8,128)(2,1)} %param.33) | copy-start | bytes 8650756
  175.6 15.4 %all-to-all-start.9 = ((bf16[4,128,512]{2,1,0:T(8,128)(2,1)}), bf16[4,128,512]{2,1,0:T(8,128)(2,1)S(1)}, u32[]{:S(2)}, u32[]{:S(2)}) async-start(bf16[4,128,512]{2,1,0:T(8,128)(2,1)} %bitcast.187), calls=%async_computation.9 | async-start | bytes 1048576 | tf_op jit(solution)/shard_map/all_to_all | solution.py:207

commit v12 on v11

--- a/solution.py
+++ b/solution.py
@@ -154,12 +154,23 @@
     combine = jnp.sum(
         jnp.where(hit, gate_values.reshape(token_count, TOPK, 1), 0.0), axis=1
     )
-    outgoing = lax.dot_general(
-        dispatch, tokens, (((0,), (0,)), ((), ())), preferred_element_type=jnp.float32
-    ).astype(jnp.bfloat16)
-    outgoing = outgoing.reshape(experts_dev, row_count, CAP, model_width)
+    chunk_width = row_count * CAP
     arrived = [
-        lax.all_to_all(outgoing[chunk], "row", 0, 0, tiled=True) for chunk in range(experts_dev)
+        lax.all_to_all(
+            lax.dot_general(
+                dispatch[:, chunk * chunk_width : (chunk + 1) * chunk_width],
+                tokens,
+                (((0,), (0,)), ((), ())),
+                preferred_element_type=jnp.float32,
+            )
+            .astype(jnp.bfloat16)
+            .reshape(row_count, CAP, model_width),
+            "row",
+            0,
+            0,
+            tiled=True,
+        )
+        for chunk in range(experts_dev)
     ]
     shared_g = jnp.dot(tokens, shared_gate, preferred_element_type=jnp.float32)
     shared_u = jnp.dot(tokens, shared_up, preferred_element_type=jnp.float32)

time: 194 us -> 194 us (level)
  matrix products: 44.3 us -> 46.4 us
    dot_general x1 -> x2, matrix products: 1.48 us -> 3.49 us  [body(): lax.dot_general(dispatch[:, chunk * chunk_width:(chunk + 1) * chunk_width...]
    unnamed x47 -> x49, local copies, waits for them, and re-layouts: 7.79 us -> 7.79 us
where the time goes in v12:
time: 194 us; the launch traced here: 191 us
  matrix products  46.4 us (24%)
  starting transfers between devices  43 us (22%)
  waiting for transfers between devices  42.1 us (22%)
  local copies, waits for them, and re-layouts  30.3 us (16%)
  other arithmetic  28.2 us (15%)
    all_to_all x2, waiting for transfers between devices, body(): lax.all_to_all(expert_out.reshape(row_count, CAP, model_width), 'row', 0,...  11.8 us
    all_to_all x1, waiting for transfers between devices, body(): lax.all_to_all(ffn_chunks, 'col', 0, 0, tiled=True).astype(jnp.float32)  11.2 us
    all_to_all x2, starting transfers between devices, body(): lax.all_to_all(lax.dot_general(dispatch[:, chunk * chunk_width:(chunk + 1...  10.4 us
    dot_general x2, matrix products, body(): jnp.einsum('td,gdf->gtf', rows_in, wu[chunk], preferred_element_type=jnp....  9.8 us
    dot_general x2, matrix products, body(): jnp.einsum('td,gdf->gtf', rows_in, wg[chunk], preferred_element_type=jnp....  9.75 us
    all_to_all x1, waiting for transfers between devices, body(): lax.all_to_all(product.reshape(row_count, rows_here, requests, width_here...  7.98 us
    unnamed x49, local copies, waits for them, and re-layouts  7.79 us
    all_to_all x2, starting transfers between devices, body(): lax.all_to_all(expert_out.reshape(row_count, CAP, model_width), 'row', 0,...  7.6 us
  transfers between devices with their start and end apart: 10, of which 10 were waited for; matrix products, arithmetic and copies ran while one was open for 41% of the time, Pallas kernels for 0%

profile of v12, /device:TPU:0, one launch (start us, length us, event | category | flops | bytes accessed | tf_op | source)
XLA Modules:
  0.0 191.2 jit_solution(16550035230333541679)
XLA Ops:
  1.7 1.1 broadcast_in_dim.111
  2.9 5.2 %all-to-all-start = ((bf16[8,64,2,512]{3,1,2,0:T(8,128)(2,1)}), bf16[8,64,2,512]{3,1,2,0:T(8,128)(2,1)}, u32[]{:S(2)}, u32[]{:S(2)}) async-start(bf16[8,64,2,512]{3,1,2,0:T(8,128)(2,1)} %broadcast_in_dim.111), calls=%async_computation | async-start | bytes 2097152 | tf_op jit(solution)/shard_map/all_to_all | solution.py:58
  8.1 1.2 broadcast_compare_fusion.1
  9.6 2.2 %maximum_bitcast_fusion = bf16[2,512,192]{1,0,2:T(2,128)(2,1)} fusion(bf16[64,2,512]{2,1,0:T(2,128)(2,1)S(1)} %copy-done.12, bf16[128,2,512]{2,1,0:T(2,128)(2,1)} %param.20), kind=kLoop, calls=%fused_computation.64 | loop fusion | flops 196608 | bytes 786432 | tf_op jit(solution)/shard_map/transpose | solution.py:50
  11.8 2.3 %maximum_bitcast_fusion.1 = bf16[2,192,512]{2,0,1:T(2,128)(2,1)} fusion(bf16[64,2,512]{2,1,0:T(2,128)(2,1)} %param.19, bf16[128,2,512]{2,1,0:T(2,128)(2,1)} %param.21), kind=kLoop, calls=%fused_computation.65 | loop fusion | flops 196608 | bytes 786432 | tf_op jit(solution)/shard_map/transpose | solution.py:54
  16.3 1.6 bitcast_select_fusion.3
  18.0 1.7 bitcast_select_fusion.2
  20.1 3.4 %all-to-all-done = bf16[8,64,2,512]{3,1,2,0:T(8,128)(2,1)} async-done(((bf16[8,64,2,512]{3,1,2,0:T(8,128)(2,1)}), bf16[8,64,2,512]{3,1,2,0:T(8,128)(2,1)}, u32[]{:S(2)}, u32[]{:S(2)}) %all-to-all-start) | async-done | bytes 1048608 | tf_op jit(solution)/shard_map/all_to_all | solution.py:58
  23.5 1.4 copy.80
  25.4 1.5 select_reduce_fusion.1
  28.0 2.6 %fusion.14 = bf16[2,512,1024]{1,2,0:T(8,128)(2,1)} fusion(f32[2,1024,512]{2,1,0:T(8,128)S(1)} %get-tuple-element.15, f32[2,512,4]{1,2,0:T(4,128)S(1)} %get-tuple-element.14, pred[2,512,256]{1,2,0:T(8,128)(4,1)S(1)} %broadcast_or_fusion), kind=kLoop, calls=%fused_computation.16 | loop fusion | flops 5242880 | bytes 6569984 | tf_op jit(solution)/shard_map/convert_element_type | solution.py:84
  31.6 3.3 %all-to-all-start.1 = ((f32[8,1,1024]{2,1,0:T(1,128)}), f32[8,1,1024]{2,1,0:T(1,128)S(1)}, u32[]{:S(2)}, u32[]{:S(2)}) async-start(f32[8,1,1024]{2,1,0:T(1,128)} %reshape.417), calls=%async_computation.1 | async-start | bytes 65536 | tf_op jit(solution)/shard_map/all_to_all | solution.py:92
  34.9 3.5 %convolution_convert_fusion.2 = bf16[2,512,512]{1,2,0:T(8,128)(2,1)S(1)} fusion(bf16[2,1024,512]{2,1,0:T(8,128)(2,1)} %bitcast_select_fusion.2, bf16[2,512,1024]{1,2,0:T(8,128)(2,1)} %fusion.14), kind=kOutput, calls=%fused_computation.36 | convolution fusion | flops 1074266112 | bytes 5242880 | tf_op jit(solution)/shard_map/ric,rck->irk/dot_general | solution.py:82
  39.7 4.2 %all-to-all-start.2 = ((bf16[8,64,2,512]{3,1,2,0:T(8,128)(2,1)}), bf16[8,64,2,512]{3,1,2,0:T(8,128)(2,1)}, u32[]{:S(2)}, u32[]{:S(2)}) async-start(bf16[8,64,2,512]{3,1,2,0:T(8,128)(2,1)} %copy.86), calls=%async_computation.2 | async-start | bytes 2097152 | tf_op jit(solution)/shard_map/all_to_all | solution.py:89
  45.6 2.2 %broadcast_in_dim.115 = f32[8,64,2,4,128]{4,3,1,2,0:T(4,128)} broadcast(f32[8,64,2,4]{3,1,2,0:T(8,128)S(1)} %copy.83), dimensions={0,1,2,3} | broadcast | bytes 2113536 | tf_op jit(solution)/shard_map/broadcast_in_dim | solution.py:99
  47.8 3.1 %reshape.392 = f32[8,64,2,512]{3,1,2,0:T(8,128)} reshape(f32[8,64,2,4,128]{4,3,1,2,0:T(4,128)} %broadcast_in_dim.115) | data formatting | bytes 4194304 | tf_op jit(solution)/shard_map/reshape | solution.py:101
  51.4 8.0 %all-to-all-done.2 = bf16[8,64,2,512]{3,1,2,0:T(8,128)(2,1)} async-done(((bf16[8,64,2,512]{3,1,2,0:T(8,128)(2,1)}), bf16[8,64,2,512]{3,1,2,0:T(8,128)(2,1)}, u32[]{:S(2)}, u32[]{:S(2)}) %all-to-all-start.2) | async-done | bytes 1048608 | tf_op jit(solution)/shard_map/all_to_all | solution.py:89
  59.4 2.2 %multiply_reduce_fusion = f32[64,2,512]{2,0,1:T(8,128)S(1)} fusion(f32[8,64,2,512]{3,1,2,0:T(8,128)} %reshape.392, bf16[8,64,2,512]{3,1,2,0:T(8,128)(2,1)} %all-to-all-done.2), kind=kLoop, calls=%fused_computation.35 | loop fusion | flops 1507328 | bytes 3407872 | tf_op jit(solution)/shard_map/reduce_sum | solution.py:102
  61.9 2.8 %fusion.60 = bf16[4,128,512]{2,1,0:T(8,128)(2,1)} fusion(bf16[128,512,1]{1,0,2:T(8,128)(2,1)S(1)} %reshape.410, bf16[64,4,8,512]{3,2,1,0:T(8,128)(2,1)} %bitcast.207), kind=kOutput, calls=%fused_computation.46 | convolution fusion | flops 268697600 | bytes 2752512 | tf_op jit(solution)/shard_map/tk,kcw->ctw/dot_general | solution.py:111
  64.7 5.3 %all-to-all-start.3 = ((bf16[4,128,512]{2,1,0:T(8,128)(2,1)}), bf16[4,128,512]{2,1,0:T(8,128)(2,1)S(1)}, u32[]{:S(2)}, u32[]{:S(2)}) async-start(bf16[4,128,512]{2,1,0:T(8,128)(2,1)} %fusion.60), calls=%async_computation.3 | async-start | bytes 1048576 | tf_op jit(solution)/shard_map/all_to_all | solution.py:118
  70.0 2.0 %reshape.388 = bf16[128,2048]{1,0:T(8,128)(2,1)} reshape(bf16[64,2,2048]{2,1,0:T(2,128)(2,1)} %param.23) | data formatting | bytes 1048576 | tf_op jit(solution)/shard_map/reshape | solution.py:121
  73.0 4.4 %reduce-window.6 = s32[64,6,128]{2,0,1:T(8,128)} reduce-window(s32[64,6,128]{2,0,1:T(8,128)} %fusion.75, s32[]{:T(128)} %constant.86.clone.1), window={size=1x1x128 pad=0_0x0_0x127_0}, to_apply=%region_6.7 | reduce-window | flops 6242304 | bytes 393220 | tf_op jit(solution)/shard_map/reduce-window
  77.4 4.1 %all-to-all-done.3 = bf16[4,128,512]{2,1,0:T(8,128)(2,1)S(1)} async-done(((bf16[4,128,512]{2,1,0:T(8,128)(2,1)}), bf16[4,128,512]{2,1,0:T(8,128)(2,1)S(1)}, u32[]{:S(2)}, u32[]{:S(2)}) %all-to-all-start.3) | async-done | bytes 524320 | tf_op jit(solution)/shard_map/all_to_all | solution.py:118
  83.5 3.5 %all-to-all-start.4 = ((bf16[4,128,512]{1,2,0:T(8,128)(2,1)}), bf16[4,128,512]{1,2,0:T(8,128)(2,1)S(1)}, u32[]{:S(2)}, u32[]{:S(2)}) async-start(bf16[4,128,512]{1,2,0:T(8,128)(2,1)} %broadcast_in_dim.125), calls=%async_computation.4 | async-start | bytes 1048576 | tf_op jit(solution)/shard_map/all_to_all | solution.py:124
  87.0 1.2 slice_reduce_fusion
  91.0 1.6 add_select_fusion.2
  93.5 1.4 copy.97
  96.9 1.7 copy.99
  99.9 1.4 fusion.66
  101.3 2.2 %convolution_convert_fusion = bf16[192,2048]{1,0:T(8,128)(2,1)} fusion(bf16[128,2048]{0,1:T(8,128)(2,1)S(1)} %fusion.66, bf16[128,384]{1,0:T(8,128)(2,1)} %get-tuple-element.7), kind=kOutput, calls=%fused_computation.23 | convolution fusion | flops 101056512 | bytes 1376256 | tf_op jit(solution)/shard_map/dot_general | solution.py:160
  103.5 6.9 %all-to-all-start.7 = ((bf16[8,24,2048]{2,1,0:T(8,128)(2,1)}), bf16[8,24,2048]{2,1,0:T(8,128)(2,1)}, u32[]{:S(2)}, u32[]{:S(2)}) async-start(bf16[8,24,2048]{2,1,0:T(8,128)(2,1)} %bitcast.185), calls=%async_computation.7 | async-start | bytes 1572864 | tf_op jit(solution)/shard_map/all_to_all | solution.py:159
  110.4 3.5 %fusion.100 = f32[128,704]{0,1:T(8,128)} fusion(bf16[2048,704]{0,1:T(8,128)(2,1)} %param.31, bf16[128,2048]{0,1:T(8,128)(2,1)S(1)} %fusion.66), kind=kOutput, calls=%fused_computation.139 | convolution fusion | flops 369098752 | bytes 3768320 | tf_op jit(solution)/shard_map/dot_general | solution.py:175
  113.9 1.3 convolution_convert_fusion.1
  115.2 5.0 %fusion.64 = f32[128,2048]{1,0:T(8,128)} fusion(bf16[704,2048]{1,0:T(8,128)(2,1)S(1)} %copy-done, bf16[2048,704]{0,1:T(8,128)(2,1)} %param.32, bf16[128,2048]{0,1:T(8,128)(2,1)S(1)} %fusion.66, f32[128,704]{0,1:T(8,128)} %fusion.100), kind=kOutput, calls=%fused_computation.52 | convolution fusion | flops 738738176 | bytes 7700480 | tf_op jit(solution)/shard_map/dot_general | solution.py:178
  120.2 2.9 %all-to-all-done.7 = bf16[8,24,2048]{2,1,0:T(8,128)(2,1)} async-done(((bf16[8,24,2048]{2,1,0:T(8,128)(2,1)}), bf16[8,24,2048]{2,1,0:T(8,128)(2,1)}, u32[]{:S(2)}, u32[]{:S(2)}) %all-to-all-start.7) | async-done | bytes 786464 | tf_op jit(solution)/shard_map/all_to_all | solution.py:159
  123.1 3.5 %all-to-all-start.5 = ((bf16[8,24,2048]{2,1,0:T(8,128)(2,1)}), bf16[8,24,2048]{2,1,0:T(8,128)(2,1)S(1)}, u32[]{:S(2)}, u32[]{:S(2)}) async-start(bf16[8,24,2048]{2,1,0:T(8,128)(2,1)} %bitcast.184), calls=%async_computation.5 | async-start | bytes 1572864 | tf_op jit(solution)/shard_map/all_to_all | solution.py:159
  126.7 5.0 %fusion.39 = f32[4,192,352]{2,1,0:T(8,128)S(1)} fusion(bf16[192,2048,1]{1,0,2:T(8,128)(2,1)} %bitcast.36, bf16[8,2048,352]{1,2,0:T(8,128)(2,1)} %param.28), kind=kOutput, calls=%fused_computation.39 | convolution fusion | flops 1107296256 | bytes 7634944 | tf_op jit(solution)/shard_map/td,gdf->gtf/dot_general | solution.py:192
  131.7 5.0 %fusion.54 = bf16[4,192,352]{2,1,0:T(8,128)(2,1)S(1)} fusion(bf16[192,2048,1]{1,0,2:T(8,128)(2,1)} %bitcast.36, bf16[8,2048,352]{1,2,0:T(8,128)(2,1)} %param.29, f32[4,192,352]{2,1,0:T(8,128)S(1)} %fusion.39), kind=kOutput, calls=%fused_computation.44 | convolution fusion | flops 1108918272 | bytes 8175616 | tf_op jit(solution)/shard_map/td,gdf->gtf/dot_general | solution.py:195
  136.7 2.4 %fusion.21 = bf16[192,2048]{1,0:T(8,128)(2,1)} fusion(bf16[4,192,352]{2,1,0:T(8,128)(2,1)S(1)} %fusion.54, bf16[8,352,2048]{2,1,0:T(8,128)(2,1)S(1)} %bitcast.204), kind=kOutput, calls=%fused_computation.21 | convolution fusion | flops 1107689472 | bytes 7143424 | tf_op jit(solution)/shard_map/gtf,gfd->td/dot_general | solution.py:199
  139.2 4.1 %all-to-all-start.8 = ((bf16[8,24,2048]{2,1,0:T(8,128)(2,1)}), bf16[8,24,2048]{2,1,0:T(8,128)(2,1)S(1)}, u32[]{:S(2)}, u32[]{:S(2)}) async-start(bf16[8,24,2048]{2,1,0:T(8,128)(2,1)} %bitcast.41), calls=%async_computation.8 | async-start | bytes 1572864 | tf_op jit(solution)/shard_map/all_to_all | solution.py:202
  143.2 4.8 %fusion.33 = f32[4,192,352]{2,1,0:T(8,128)S(1)} fusion(bf16[192,2048,1]{1,0,2:T(8,128)(2,1)S(1)} %bitcast.190, bf16[8,2048,352]{1,2,0:T(8,128)(2,1)} %param.28), kind=kOutput, calls=%fused_computation.37 | convolution fusion | flops 1107296256 | bytes 7634944 | tf_op jit(solution)/shard_map/td,gdf->gtf/dot_general | solution.py:192
  148.0 4.8 %fusion.51 = bf16[4,192,352]{2,1,0:T(8,128)(2,1)S(1)} fusion(bf16[192,2048,1]{1,0,2:T(8,128)(2,1)S(1)} %bitcast.191, bf16[8,2048,352]{1,2,0:T(8,128)(2,1)} %param.29, f32[4,192,352]{2,1,0:T(8,128)S(1)} %fusion.33), kind=kOutput, calls=%fused_computation.43 | convolution fusion | flops 1108918272 | bytes 8175616 | tf_op jit(solution)/shard_map/td,gdf->gtf/dot_general | solution.py:195
  152.9 2.3 %fusion.24 = bf16[192,2048]{1,0:T(8,128)(2,1)} fusion(bf16[4,192,352]{2,1,0:T(8,128)(2,1)S(1)} %fusion.51, bf16[8,352,2048]{2,1,0:T(8,128)(2,1)S(1)} %bitcast.206), kind=kOutput, calls=%fused_computation.22 | convolution fusion | flops 1107689472 | bytes 7143424 | tf_op jit(solution)/shard_map/gtf,gfd->td/dot_general | solution.py:199
  155.8 3.5 %all-to-all-start.6 = ((bf16[8,24,2048]{2,1,0:T(8,128)(2,1)}), bf16[8,24,2048]{2,1,0:T(8,128)(2,1)S(1)}, u32[]{:S(2)}, u32[]{:S(2)}) async-start(bf16[8,24,2048]{2,1,0:T(8,128)(2,1)} %bitcast.30), calls=%async_computation.6 | async-start | bytes 1572864 | tf_op jit(solution)/shard_map/all_to_all | solution.py:202
  159.5 1.4 fusion.99
  160.8 11.1 %all-to-all-done.6 = bf16[8,24,2048]{2,1,0:T(8,128)(2,1)S(1)} async-done(((bf16[8,24,2048]{2,1,0:T(8,128)(2,1)}), bf16[8,24,2048]{2,1,0:T(8,128)(2,1)S(1)}, u32[]{:S(2)}, u32[]{:S(2)}) %all-to-all-start.6) | async-done | bytes 786464 | tf_op jit(solution)/shard_map/all_to_all | solution.py:202
  175.0 3.5 %all-to-all-start.9 = ((bf16[4,128,512]{2,1,0:T(8,128)(2,1)}), bf16[4,128,512]{2,1,0:T(8,128)(2,1)S(1)}, u32[]{:S(2)}, u32[]{:S(2)}) async-start(bf16[4,128,512]{2,1,0:T(8,128)(2,1)} %bitcast.187), calls=%async_computation.9 | async-start | bytes 1048576 | tf_op jit(solution)/shard_map/all_to_all | solution.py:218
  179.2 11.2 %all-to-all-done.9 = bf16[4,128,512]{2,1,0:T(8,128)(2,1)S(1)} async-done(((bf16[4,128,512]{2,1,0:T(8,128)(2,1)}), bf16[4,128,512]{2,1,0:T(8,128)(2,1)S(1)}, u32[]{:S(2)}, u32[]{:S(2)}) %all-to-all-start.9) | async-done | bytes 524320 | tf_op jit(solution)/shard_map/all_to_all | solution.py:218
  (110 shorter events, 25.2 us)
Async XLA Ops:
  0.6 114.6 %copy-start = (bf16[704,2048]{1,0:T(8,128)(2,1)S(1)}, bf16[704,2048]{1,0:T(8,128)(2,1)}, u32[]{:S(2)}) copy-start(bf16[704,2048]{1,0:T(8,128)(2,1)} %param.33) | copy-start | bytes 8650756
  0.6 8.9 %copy-start.12 = (bf16[64,2,512]{2,1,0:T(2,128)(2,1)S(1)}, bf16[64,2,512]{2,1,0:T(2,128)(2,1)}, u32[]{:S(2)}) copy-start(bf16[64,2,512]{2,1,0:T(2,128)(2,1)} %param.18) | copy-start | bytes 393220
  2.9 20.7 %all-to-all-start = ((bf16[8,64,2,512]{3,1,2,0:T(8,128)(2,1)}), bf16[8,64,2,512]{3,1,2,0:T(8,128)(2,1)}, u32[]{:S(2)}, u32[]{:S(2)}) async-start(bf16[8,64,2,512]{3,1,2,0:T(8,128)(2,1)} %broadcast_in_dim.111), calls=%async_computation | async-start | bytes 2097152 | tf_op jit(solution)/shard_map/all_to_all | solution.py:58
  14.1 2.2 %copy-start.8 = (pred[512,1024]{0,1:T(8,128)(4,1)S(1)}, pred[512,1024]{0,1:T(8,128)(4,1)}, u32[]{:S(2)}) copy-start(pred[512,1024]{0,1:T(8,128)(4,1)} %broadcast_compare_fusion.1) | copy-start | bytes 1572868
  16.3 3.4 %copy-start.14 = (s32[2]{0:T(128)S(1)}, s32[2]{0:T(128)}, u32[]{:S(2)}) copy-start(s32[2]{0:T(128)} %param.22) | copy-start | bytes 28
  23.5 1.9 copy-start.2
  31.6 8.1 %all-to-all-start.1 = ((f32[8,1,1024]{2,1,0:T(1,128)}), f32[8,1,1024]{2,1,0:T(1,128)S(1)}, u32[]{:S(2)}, u32[]{:S(2)}) async-start(f32[8,1,1024]{2,1,0:T(1,128)} %reshape.417), calls=%async_computation.1 | async-start | bytes 65536 | tf_op jit(solution)/shard_map/all_to_all | solution.py:92
  39.7 19.7 %all-to-all-start.2 = ((bf16[8,64,2,512]{3,1,2,0:T(8,128)(2,1)}), bf16[8,64,2,512]{3,1,2,0:T(8,128)(2,1)}, u32[]{:S(2)}, u32[]{:S(2)}) async-start(bf16[8,64,2,512]{3,1,2,0:T(8,128)(2,1)} %copy.86), calls=%async_computation.2 | async-start | bytes 2097152 | tf_op jit(solution)/shard_map/all_to_all | solution.py:89
  61.6 10.4 %copy-start.13 = (s32[64,2,6]{0,1,2:T(2,128)S(1)}, s32[64,2,6]{0,1,2:T(2,128)}, u32[]{:S(2)}) copy-start(s32[64,2,6]{0,1,2:T(2,128)} %param.26) | copy-start | bytes 9220
  64.7 16.8 %all-to-all-start.3 = ((bf16[4,128,512]{2,1,0:T(8,128)(2,1)}), bf16[4,128,512]{2,1,0:T(8,128)(2,1)S(1)}, u32[]{:S(2)}, u32[]{:S(2)}) async-start(bf16[4,128,512]{2,1,0:T(8,128)(2,1)} %fusion.60), calls=%async_computation.3 | async-start | bytes 1048576 | tf_op jit(solution)/shard_map/all_to_all | solution.py:118
  72.1 9.4 %copy-start.9 = (s32[64,2,6]{2,1,0:T(2,128)}, s32[64,2,6]{2,1,0:T(2,128)S(1)}, u32[]{:S(2)}) copy-start(s32[64,2,6]{2,1,0:T(2,128)S(1)} %copy.92) | copy-start | bytes 9220
  83.5 15.6 %all-to-all-start.4 = ((bf16[4,128,512]{1,2,0:T(8,128)(2,1)}), bf16[4,128,512]{1,2,0:T(8,128)(2,1)S(1)}, u32[]{:S(2)}, u32[]{:S(2)}) async-start(bf16[4,128,512]{1,2,0:T(8,128)(2,1)} %broadcast_in_dim.125), calls=%async_computation.4 | async-start | bytes 1048576 | tf_op jit(solution)/shard_map/all_to_all | solution.py:124
  99.1 0.8 copy-start.5
  103.5 19.6 %all-to-all-start.7 = ((bf16[8,24,2048]{2,1,0:T(8,128)(2,1)}), bf16[8,24,2048]{2,1,0:T(8,128)(2,1)}, u32[]{:S(2)}, u32[]{:S(2)}) async-start(bf16[8,24,2048]{2,1,0:T(8,128)(2,1)} %bitcast.185), calls=%async_computation.7 | async-start | bytes 1572864 | tf_op jit(solution)/shard_map/all_to_all | solution.py:159
  110.4 3.5 %copy-start.11 = (bf16[128,384]{1,0:T(8,128)(2,1)S(1)}, bf16[128,384]{1,0:T(8,128)(2,1)}, u32[]{:S(2)}) copy-start(bf16[128,384]{1,0:T(8,128)(2,1)} %get-tuple-element.7) | copy-start | bytes 294916
  123.1 16.1 %all-to-all-start.5 = ((bf16[8,24,2048]{2,1,0:T(8,128)(2,1)}), bf16[8,24,2048]{2,1,0:T(8,128)(2,1)S(1)}, u32[]{:S(2)}, u32[]{:S(2)}) async-start(bf16[8,24,2048]{2,1,0:T(8,128)(2,1)} %bitcast.184), calls=%async_computation.5 | async-start | bytes 1572864 | tf_op jit(solution)/shard_map/all_to_all | solution.py:159
  126.6 10.1 %slice-start = ((s8[11534336]{0:T(1024)(128)(4,1)}), s8[4194304]{0:T(1024)(128)(4,1)S(1)}, s32[]{:S(2)}) async-start(s8[11534336]{0:T(1024)(128)(4,1)} %bitcast.203), calls=%async_computation.10 | async-start | bytes 8388608
  126.6 10.1 %slice-start.1 = ((s8[11534336]{0:T(1024)(128)(4,1)}), s8[4194304]{0:T(1024)(128)(4,1)S(1)}, s32[]{:S(2)}) async-start(s8[11534336]{0:T(1024)(128)(4,1)} %bitcast.203), calls=%async_computation.11 | async-start | bytes 8388608
  131.7 5.1 %slice-start.2 = ((s8[11534336]{0:T(1024)(128)(4,1)}), s8[3145728]{0:T(1024)(128)(4,1)S(1)}, s32[]{:S(2)}) async-start(s8[11534336]{0:T(1024)(128)(4,1)} %bitcast.203), calls=%async_computation.12 | async-start | bytes 6291456
  139.2 16.7 %all-to-all-start.8 = ((bf16[8,24,2048]{2,1,0:T(8,128)(2,1)}), bf16[8,24,2048]{2,1,0:T(8,128)(2,1)S(1)}, u32[]{:S(2)}, u32[]{:S(2)}) async-start(bf16[8,24,2048]{2,1,0:T(8,128)(2,1)} %bitcast.41), calls=%async_computation.8 | async-start | bytes 1572864 | tf_op jit(solution)/shard_map/all_to_all | solution.py:202
  143.2 9.6 %slice-start.3 = ((s8[11534336]{0:T(1024)(128)(4,1)}), s8[4194304]{0:T(1024)(128)(4,1)S(1)}, s32[]{:S(2)}) async-start(s8[11534336]{0:T(1024)(128)(4,1)} %bitcast.205), calls=%async_computation.13 | async-start | bytes 8388608
  143.2 9.6 %slice-start.4 = ((s8[11534336]{0:T(1024)(128)(4,1)}), s8[4194304]{0:T(1024)(128)(4,1)S(1)}, s32[]{:S(2)}) async-start(s8[11534336]{0:T(1024)(128)(4,1)} %bitcast.205), calls=%async_computation.14 | async-start | bytes 8388608
  148.0 4.8 %slice-start.5 = ((s8[11534336]{0:T(1024)(128)(4,1)}), s8[3145728]{0:T(1024)(128)(4,1)S(1)}, s32[]{:S(2)}) async-start(s8[11534336]{0:T(1024)(128)(4,1)} %bitcast.205), calls=%async_computation.15 | async-start | bytes 6291456
  152.8 6.5 %copy-start.10 = (f32[128,384]{0,1:T(8,128)S(1)}, f32[128,384]{0,1:T(8,128)}, u32[]{:S(2)}) copy-start(f32[128,384]{0,1:T(8,128)} %copy.99) | copy-start | bytes 589828
  155.8 16.5 %copy-start.3 = (bf16[8,24,2048]{2,1,0:T(8,128)(2,1)}, bf16[8,24,2048]{2,1,0:T(8,128)(2,1)S(1)}, u32[]{:S(2)}) copy-start(bf16[8,24,2048]{2,1,0:T(8,128)(2,1)S(1)} %all-to-all-done.8) | copy-start | bytes 2359300
  155.8 16.1 %all-to-all-start.6 = ((bf16[8,24,2048]{2,1,0:T(8,128)(2,1)}), bf16[8,24,2048]{2,1,0:T(8,128)(2,1)S(1)}, u32[]{:S(2)}, u32[]{:S(2)}) async-start(bf16[8,24,2048]{2,1,0:T(8,128)(2,1)} %bitcast.30), calls=%async_computation.6 | async-start | bytes 1572864 | tf_op jit(solution)/shard_map/all_to_all | solution.py:202
  172.0 1.2 copy-start.6
  172.0 1.5 copy-start.7
  172.3 1.5 copy-start.4
  172.7 18.5 %copy-start.1 = (bf16[704,2048]{1,0:T(8,128)(2,1)S(1)}, bf16[704,2048]{1,0:T(8,128)(2,1)}, u32[]{:S(2)}) copy-start(bf16[704,2048]{1,0:T(8,128)(2,1)} %param.33) | copy-start | bytes 8650756
  175.0 15.4 %all-to-all-start.9 = ((bf16[4,128,512]{2,1,0:T(8,128)(2,1)}), bf16[4,128,512]{2,1,0:T(8,128)(2,1)S(1)}, u32[]{:S(2)}, u32[]{:S(2)}) async-start(bf16[4,128,512]{2,1,0:T(8,128)(2,1)} %bitcast.187), calls=%async_computation.9 | async-start | bytes 1048576 | tf_op jit(solution)/shard_map/all_to_all | solution.py:218
